TPU v7x, 32 devices: a whole 2x2x4 slice. The times are simulated.
32 devices in a mesh: grp: 2 (over x), blk: 16 (over z, y, core).
Axes of the slice: x: 2, y: 2, z: 4, core: 2. Of those that a mesh axis runs over, the one named last changes fastest.
Arguments:
- tokens: bfloat16 [16384, 1024], P(('grp', 'blk')), parts along dimension 0, may hold values from -6 to 6
- patch_of_row: int32 [16384], P(('grp', 'blk')), parts along dimension 0, may hold values from 0 to 2047, as said below
- latents: bfloat16 [256, 1024], P('blk'), may hold values from -110 to 110
- contrast_gain: bfloat16 [4, 1024], replicated, may hold values from 0.099609375 to 1.8984375
- norm_gain: bfloat16 [1024], replicated, may hold values from 0.099609375 to 1.8984375
- w_query: bfloat16 [1024, 1024], replicated, may hold values from -0.1875 to 0.1875
- w_key: bfloat16 [1024, 1024], replicated, may hold values from -0.1875 to 0.1875
- w_value: bfloat16 [1024, 1024], replicated, may hold values from -0.1875 to 0.1875
- w_out: bfloat16 [1024, 1024], replicated, may hold values from -0.1875 to 0.1875
Outputs:
- new_latents: bfloat16 [512, 1024], P(('grp', 'blk')), parts along dimension 0
There are 2 independent parts, one for each index of `grp`. A program takes and returns all parts, laid end to end along the dimension named above; an argument that names none is the same for every part. Nothing has to cross between parts.
Inputs may be any that keep to these rules, and one draw needn't show every extreme that they name: `patch_of_row`: for each contrast c, rows c * 2048 to (c + 1) * 2048 - 1 name every patch once, and row c * 2048 + s names a patch p with p // 128 == s % 16.
All inputs are finite; a program needn't handle non-finite values.
Results may differ from a plain program's by a relative error of at most 0.0065.
Values may be sent and summed in bfloat16 or wider, within the bound.
No kernel may reach another device: no remote copies, remote signals or barrier semaphores. Data moves between devices by JAX's collectives and lax.ppermute only.
A program may use at most 64 MiB of HBM per device.

v0:
```python
import jax
import jax.numpy as jnp
from jax import lax
from jax.sharding import PartitionSpec as P

HEADS = 16
CONTRASTS = 4


def shifted(block, axis, distance):
    devices = range(lax.axis_size(axis))
    route = [((i - distance) % len(devices), i) for i in devices]
    return lax.ppermute(block, axis, route)


def absorb(tile, maxima, totals, accum, key_heads, value_heads):
    tile_rows, model_width = tile.shape
    head_count, head_width = (key_heads.shape[1], key_heads.shape[2])
    tile_heads = tile.reshape(tile_rows, head_count, head_width)
    scores = jnp.einsum("lhd,khd->lhk", tile_heads, key_heads, preferred_element_type=jnp.float32)
    raised = jnp.maximum(maxima, jnp.max(scores, axis=-1))
    factor = jnp.exp(maxima - raised)
    weights = jnp.exp(scores - raised[..., None])
    totals = totals * factor + jnp.sum(weights, axis=-1)
    summed = jnp.einsum(
        "lhk,khd->lhd",
        weights.astype(jnp.bfloat16),
        value_heads,
        preferred_element_type=jnp.float32,
    )
    accum = accum.reshape(tile_rows, head_count, head_width) * factor[..., None] + summed
    return (raised, totals, accum.reshape(tile_rows, model_width))


def fresh_state(tile_rows, head_count, model_width):
    return (
        jnp.full((tile_rows, head_count), -1e30, jnp.float32),
        jnp.zeros((tile_rows, head_count), jnp.float32),
        jnp.zeros((tile_rows, model_width), jnp.float32),
    )


def pass_one(state):
    return (
        shifted(state[0].astype(jnp.bfloat16), "blk", 1).astype(jnp.float32),
        shifted(state[1].astype(jnp.bfloat16), "blk", 1).astype(jnp.float32),
        shifted(state[2].astype(jnp.bfloat16), "blk", 1).astype(jnp.float32),
    )


def local(tokens, patch_of_row, latents, contrast_gain, norm_gain, w_query, w_key, w_value, w_out):
    cycle_size = lax.axis_size("blk")
    my_index = lax.axis_index("blk")
    tok_rows, model_width = tokens.shape
    head_count = HEADS
    head_width = model_width // head_count
    per_peer = tok_rows // cycle_size
    patches_dev = tok_rows // CONTRASTS
    received = lax.all_to_all(
        tokens.reshape(per_peer, cycle_size, model_width),
        "blk",
        split_axis=1,
        concat_axis=1,
        tiled=True,
    )
    received_ids = lax.all_to_all(
        patch_of_row.reshape(per_peer, cycle_size), "blk", split_axis=1, concat_axis=1, tiled=True
    )
    source_dev = lax.broadcasted_iota(jnp.int32, (per_peer, cycle_size), 1)
    row_step = lax.broadcasted_iota(jnp.int32, (per_peer, cycle_size), 0)
    slot_index = source_dev * tok_rows + my_index + cycle_size * row_step
    contrast_id = slot_index // (patches_dev * cycle_size)
    target_row = (contrast_id * patches_dev + received_ids - my_index * patches_dev).reshape(
        tok_rows
    )
    inverse = (
        jnp.zeros((tok_rows,), jnp.int32).at[target_row].set(jnp.arange(tok_rows, dtype=jnp.int32))
    )
    arranged = received.reshape(tok_rows, model_width)[inverse].reshape(
        CONTRASTS, patches_dev, model_width
    )
    joined = jnp.sum(
        arranged.astype(jnp.float32) * contrast_gain.astype(jnp.float32)[:, None, :], axis=0
    )
    inverse_rms = lax.rsqrt(jnp.mean(joined * joined, axis=-1, keepdims=True) + 1e-05)
    normed = (joined * inverse_rms * norm_gain.astype(jnp.float32)).astype(jnp.bfloat16)
    key_rows = jnp.dot(normed, w_key, preferred_element_type=jnp.float32).astype(jnp.bfloat16)
    value_rows = jnp.dot(normed, w_value, preferred_element_type=jnp.float32).astype(jnp.bfloat16)
    key_heads = key_rows.reshape(patches_dev, head_count, head_width)
    value_heads = value_rows.reshape(patches_dev, head_count, head_width)
    queries = (
        jnp.dot(latents, w_query, preferred_element_type=jnp.float32) * head_width ** (-0.5)
    ).astype(jnp.bfloat16)
    lat_rows = latents.shape[0]

    def hop_step(index_hop, state_carry):
        tile, maxima, totals, accum = state_carry
        state = absorb(tile, maxima, totals, accum, key_heads, value_heads)
        tile = shifted(tile, "blk", 1)
        maxima, totals, accum = pass_one(state)
        return (tile, maxima, totals, accum)

    begin = (queries,) + fresh_state(lat_rows, head_count, model_width)
    tile, maxima, totals, accum = lax.fori_loop(0, cycle_size - 1, hop_step, begin)
    maxima, totals, accum = pass_one(absorb(tile, maxima, totals, accum, key_heads, value_heads))
    attended = (
        (accum.reshape(lat_rows, head_count, head_width) / totals[..., None])
        .reshape(lat_rows, model_width)
        .astype(jnp.bfloat16)
    )
    mixed = latents.astype(jnp.float32) + jnp.dot(
        attended, w_out, preferred_element_type=jnp.float32
    )
    return mixed.astype(jnp.bfloat16)


def solution(mesh):
    in_specs = (
        P(("grp", "blk"), None),
        P(("grp", "blk")),
        P("blk", None),
        P(),
        P(),
        P(),
        P(),
        P(),
        P(),
    )
    out_specs = P(("grp", "blk"), None)
    return jax.shard_map(local, mesh=mesh, in_specs=in_specs, out_specs=out_specs, check_vma=False)
```

profile of v0, /device:TPU:0, one launch (start us, length us, event | category | flops | bytes accessed | tf_op | source)
XLA Modules:
  0.0 180.4 jit_solution(3693052724654784124)
XLA Ops:
  0.0 0.9 all_to_all.12
  0.9 0.7 copy.56
  1.6 7.4 %all-to-all-start.1 = ((s32[32,16,1]{0,2,1:T(1,128)}), s32[32,16,1]{0,2,1:T(1,128)S(1)}, u32[]{:S(2)}, u32[]{:S(2)}) async-start(s32[32,16,1]{0,2,1:T(1,128)} %copy.56), calls=%async_computation.1 | async-start | bytes 16384 | tf_op jit(solution)/shard_map/all_to_all | solution.py:66
  9.0 2.8 %copy.54 = bf16[32,16,1024]{2,0,1:T(8,128)(2,1)} copy(bf16[32,16,1024]{2,1,0:T(8,128)(2,1)} %bitcast.44) | data formatting | bytes 2097152 | tf_op jit(solution)/shard_map/reshape | solution.py:60
  11.9 3.5 %all-to-all-done.1 = s32[32,16,1]{0,2,1:T(1,128)S(1)} async-done(((s32[32,16,1]{0,2,1:T(1,128)}), s32[32,16,1]{0,2,1:T(1,128)S(1)}, u32[]{:S(2)}, u32[]{:S(2)}) %all-to-all-start.1) | async-done | bytes 2080 | tf_op jit(solution)/shard_map/all_to_all | solution.py:66
  15.3 4.3 %all-to-all-start = ((bf16[32,16,1024]{2,0,1:T(8,128)(2,1)}), bf16[32,16,1024]{2,0,1:T(8,128)(2,1)}, u32[]{:S(2)}, u32[]{:S(2)}) async-start(bf16[32,16,1024]{2,0,1:T(8,128)(2,1)} %copy.54), calls=%async_computation | async-start | bytes 2097152 | tf_op jit(solution)/shard_map/all_to_all | solution.py:59
  19.9 2.0 %fusion.12 = bf16[16,1024]{1,0:T(8,128)(2,1)S(1)} fusion(bf16[16,1024]{1,0:T(8,128)(2,1)S(1)} %copy-done.1, bf16[1024,1024]{1,0:T(8,128)(2,1)} %param.16), kind=kOutput, calls=%fused_computation.28 | convolution fusion | flops 33587200 | bytes 2162688 | tf_op jit(solution)/shard_map/dot_general | solution.py:92
  22.1 2.4 %scatter_custom_fusion = s32[512]{0:T(512)S(1)} fusion(s32[512]{0:T(512)S(1)} %bitcast.45, s32[512]{0:T(512)S(1)} %iota.19, s32[]{:T(128)} %constant.23.clone.1), kind=kCustom, calls=%fused_computation.49 | custom fusion | bytes 2052 | tf_op jit(solution)/shard_map/scatter | solution.py:77
  24.6 18.0 %all-to-all-done = bf16[32,16,1024]{2,0,1:T(8,128)(2,1)} async-done(((bf16[32,16,1024]{2,0,1:T(8,128)(2,1)}), bf16[32,16,1024]{2,0,1:T(8,128)(2,1)}, u32[]{:S(2)}, u32[]{:S(2)}) %all-to-all-start) | async-done | bytes 1048608 | tf_op jit(solution)/shard_map/all_to_all | solution.py:59
  42.6 1.8 %copy.55 = bf16[32,16,1024]{2,1,0:T(8,128)(2,1)S(1)} copy(bf16[32,16,1024]{2,0,1:T(8,128)(2,1)} %all-to-all-done) | data formatting | bytes 2097152 | tf_op jit(solution)/shard_map/all_to_all | solution.py:59
  44.4 2.8 %gather_fusion = bf16[512,1024]{1,0:T(8,128)(2,1)} fusion(bf16[512,1024]{1,0:T(8,128)(2,1)S(1)} %bitcast.40, s32[1024]{0:T(1024)S(1)} %pad_clamp_fusion), kind=kCustom, calls=%fused_computation | custom fusion | bytes 2099200 | tf_op jit(solution)/shard_map/gather | solution.py:79
  47.2 1.5 fusion.9
  48.8 0.5 convolution_convert_fusion.1
  49.6 2.1 %convolution_convert_fusion = bf16[128,1024]{1,0:T(8,128)(2,1)S(1)} fusion(bf16[1024,1024]{1,0:T(8,128)(2,1)} %param.18, f32[128,1024]{1,0:T(8,128)S(1)} %fusion.9, f32[1024]{0:T(1024)} %copy-done.2, f32[128]{0:T(128)} %copy-done.4), kind=kOutput, calls=%fused_computation.20 | convolution fusion | flops 268959744 | bytes 2888192 | tf_op jit(solution)/shard_map/dot_general | solution.py:88
  51.9 118.4 %while.17 = (s32[]{:T(128)}, bf16[16,1024]{1,0:T(8,128)(2,1)S(1)}, f32[16,16]{0,1:T(8,128)S(1)}, f32[16,16]{0,1:T(8,128)S(1)}, f32[16,1024]{1,0:T(8,128)S(1)}, /...) while((s32[]{:T(128)}, bf16[16,1024]{1,0:T(8,128)(2,1)S(1)}, ...), condition=%wide.region_6.7_spmd.clone, body=%wide.region_3.6_spmd.clone.sunk | while | flops 8636675 | bytes 1955081 | solution.py:104
  52.6 0.3 fusion.48
  53.1 0.6 collective-permute-start.3
  53.7 1.3 collective-permute-start
  55.0 0.8 collective-permute-start.1
  55.8 2.2 %collective-permute-start.2 = (bf16[16,16]{0,1:T(8,128)(2,1)S(1)}, bf16[16,16]{0,1:T(8,128)(2,1)S(1)}, u32[]{:S(2)}, u32[]{:S(2)}) collective-permute-start(bf16[16,16]{0,1:T(8,128)(2,1)S(1)} %get-tuple-element.157), channel_id=1, source_target_pairs={{15,0},{0,1},{1,2},{2,3},{3,4},{4,5},{5,6},{6,7},{7,8},{8,9},{9,10... | collective-permute-start | bytes 1544 | tf_op jit(solution)/shard_map/while/body/eval_jaxpr/ppermute | solution.py:13
  58.0 2.7 %collective-permute-done.1 = bf16[16,16]{0,1:T(8,128)(2,1)S(1)} collective-permute-done((bf16[16,16]{0,1:T(8,128)(2,1)S(1)}, bf16[16,16]{0,1:T(8,128)(2,1)S(1)}, u32[]{:S(2)}, u32[]{:S(2)}) %collective-permute-start.1) | collective-permute-done | bytes 544 | tf_op jit(solution)/shard_map/while/body/eval_jaxpr/ppermute | solution.py:13
  60.7 0.8 collective-permute-done.2
  62.3 0.3 fusion.48
  63.1 2.5 %collective-permute-start.2 = (bf16[16,16]{0,1:T(8,128)(2,1)S(1)}, bf16[16,16]{0,1:T(8,128)(2,1)S(1)}, u32[]{:S(2)}, u32[]{:S(2)}) collective-permute-start(bf16[16,16]{0,1:T(8,128)(2,1)S(1)} %get-tuple-element.157), channel_id=1, source_target_pairs={{15,0},{0,1},{1,2},{2,3},{3,4},{4,5},{5,6},{6,7},{7,8},{8,9},{9,10... | collective-permute-start | bytes 1544 | tf_op jit(solution)/shard_map/while/body/eval_jaxpr/ppermute | solution.py:13
  65.6 3.6 %collective-permute-done.1 = bf16[16,16]{0,1:T(8,128)(2,1)S(1)} collective-permute-done((bf16[16,16]{0,1:T(8,128)(2,1)S(1)}, bf16[16,16]{0,1:T(8,128)(2,1)S(1)}, u32[]{:S(2)}, u32[]{:S(2)}) %collective-permute-start.1) | collective-permute-done | bytes 544 | tf_op jit(solution)/shard_map/while/body/eval_jaxpr/ppermute | solution.py:13
  70.1 0.3 fusion.48
  70.7 1.1 collective-permute-start.2
  71.8 5.2 %collective-permute-done.1 = bf16[16,16]{0,1:T(8,128)(2,1)S(1)} collective-permute-done((bf16[16,16]{0,1:T(8,128)(2,1)S(1)}, bf16[16,16]{0,1:T(8,128)(2,1)S(1)}, u32[]{:S(2)}, u32[]{:S(2)}) %collective-permute-start.1) | collective-permute-done | bytes 544 | tf_op jit(solution)/shard_map/while/body/eval_jaxpr/ppermute | solution.py:13
  77.8 0.3 fusion.48
  78.5 6.2 %collective-permute-done.1 = bf16[16,16]{0,1:T(8,128)(2,1)S(1)} collective-permute-done((bf16[16,16]{0,1:T(8,128)(2,1)S(1)}, bf16[16,16]{0,1:T(8,128)(2,1)S(1)}, u32[]{:S(2)}, u32[]{:S(2)}) %collective-permute-start.1) | collective-permute-done | bytes 544 | tf_op jit(solution)/shard_map/while/body/eval_jaxpr/ppermute | solution.py:13
  85.6 0.3 fusion.48
  86.3 6.2 %collective-permute-done.1 = bf16[16,16]{0,1:T(8,128)(2,1)S(1)} collective-permute-done((bf16[16,16]{0,1:T(8,128)(2,1)S(1)}, bf16[16,16]{0,1:T(8,128)(2,1)S(1)}, u32[]{:S(2)}, u32[]{:S(2)}) %collective-permute-start.1) | collective-permute-done | bytes 544 | tf_op jit(solution)/shard_map/while/body/eval_jaxpr/ppermute | solution.py:13
  93.3 0.3 fusion.48
  94.1 6.2 %collective-permute-done.1 = bf16[16,16]{0,1:T(8,128)(2,1)S(1)} collective-permute-done((bf16[16,16]{0,1:T(8,128)(2,1)S(1)}, bf16[16,16]{0,1:T(8,128)(2,1)S(1)}, u32[]{:S(2)}, u32[]{:S(2)}) %collective-permute-start.1) | collective-permute-done | bytes 544 | tf_op jit(solution)/shard_map/while/body/eval_jaxpr/ppermute | solution.py:13
  101.1 0.3 fusion.48
  101.8 6.2 %collective-permute-done.1 = bf16[16,16]{0,1:T(8,128)(2,1)S(1)} collective-permute-done((bf16[16,16]{0,1:T(8,128)(2,1)S(1)}, bf16[16,16]{0,1:T(8,128)(2,1)S(1)}, u32[]{:S(2)}, u32[]{:S(2)}) %collective-permute-start.1) | collective-permute-done | bytes 544 | tf_op jit(solution)/shard_map/while/body/eval_jaxpr/ppermute | solution.py:13
  108.9 0.3 fusion.48
  109.6 6.2 %collective-permute-done.1 = bf16[16,16]{0,1:T(8,128)(2,1)S(1)} collective-permute-done((bf16[16,16]{0,1:T(8,128)(2,1)S(1)}, bf16[16,16]{0,1:T(8,128)(2,1)S(1)}, u32[]{:S(2)}, u32[]{:S(2)}) %collective-permute-start.1) | collective-permute-done | bytes 544 | tf_op jit(solution)/shard_map/while/body/eval_jaxpr/ppermute | solution.py:13
  117.3 6.2 %collective-permute-done.1 = bf16[16,16]{0,1:T(8,128)(2,1)S(1)} collective-permute-done((bf16[16,16]{0,1:T(8,128)(2,1)S(1)}, bf16[16,16]{0,1:T(8,128)(2,1)S(1)}, u32[]{:S(2)}, u32[]{:S(2)}) %collective-permute-start.1) | collective-permute-done | bytes 544 | tf_op jit(solution)/shard_map/while/body/eval_jaxpr/ppermute | solution.py:13
  125.1 6.2 %collective-permute-done.1 = bf16[16,16]{0,1:T(8,128)(2,1)S(1)} collective-permute-done((bf16[16,16]{0,1:T(8,128)(2,1)S(1)}, bf16[16,16]{0,1:T(8,128)(2,1)S(1)}, u32[]{:S(2)}, u32[]{:S(2)}) %collective-permute-start.1) | collective-permute-done | bytes 544 | tf_op jit(solution)/shard_map/while/body/eval_jaxpr/ppermute | solution.py:13
  132.9 6.2 %collective-permute-done.1 = bf16[16,16]{0,1:T(8,128)(2,1)S(1)} collective-permute-done((bf16[16,16]{0,1:T(8,128)(2,1)S(1)}, bf16[16,16]{0,1:T(8,128)(2,1)S(1)}, u32[]{:S(2)}, u32[]{:S(2)}) %collective-permute-start.1) | collective-permute-done | bytes 544 | tf_op jit(solution)/shard_map/while/body/eval_jaxpr/ppermute | solution.py:13
  139.9 0.3 fusion.48
  140.6 6.2 %collective-permute-done.1 = bf16[16,16]{0,1:T(8,128)(2,1)S(1)} collective-permute-done((bf16[16,16]{0,1:T(8,128)(2,1)S(1)}, bf16[16,16]{0,1:T(8,128)(2,1)S(1)}, u32[]{:S(2)}, u32[]{:S(2)}) %collective-permute-start.1) | collective-permute-done | bytes 544 | tf_op jit(solution)/shard_map/while/body/eval_jaxpr/ppermute | solution.py:13
  148.4 6.2 %collective-permute-done.1 = bf16[16,16]{0,1:T(8,128)(2,1)S(1)} collective-permute-done((bf16[16,16]{0,1:T(8,128)(2,1)S(1)}, bf16[16,16]{0,1:T(8,128)(2,1)S(1)}, u32[]{:S(2)}, u32[]{:S(2)}) %collective-permute-start.1) | collective-permute-done | bytes 544 | tf_op jit(solution)/shard_map/while/body/eval_jaxpr/ppermute | solution.py:13
  156.2 6.2 %collective-permute-done.1 = bf16[16,16]{0,1:T(8,128)(2,1)S(1)} collective-permute-done((bf16[16,16]{0,1:T(8,128)(2,1)S(1)}, bf16[16,16]{0,1:T(8,128)(2,1)S(1)}, u32[]{:S(2)}, u32[]{:S(2)}) %collective-permute-start.1) | collective-permute-done | bytes 544 | tf_op jit(solution)/shard_map/while/body/eval_jaxpr/ppermute | solution.py:13
  163.9 6.2 %collective-permute-done.1 = bf16[16,16]{0,1:T(8,128)(2,1)S(1)} collective-permute-done((bf16[16,16]{0,1:T(8,128)(2,1)S(1)}, bf16[16,16]{0,1:T(8,128)(2,1)S(1)}, u32[]{:S(2)}, u32[]{:S(2)}) %collective-permute-start.1) | collective-permute-done | bytes 544 | tf_op jit(solution)/shard_map/while/body/eval_jaxpr/ppermute | solution.py:13
  171.5 6.0 %collective-permute-done.5 = bf16[16,16]{0,1:T(8,128)(2,1)S(1)} collective-permute-done((bf16[16,16]{0,1:T(8,128)(2,1)S(1)}, bf16[16,16]{0,1:T(8,128)(2,1)S(1)}, u32[]{:S(2)}, u32[]{:S(2)}) %collective-permute-start.5) | collective-permute-done | bytes 544 | tf_op jit(solution)/shard_map/ppermute | solution.py:13
  177.8 2.6 %fusion.13 = bf16[16,1024]{1,0:T(8,128)(2,1)} fusion(bf16[1024,1024]{1,0:T(8,128)(2,1)} %param.19, bf16[16,1024]{1,0:T(8,128)(2,1)S(1)} %copy-done.1, f32[16,1024]{1,0:T(8,128)S(1)} %div.36, bf16[16,1024]{1,0:T(8,128)(2,1)S(1)} %collective-permute-done.4), kind=kOutput, calls=%fused_computation.29 | convolution fusion | flops 33652736 | bytes 2260992 | tf_op jit(solution)/shard_map/dot_general | solution.py:111
  (345 shorter events, 20.8 us)
Async XLA Ops:
  1.6 13.7 %all-to-all-start.1 = ((s32[32,16,1]{0,2,1:T(1,128)}), s32[32,16,1]{0,2,1:T(1,128)S(1)}, u32[]{:S(2)}, u32[]{:S(2)}) async-start(s32[32,16,1]{0,2,1:T(1,128)} %copy.56), calls=%async_computation.1 | async-start | bytes 16384 | tf_op jit(solution)/shard_map/all_to_all | solution.py:66
  15.3 27.3 %all-to-all-start = ((bf16[32,16,1024]{2,0,1:T(8,128)(2,1)}), bf16[32,16,1024]{2,0,1:T(8,128)(2,1)}, u32[]{:S(2)}, u32[]{:S(2)}) async-start(bf16[32,16,1024]{2,0,1:T(8,128)(2,1)} %copy.54), calls=%async_computation | async-start | bytes 2097152 | tf_op jit(solution)/shard_map/all_to_all | solution.py:59
  53.1 8.5 %collective-permute-start.3 = (bf16[16,1024]{1,0:T(8,128)(2,1)S(1)}, bf16[16,1024]{1,0:T(8,128)(2,1)S(1)}, u32[]{:S(2)}, u32[]{:S(2)}) collective-permute-start(bf16[16,1024]{1,0:T(8,128)(2,1)S(1)} %convert_element_type.136), channel_id=1, source_target_pairs={{15,0},{0,1},{1,2},{2,3},{3,4},{4,5},{5,6},{6,7},{7,8},{8,9},{9,10... | collective-permute-start | bytes 98312 | tf_op jit(solution)/shard_map/while/body/eval_jaxpr/ppermute | solution.py:13
  53.7 7.8 %collective-permute-start = (bf16[16,1024]{1,0:T(8,128)(2,1)S(1)}, bf16[16,1024]{1,0:T(8,128)(2,1)S(1)}, u32[]{:S(2)}, u32[]{:S(2)}) collective-permute-start(bf16[16,1024]{1,0:T(8,128)(2,1)S(1)} %copy.90), channel_id=1, source_target_pairs={{15,0},{0,1},{1,2},{2,3},{3,4},{4,5},{5,6},{6,7},{7,8},{8,9},{9,10... | collective-permute-start | bytes 98312 | tf_op jit(solution)/shard_map/while/body/eval_jaxpr/ppermute | solution.py:13
  62.7 6.5 %collective-permute-start.3 = (bf16[16,1024]{1,0:T(8,128)(2,1)S(1)}, bf16[16,1024]{1,0:T(8,128)(2,1)S(1)}, u32[]{:S(2)}, u32[]{:S(2)}) collective-permute-start(bf16[16,1024]{1,0:T(8,128)(2,1)S(1)} %convert_element_type.136), channel_id=1, source_target_pairs={{15,0},{0,1},{1,2},{2,3},{3,4},{4,5},{5,6},{6,7},{7,8},{8,9},{9,10... | collective-permute-start | bytes 98312 | tf_op jit(solution)/shard_map/while/body/eval_jaxpr/ppermute | solution.py:13
  62.8 6.5 %collective-permute-start = (bf16[16,1024]{1,0:T(8,128)(2,1)S(1)}, bf16[16,1024]{1,0:T(8,128)(2,1)S(1)}, u32[]{:S(2)}, u32[]{:S(2)}) collective-permute-start(bf16[16,1024]{1,0:T(8,128)(2,1)S(1)} %copy.90), channel_id=1, source_target_pairs={{15,0},{0,1},{1,2},{2,3},{3,4},{4,5},{5,6},{6,7},{7,8},{8,9},{9,10... | collective-permute-start | bytes 98312 | tf_op jit(solution)/shard_map/while/body/eval_jaxpr/ppermute | solution.py:13
  70.5 6.5 %collective-permute-start.3 = (bf16[16,1024]{1,0:T(8,128)(2,1)S(1)}, bf16[16,1024]{1,0:T(8,128)(2,1)S(1)}, u32[]{:S(2)}, u32[]{:S(2)}) collective-permute-start(bf16[16,1024]{1,0:T(8,128)(2,1)S(1)} %convert_element_type.136), channel_id=1, source_target_pairs={{15,0},{0,1},{1,2},{2,3},{3,4},{4,5},{5,6},{6,7},{7,8},{8,9},{9,10... | collective-permute-start | bytes 98312 | tf_op jit(solution)/shard_map/while/body/eval_jaxpr/ppermute | solution.py:13
  70.6 6.5 %collective-permute-start = (bf16[16,1024]{1,0:T(8,128)(2,1)S(1)}, bf16[16,1024]{1,0:T(8,128)(2,1)S(1)}, u32[]{:S(2)}, u32[]{:S(2)}) collective-permute-start(bf16[16,1024]{1,0:T(8,128)(2,1)S(1)} %copy.90), channel_id=1, source_target_pairs={{15,0},{0,1},{1,2},{2,3},{3,4},{4,5},{5,6},{6,7},{7,8},{8,9},{9,10... | collective-permute-start | bytes 98312 | tf_op jit(solution)/shard_map/while/body/eval_jaxpr/ppermute | solution.py:13
  70.6 6.4 %collective-permute-start.1 = (bf16[16,16]{0,1:T(8,128)(2,1)S(1)}, bf16[16,16]{0,1:T(8,128)(2,1)S(1)}, u32[]{:S(2)}, u32[]{:S(2)}) collective-permute-start(bf16[16,16]{0,1:T(8,128)(2,1)S(1)} %get-tuple-element.154), channel_id=1, source_target_pairs={{15,0},{0,1},{1,2},{2,3},{3,4},{4,5},{5,6},{6,7},{7,8},{8,9},{9,10... | collective-permute-start | bytes 1544 | tf_op jit(solution)/shard_map/while/body/eval_jaxpr/ppermute | solution.py:13
  70.7 6.3 %collective-permute-start.2 = (bf16[16,16]{0,1:T(8,128)(2,1)S(1)}, bf16[16,16]{0,1:T(8,128)(2,1)S(1)}, u32[]{:S(2)}, u32[]{:S(2)}) collective-permute-start(bf16[16,16]{0,1:T(8,128)(2,1)S(1)} %get-tuple-element.157), channel_id=1, source_target_pairs={{15,0},{0,1},{1,2},{2,3},{3,4},{4,5},{5,6},{6,7},{7,8},{8,9},{9,10... | collective-permute-start | bytes 1544 | tf_op jit(solution)/shard_map/while/body/eval_jaxpr/ppermute | solution.py:13
  78.3 6.5 %collective-permute-start.3 = (bf16[16,1024]{1,0:T(8,128)(2,1)S(1)}, bf16[16,1024]{1,0:T(8,128)(2,1)S(1)}, u32[]{:S(2)}, u32[]{:S(2)}) collective-permute-start(bf16[16,1024]{1,0:T(8,128)(2,1)S(1)} %convert_element_type.136), channel_id=1, source_target_pairs={{15,0},{0,1},{1,2},{2,3},{3,4},{4,5},{5,6},{6,7},{7,8},{8,9},{9,10... | collective-permute-start | bytes 98312 | tf_op jit(solution)/shard_map/while/body/eval_jaxpr/ppermute | solution.py:13
  78.3 6.5 %collective-permute-start = (bf16[16,1024]{1,0:T(8,128)(2,1)S(1)}, bf16[16,1024]{1,0:T(8,128)(2,1)S(1)}, u32[]{:S(2)}, u32[]{:S(2)}) collective-permute-start(bf16[16,1024]{1,0:T(8,128)(2,1)S(1)} %copy.90), channel_id=1, source_target_pairs={{15,0},{0,1},{1,2},{2,3},{3,4},{4,5},{5,6},{6,7},{7,8},{8,9},{9,10... | collective-permute-start | bytes 98312 | tf_op jit(solution)/shard_map/while/body/eval_jaxpr/ppermute | solution.py:13
  78.4 6.4 %collective-permute-start.1 = (bf16[16,16]{0,1:T(8,128)(2,1)S(1)}, bf16[16,16]{0,1:T(8,128)(2,1)S(1)}, u32[]{:S(2)}, u32[]{:S(2)}) collective-permute-start(bf16[16,16]{0,1:T(8,128)(2,1)S(1)} %get-tuple-element.154), channel_id=1, source_target_pairs={{15,0},{0,1},{1,2},{2,3},{3,4},{4,5},{5,6},{6,7},{7,8},{8,9},{9,10... | collective-permute-start | bytes 1544 | tf_op jit(solution)/shard_map/while/body/eval_jaxpr/ppermute | solution.py:13
  78.5 6.3 %collective-permute-start.2 = (bf16[16,16]{0,1:T(8,128)(2,1)S(1)}, bf16[16,16]{0,1:T(8,128)(2,1)S(1)}, u32[]{:S(2)}, u32[]{:S(2)}) collective-permute-start(bf16[16,16]{0,1:T(8,128)(2,1)S(1)} %get-tuple-element.157), channel_id=1, source_target_pairs={{15,0},{0,1},{1,2},{2,3},{3,4},{4,5},{5,6},{6,7},{7,8},{8,9},{9,10... | collective-permute-start | bytes 1544 | tf_op jit(solution)/shard_map/while/body/eval_jaxpr/ppermute | solution.py:13
  86.0 6.5 %collective-permute-start.3 = (bf16[16,1024]{1,0:T(8,128)(2,1)S(1)}, bf16[16,1024]{1,0:T(8,128)(2,1)S(1)}, u32[]{:S(2)}, u32[]{:S(2)}) collective-permute-start(bf16[16,1024]{1,0:T(8,128)(2,1)S(1)} %convert_element_type.136), channel_id=1, source_target_pairs={{15,0},{0,1},{1,2},{2,3},{3,4},{4,5},{5,6},{6,7},{7,8},{8,9},{9,10... | collective-permute-start | bytes 98312 | tf_op jit(solution)/shard_map/while/body/eval_jaxpr/ppermute | solution.py:13
  86.1 6.5 %collective-permute-start = (bf16[16,1024]{1,0:T(8,128)(2,1)S(1)}, bf16[16,1024]{1,0:T(8,128)(2,1)S(1)}, u32[]{:S(2)}, u32[]{:S(2)}) collective-permute-start(bf16[16,1024]{1,0:T(8,128)(2,1)S(1)} %copy.90), channel_id=1, source_target_pairs={{15,0},{0,1},{1,2},{2,3},{3,4},{4,5},{5,6},{6,7},{7,8},{8,9},{9,10... | collective-permute-start | bytes 98312 | tf_op jit(solution)/shard_map/while/body/eval_jaxpr/ppermute | solution.py:13
  86.2 6.4 %collective-permute-start.1 = (bf16[16,16]{0,1:T(8,128)(2,1)S(1)}, bf16[16,16]{0,1:T(8,128)(2,1)S(1)}, u32[]{:S(2)}, u32[]{:S(2)}) collective-permute-start(bf16[16,16]{0,1:T(8,128)(2,1)S(1)} %get-tuple-element.154), channel_id=1, source_target_pairs={{15,0},{0,1},{1,2},{2,3},{3,4},{4,5},{5,6},{6,7},{7,8},{8,9},{9,10... | collective-permute-start | bytes 1544 | tf_op jit(solution)/shard_map/while/body/eval_jaxpr/ppermute | solution.py:13
  93.8 6.5 %collective-permute-start.3 = (bf16[16,1024]{1,0:T(8,128)(2,1)S(1)}, bf16[16,1024]{1,0:T(8,128)(2,1)S(1)}, u32[]{:S(2)}, u32[]{:S(2)}) collective-permute-start(bf16[16,1024]{1,0:T(8,128)(2,1)S(1)} %convert_element_type.136), channel_id=1, source_target_pairs={{15,0},{0,1},{1,2},{2,3},{3,4},{4,5},{5,6},{6,7},{7,8},{8,9},{9,10... | collective-permute-start | bytes 98312 | tf_op jit(solution)/shard_map/while/body/eval_jaxpr/ppermute | solution.py:13
  93.9 6.5 %collective-permute-start = (bf16[16,1024]{1,0:T(8,128)(2,1)S(1)}, bf16[16,1024]{1,0:T(8,128)(2,1)S(1)}, u32[]{:S(2)}, u32[]{:S(2)}) collective-permute-start(bf16[16,1024]{1,0:T(8,128)(2,1)S(1)} %copy.90), channel_id=1, source_target_pairs={{15,0},{0,1},{1,2},{2,3},{3,4},{4,5},{5,6},{6,7},{7,8},{8,9},{9,10... | collective-permute-start | bytes 98312 | tf_op jit(solution)/shard_map/while/body/eval_jaxpr/ppermute | solution.py:13
  93.9 6.4 %collective-permute-start.1 = (bf16[16,16]{0,1:T(8,128)(2,1)S(1)}, bf16[16,16]{0,1:T(8,128)(2,1)S(1)}, u32[]{:S(2)}, u32[]{:S(2)}) collective-permute-start(bf16[16,16]{0,1:T(8,128)(2,1)S(1)} %get-tuple-element.154), channel_id=1, source_target_pairs={{15,0},{0,1},{1,2},{2,3},{3,4},{4,5},{5,6},{6,7},{7,8},{8,9},{9,10... | collective-permute-start | bytes 1544 | tf_op jit(solution)/shard_map/while/body/eval_jaxpr/ppermute | solution.py:13
  101.6 6.5 %collective-permute-start.3 = (bf16[16,1024]{1,0:T(8,128)(2,1)S(1)}, bf16[16,1024]{1,0:T(8,128)(2,1)S(1)}, u32[]{:S(2)}, u32[]{:S(2)}) collective-permute-start(bf16[16,1024]{1,0:T(8,128)(2,1)S(1)} %convert_element_type.136), channel_id=1, source_target_pairs={{15,0},{0,1},{1,2},{2,3},{3,4},{4,5},{5,6},{6,7},{7,8},{8,9},{9,10... | collective-permute-start | bytes 98312 | tf_op jit(solution)/shard_map/while/body/eval_jaxpr/ppermute | solution.py:13
  101.6 6.5 %collective-permute-start = (bf16[16,1024]{1,0:T(8,128)(2,1)S(1)}, bf16[16,1024]{1,0:T(8,128)(2,1)S(1)}, u32[]{:S(2)}, u32[]{:S(2)}) collective-permute-start(bf16[16,1024]{1,0:T(8,128)(2,1)S(1)} %copy.90), channel_id=1, source_target_pairs={{15,0},{0,1},{1,2},{2,3},{3,4},{4,5},{5,6},{6,7},{7,8},{8,9},{9,10... | collective-permute-start | bytes 98312 | tf_op jit(solution)/shard_map/while/body/eval_jaxpr/ppermute | solution.py:13
  101.7 6.4 %collective-permute-start.1 = (bf16[16,16]{0,1:T(8,128)(2,1)S(1)}, bf16[16,16]{0,1:T(8,128)(2,1)S(1)}, u32[]{:S(2)}, u32[]{:S(2)}) collective-permute-start(bf16[16,16]{0,1:T(8,128)(2,1)S(1)} %get-tuple-element.154), channel_id=1, source_target_pairs={{15,0},{0,1},{1,2},{2,3},{3,4},{4,5},{5,6},{6,7},{7,8},{8,9},{9,10... | collective-permute-start | bytes 1544 | tf_op jit(solution)/shard_map/while/body/eval_jaxpr/ppermute | solution.py:13
  109.3 6.5 %collective-permute-start.3 = (bf16[16,1024]{1,0:T(8,128)(2,1)S(1)}, bf16[16,1024]{1,0:T(8,128)(2,1)S(1)}, u32[]{:S(2)}, u32[]{:S(2)}) collective-permute-start(bf16[16,1024]{1,0:T(8,128)(2,1)S(1)} %convert_element_type.136), channel_id=1, source_target_pairs={{15,0},{0,1},{1,2},{2,3},{3,4},{4,5},{5,6},{6,7},{7,8},{8,9},{9,10... | collective-permute-start | bytes 98312 | tf_op jit(solution)/shard_map/while/body/eval_jaxpr/ppermute | solution.py:13
  109.4 6.5 %collective-permute-start = (bf16[16,1024]{1,0:T(8,128)(2,1)S(1)}, bf16[16,1024]{1,0:T(8,128)(2,1)S(1)}, u32[]{:S(2)}, u32[]{:S(2)}) collective-permute-start(bf16[16,1024]{1,0:T(8,128)(2,1)S(1)} %copy.90), channel_id=1, source_target_pairs={{15,0},{0,1},{1,2},{2,3},{3,4},{4,5},{5,6},{6,7},{7,8},{8,9},{9,10... | collective-permute-start | bytes 98312 | tf_op jit(solution)/shard_map/while/body/eval_jaxpr/ppermute | solution.py:13
  109.4 6.4 %collective-permute-start.1 = (bf16[16,16]{0,1:T(8,128)(2,1)S(1)}, bf16[16,16]{0,1:T(8,128)(2,1)S(1)}, u32[]{:S(2)}, u32[]{:S(2)}) collective-permute-start(bf16[16,16]{0,1:T(8,128)(2,1)S(1)} %get-tuple-element.154), channel_id=1, source_target_pairs={{15,0},{0,1},{1,2},{2,3},{3,4},{4,5},{5,6},{6,7},{7,8},{8,9},{9,10... | collective-permute-start | bytes 1544 | tf_op jit(solution)/shard_map/while/body/eval_jaxpr/ppermute | solution.py:13
  117.1 6.5 %collective-permute-start.3 = (bf16[16,1024]{1,0:T(8,128)(2,1)S(1)}, bf16[16,1024]{1,0:T(8,128)(2,1)S(1)}, u32[]{:S(2)}, u32[]{:S(2)}) collective-permute-start(bf16[16,1024]{1,0:T(8,128)(2,1)S(1)} %convert_element_type.136), channel_id=1, source_target_pairs={{15,0},{0,1},{1,2},{2,3},{3,4},{4,5},{5,6},{6,7},{7,8},{8,9},{9,10... | collective-permute-start | bytes 98312 | tf_op jit(solution)/shard_map/while/body/eval_jaxpr/ppermute | solution.py:13
  117.1 6.5 %collective-permute-start = (bf16[16,1024]{1,0:T(8,128)(2,1)S(1)}, bf16[16,1024]{1,0:T(8,128)(2,1)S(1)}, u32[]{:S(2)}, u32[]{:S(2)}) collective-permute-start(bf16[16,1024]{1,0:T(8,128)(2,1)S(1)} %copy.90), channel_id=1, source_target_pairs={{15,0},{0,1},{1,2},{2,3},{3,4},{4,5},{5,6},{6,7},{7,8},{8,9},{9,10... | collective-permute-start | bytes 98312 | tf_op jit(solution)/shard_map/while/body/eval_jaxpr/ppermute | solution.py:13
  117.2 6.4 %collective-permute-start.1 = (bf16[16,16]{0,1:T(8,128)(2,1)S(1)}, bf16[16,16]{0,1:T(8,128)(2,1)S(1)}, u32[]{:S(2)}, u32[]{:S(2)}) collective-permute-start(bf16[16,16]{0,1:T(8,128)(2,1)S(1)} %get-tuple-element.154), channel_id=1, source_target_pairs={{15,0},{0,1},{1,2},{2,3},{3,4},{4,5},{5,6},{6,7},{7,8},{8,9},{9,10... | collective-permute-start | bytes 1544 | tf_op jit(solution)/shard_map/while/body/eval_jaxpr/ppermute | solution.py:13
  124.8 6.5 %collective-permute-start.3 = (bf16[16,1024]{1,0:T(8,128)(2,1)S(1)}, bf16[16,1024]{1,0:T(8,128)(2,1)S(1)}, u32[]{:S(2)}, u32[]{:S(2)}) collective-permute-start(bf16[16,1024]{1,0:T(8,128)(2,1)S(1)} %convert_element_type.136), channel_id=1, source_target_pairs={{15,0},{0,1},{1,2},{2,3},{3,4},{4,5},{5,6},{6,7},{7,8},{8,9},{9,10... | collective-permute-start | bytes 98312 | tf_op jit(solution)/shard_map/while/body/eval_jaxpr/ppermute | solution.py:13
  124.9 6.5 %collective-permute-start = (bf16[16,1024]{1,0:T(8,128)(2,1)S(1)}, bf16[16,1024]{1,0:T(8,128)(2,1)S(1)}, u32[]{:S(2)}, u32[]{:S(2)}) collective-permute-start(bf16[16,1024]{1,0:T(8,128)(2,1)S(1)} %copy.90), channel_id=1, source_target_pairs={{15,0},{0,1},{1,2},{2,3},{3,4},{4,5},{5,6},{6,7},{7,8},{8,9},{9,10... | collective-permute-start | bytes 98312 | tf_op jit(solution)/shard_map/while/body/eval_jaxpr/ppermute | solution.py:13
  125.0 6.4 %collective-permute-start.1 = (bf16[16,16]{0,1:T(8,128)(2,1)S(1)}, bf16[16,16]{0,1:T(8,128)(2,1)S(1)}, u32[]{:S(2)}, u32[]{:S(2)}) collective-permute-start(bf16[16,16]{0,1:T(8,128)(2,1)S(1)} %get-tuple-element.154), channel_id=1, source_target_pairs={{15,0},{0,1},{1,2},{2,3},{3,4},{4,5},{5,6},{6,7},{7,8},{8,9},{9,10... | collective-permute-start | bytes 1544 | tf_op jit(solution)/shard_map/while/body/eval_jaxpr/ppermute | solution.py:13
  132.6 6.5 %collective-permute-start.3 = (bf16[16,1024]{1,0:T(8,128)(2,1)S(1)}, bf16[16,1024]{1,0:T(8,128)(2,1)S(1)}, u32[]{:S(2)}, u32[]{:S(2)}) collective-permute-start(bf16[16,1024]{1,0:T(8,128)(2,1)S(1)} %convert_element_type.136), channel_id=1, source_target_pairs={{15,0},{0,1},{1,2},{2,3},{3,4},{4,5},{5,6},{6,7},{7,8},{8,9},{9,10... | collective-permute-start | bytes 98312 | tf_op jit(solution)/shard_map/while/body/eval_jaxpr/ppermute | solution.py:13
  132.7 6.5 %collective-permute-start = (bf16[16,1024]{1,0:T(8,128)(2,1)S(1)}, bf16[16,1024]{1,0:T(8,128)(2,1)S(1)}, u32[]{:S(2)}, u32[]{:S(2)}) collective-permute-start(bf16[16,1024]{1,0:T(8,128)(2,1)S(1)} %copy.90), channel_id=1, source_target_pairs={{15,0},{0,1},{1,2},{2,3},{3,4},{4,5},{5,6},{6,7},{7,8},{8,9},{9,10... | collective-permute-start | bytes 98312 | tf_op jit(solution)/shard_map/while/body/eval_jaxpr/ppermute | solution.py:13
  132.7 6.4 %collective-permute-start.1 = (bf16[16,16]{0,1:T(8,128)(2,1)S(1)}, bf16[16,16]{0,1:T(8,128)(2,1)S(1)}, u32[]{:S(2)}, u32[]{:S(2)}) collective-permute-start(bf16[16,16]{0,1:T(8,128)(2,1)S(1)} %get-tuple-element.154), channel_id=1, source_target_pairs={{15,0},{0,1},{1,2},{2,3},{3,4},{4,5},{5,6},{6,7},{7,8},{8,9},{9,10... | collective-permute-start | bytes 1544 | tf_op jit(solution)/shard_map/while/body/eval_jaxpr/ppermute | solution.py:13
  140.4 6.5 %collective-permute-start.3 = (bf16[16,1024]{1,0:T(8,128)(2,1)S(1)}, bf16[16,1024]{1,0:T(8,128)(2,1)S(1)}, u32[]{:S(2)}, u32[]{:S(2)}) collective-permute-start(bf16[16,1024]{1,0:T(8,128)(2,1)S(1)} %convert_element_type.136), channel_id=1, source_target_pairs={{15,0},{0,1},{1,2},{2,3},{3,4},{4,5},{5,6},{6,7},{7,8},{8,9},{9,10... | collective-permute-start | bytes 98312 | tf_op jit(solution)/shard_map/while/body/eval_jaxpr/ppermute | solution.py:13
  140.4 6.5 %collective-permute-start = (bf16[16,1024]{1,0:T(8,128)(2,1)S(1)}, bf16[16,1024]{1,0:T(8,128)(2,1)S(1)}, u32[]{:S(2)}, u32[]{:S(2)}) collective-permute-start(bf16[16,1024]{1,0:T(8,128)(2,1)S(1)} %copy.90), channel_id=1, source_target_pairs={{15,0},{0,1},{1,2},{2,3},{3,4},{4,5},{5,6},{6,7},{7,8},{8,9},{9,10... | collective-permute-start | bytes 98312 | tf_op jit(solution)/shard_map/while/body/eval_jaxpr/ppermute | solution.py:13
  140.5 6.4 %collective-permute-start.1 = (bf16[16,16]{0,1:T(8,128)(2,1)S(1)}, bf16[16,16]{0,1:T(8,128)(2,1)S(1)}, u32[]{:S(2)}, u32[]{:S(2)}) collective-permute-start(bf16[16,16]{0,1:T(8,128)(2,1)S(1)} %get-tuple-element.154), channel_id=1, source_target_pairs={{15,0},{0,1},{1,2},{2,3},{3,4},{4,5},{5,6},{6,7},{7,8},{8,9},{9,10... | collective-permute-start | bytes 1544 | tf_op jit(solution)/shard_map/while/body/eval_jaxpr/ppermute | solution.py:13
  148.1 6.5 %collective-permute-start.3 = (bf16[16,1024]{1,0:T(8,128)(2,1)S(1)}, bf16[16,1024]{1,0:T(8,128)(2,1)S(1)}, u32[]{:S(2)}, u32[]{:S(2)}) collective-permute-start(bf16[16,1024]{1,0:T(8,128)(2,1)S(1)} %convert_element_type.136), channel_id=1, source_target_pairs={{15,0},{0,1},{1,2},{2,3},{3,4},{4,5},{5,6},{6,7},{7,8},{8,9},{9,10... | collective-permute-start | bytes 98312 | tf_op jit(solution)/shard_map/while/body/eval_jaxpr/ppermute | solution.py:13
  148.2 6.5 %collective-permute-start = (bf16[16,1024]{1,0:T(8,128)(2,1)S(1)}, bf16[16,1024]{1,0:T(8,128)(2,1)S(1)}, u32[]{:S(2)}, u32[]{:S(2)}) collective-permute-start(bf16[16,1024]{1,0:T(8,128)(2,1)S(1)} %copy.90), channel_id=1, source_target_pairs={{15,0},{0,1},{1,2},{2,3},{3,4},{4,5},{5,6},{6,7},{7,8},{8,9},{9,10... | collective-permute-start | bytes 98312 | tf_op jit(solution)/shard_map/while/body/eval_jaxpr/ppermute | solution.py:13
  148.3 6.4 %collective-permute-start.1 = (bf16[16,16]{0,1:T(8,128)(2,1)S(1)}, bf16[16,16]{0,1:T(8,128)(2,1)S(1)}, u32[]{:S(2)}, u32[]{:S(2)}) collective-permute-start(bf16[16,16]{0,1:T(8,128)(2,1)S(1)} %get-tuple-element.154), channel_id=1, source_target_pairs={{15,0},{0,1},{1,2},{2,3},{3,4},{4,5},{5,6},{6,7},{7,8},{8,9},{9,10... | collective-permute-start | bytes 1544 | tf_op jit(solution)/shard_map/while/body/eval_jaxpr/ppermute | solution.py:13
  155.9 6.5 %collective-permute-start.3 = (bf16[16,1024]{1,0:T(8,128)(2,1)S(1)}, bf16[16,1024]{1,0:T(8,128)(2,1)S(1)}, u32[]{:S(2)}, u32[]{:S(2)}) collective-permute-start(bf16[16,1024]{1,0:T(8,128)(2,1)S(1)} %convert_element_type.136), channel_id=1, source_target_pairs={{15,0},{0,1},{1,2},{2,3},{3,4},{4,5},{5,6},{6,7},{7,8},{8,9},{9,10... | collective-permute-start | bytes 98312 | tf_op jit(solution)/shard_map/while/body/eval_jaxpr/ppermute | solution.py:13
  156.0 6.5 %collective-permute-start = (bf16[16,1024]{1,0:T(8,128)(2,1)S(1)}, bf16[16,1024]{1,0:T(8,128)(2,1)S(1)}, u32[]{:S(2)}, u32[]{:S(2)}) collective-permute-start(bf16[16,1024]{1,0:T(8,128)(2,1)S(1)} %copy.90), channel_id=1, source_target_pairs={{15,0},{0,1},{1,2},{2,3},{3,4},{4,5},{5,6},{6,7},{7,8},{8,9},{9,10... | collective-permute-start | bytes 98312 | tf_op jit(solution)/shard_map/while/body/eval_jaxpr/ppermute | solution.py:13
  156.0 6.4 %collective-permute-start.1 = (bf16[16,16]{0,1:T(8,128)(2,1)S(1)}, bf16[16,16]{0,1:T(8,128)(2,1)S(1)}, u32[]{:S(2)}, u32[]{:S(2)}) collective-permute-start(bf16[16,16]{0,1:T(8,128)(2,1)S(1)} %get-tuple-element.154), channel_id=1, source_target_pairs={{15,0},{0,1},{1,2},{2,3},{3,4},{4,5},{5,6},{6,7},{7,8},{8,9},{9,10... | collective-permute-start | bytes 1544 | tf_op jit(solution)/shard_map/while/body/eval_jaxpr/ppermute | solution.py:13
  163.7 6.5 %collective-permute-start.3 = (bf16[16,1024]{1,0:T(8,128)(2,1)S(1)}, bf16[16,1024]{1,0:T(8,128)(2,1)S(1)}, u32[]{:S(2)}, u32[]{:S(2)}) collective-permute-start(bf16[16,1024]{1,0:T(8,128)(2,1)S(1)} %convert_element_type.136), channel_id=1, source_target_pairs={{15,0},{0,1},{1,2},{2,3},{3,4},{4,5},{5,6},{6,7},{7,8},{8,9},{9,10... | collective-permute-start | bytes 98312 | tf_op jit(solution)/shard_map/while/body/eval_jaxpr/ppermute | solution.py:13
  163.7 6.5 %collective-permute-start = (bf16[16,1024]{1,0:T(8,128)(2,1)S(1)}, bf16[16,1024]{1,0:T(8,128)(2,1)S(1)}, u32[]{:S(2)}, u32[]{:S(2)}) collective-permute-start(bf16[16,1024]{1,0:T(8,128)(2,1)S(1)} %copy.90), channel_id=1, source_target_pairs={{15,0},{0,1},{1,2},{2,3},{3,4},{4,5},{5,6},{6,7},{7,8},{8,9},{9,10... | collective-permute-start | bytes 98312 | tf_op jit(solution)/shard_map/while/body/eval_jaxpr/ppermute | solution.py:13
  163.8 6.4 %collective-permute-start.1 = (bf16[16,16]{0,1:T(8,128)(2,1)S(1)}, bf16[16,16]{0,1:T(8,128)(2,1)S(1)}, u32[]{:S(2)}, u32[]{:S(2)}) collective-permute-start(bf16[16,16]{0,1:T(8,128)(2,1)S(1)} %get-tuple-element.154), channel_id=1, source_target_pairs={{15,0},{0,1},{1,2},{2,3},{3,4},{4,5},{5,6},{6,7},{7,8},{8,9},{9,10... | collective-permute-start | bytes 1544 | tf_op jit(solution)/shard_map/while/body/eval_jaxpr/ppermute | solution.py:13
  171.4 6.4 %collective-permute-start.4 = (bf16[16,1024]{1,0:T(8,128)(2,1)S(1)}, bf16[16,1024]{1,0:T(8,128)(2,1)S(1)}, u32[]{:S(2)}, u32[]{:S(2)}) collective-permute-start(bf16[16,1024]{1,0:T(8,128)(2,1)S(1)} %convert_element_type.86), channel_id=1, source_target_pairs={{15,0},{0,1},{1,2},{2,3},{3,4},{4,5},{5,6},{6,7},{7,8},{8,9},{9,10... | collective-permute-start | bytes 98312 | tf_op jit(solution)/shard_map/ppermute | solution.py:13
  (22 other events, 210.4 us)
where the time goes:
time: 181 us; the launch traced here: 180 us
  waiting for transfers between devices  115 us (64%)
  starting transfers between devices  23.6 us (13%)
  local copies, waits for them, and re-layouts  17.7 us (10%)
  matrix products  16.3 us (9%)
  other arithmetic  5.59 us (3%)
    ppermute x62, waiting for transfers between devices, shifted(): return lax.ppermute(block, axis, route)  93.7 us
    all_to_all x1, waiting for transfers between devices, local(): lax.all_to_all(tokens.reshape(per_peer, cycle_size, model_width), 'blk',...  18 us
    ppermute x62, starting transfers between devices, shifted(): return lax.ppermute(block, axis, route)  11.9 us
    all_to_all x1, starting transfers between devices, local(): lax.all_to_all(patch_of_row.reshape(per_peer, cycle_size), 'blk', split_a...  7.39 us
    dot_general x16, matrix products, absorb(): jnp.einsum('lhk,khd->lhd', weights.astype(jnp.bfloat16), value_heads, pre...  5.02 us
    all_to_all x1, starting transfers between devices, local(): lax.all_to_all(tokens.reshape(per_peer, cycle_size, model_width), 'blk',...  4.33 us
    dot_general x16, matrix products, absorb(): jnp.einsum('lhd,khd->lhk', tile_heads, key_heads, preferred_element_type=...  4.1 us
  transfers between devices with their start and end apart: 64, of which 19 were waited for; matrix products, arithmetic and copies ran while one was open for 4% of the time, Pallas kernels for 0%

commit v1 on v0

v1 whole, which is shorter than its diff:
```python
import jax
import jax.numpy as jnp
from jax import lax
from jax.sharding import PartitionSpec as P

HEADS = 16
CONTRASTS = 4


def split_exact(value, upward):
    high = value.astype(jnp.bfloat16)
    rest = value - high.astype(jnp.float32)
    if upward:
        rest = rest + jnp.abs(rest) * (2.0 ** -8)
    low = rest.astype(jnp.bfloat16)
    return high, low


def joined_rows(tokens, patch_of_row, contrast_gain, cycle_size, my_index):
    tok_rows, model_width = tokens.shape
    per_peer = tok_rows // cycle_size
    patches_dev = tok_rows // CONTRASTS
    all_ids = lax.all_gather(patch_of_row, "blk", tiled=True)
    received = lax.all_to_all(
        tokens.reshape(per_peer, cycle_size, model_width),
        "blk",
        split_axis=1,
        concat_axis=1,
        tiled=True,
    )
    received_ids = jnp.transpose(
        lax.dynamic_index_in_dim(
            all_ids.reshape(cycle_size, per_peer, cycle_size), my_index, axis=2, keepdims=False
        )
    )
    source_dev = lax.broadcasted_iota(jnp.int32, (per_peer, cycle_size), 1)
    row_step = lax.broadcasted_iota(jnp.int32, (per_peer, cycle_size), 0)
    slot_index = source_dev * tok_rows + my_index + cycle_size * row_step
    contrast_id = slot_index // (patches_dev * cycle_size)
    target_row = (contrast_id * patches_dev + received_ids - my_index * patches_dev).reshape(
        tok_rows
    )
    inverse = (
        jnp.zeros((tok_rows,), jnp.int32).at[target_row].set(jnp.arange(tok_rows, dtype=jnp.int32))
    )
    arranged = received.reshape(tok_rows, model_width)[inverse].reshape(
        CONTRASTS, patches_dev, model_width
    )
    return jnp.sum(
        arranged.astype(jnp.float32) * contrast_gain.astype(jnp.float32)[:, None, :], axis=0
    )


def local(tokens, patch_of_row, latents, contrast_gain, norm_gain, w_query, w_key, w_value, w_out):
    cycle_size = lax.axis_size("blk")
    my_index = lax.axis_index("blk")
    model_width = tokens.shape[1]
    head_count = HEADS
    head_width = model_width // head_count
    lat_rows = latents.shape[0]

    queries = (
        jnp.dot(latents, w_query, preferred_element_type=jnp.float32) * head_width ** (-0.5)
    ).astype(jnp.bfloat16)
    all_queries = lax.all_gather(queries, "blk", tiled=True)
    all_lat = all_queries.shape[0]

    joined = joined_rows(tokens, patch_of_row, contrast_gain, cycle_size, my_index)
    patches_dev = joined.shape[0]
    inverse_rms = lax.rsqrt(jnp.mean(joined * joined, axis=-1, keepdims=True) + 1e-05)
    normed = (joined * inverse_rms * norm_gain.astype(jnp.float32)).astype(jnp.bfloat16)
    key_rows = jnp.dot(normed, w_key, preferred_element_type=jnp.float32).astype(jnp.bfloat16)
    value_rows = jnp.dot(normed, w_value, preferred_element_type=jnp.float32).astype(jnp.bfloat16)
    key_heads = key_rows.reshape(patches_dev, head_count, head_width)
    value_heads = value_rows.reshape(patches_dev, head_count, head_width)

    query_heads = all_queries.reshape(all_lat, head_count, head_width)
    scores = jnp.einsum(
        "lhd,khd->lhk", query_heads, key_heads, preferred_element_type=jnp.float32
    )
    maxima = jnp.max(scores, axis=-1)
    max_high, max_low = split_exact(maxima, True)
    shift = max_high.astype(jnp.float32) + max_low.astype(jnp.float32)
    weights = jnp.exp(scores - shift[..., None])
    totals = jnp.sum(weights, axis=-1)
    tot_high, tot_low = split_exact(totals, False)
    summed = jnp.einsum(
        "lhk,khd->lhd",
        weights.astype(jnp.bfloat16),
        value_heads,
        preferred_element_type=jnp.float32,
    )
    stats = jnp.stack([max_high, max_low, tot_high, tot_low], axis=-1).reshape(
        cycle_size, lat_rows, head_count * 4
    )
    payload = jnp.concatenate(
        [summed.astype(jnp.bfloat16).reshape(cycle_size, lat_rows, model_width), stats], axis=-1
    )
    gathered = lax.all_to_all(payload, "blk", split_axis=0, concat_axis=0, tiled=True)
    part_sums = gathered[:, :, :model_width].astype(jnp.float32).reshape(
        cycle_size, lat_rows, head_count, head_width
    )
    part_stats = gathered[:, :, model_width:].astype(jnp.float32).reshape(
        cycle_size, lat_rows, head_count, 4
    )
    part_max = part_stats[..., 0] + part_stats[..., 1]
    part_tot = part_stats[..., 2] + part_stats[..., 3]
    top = jnp.max(part_max, axis=0)
    factor = jnp.exp(part_max - top[None])
    total = jnp.sum(part_tot * factor, axis=0)
    accum = jnp.sum(part_sums * factor[..., None], axis=0)
    attended = (accum / total[..., None]).reshape(lat_rows, model_width).astype(jnp.bfloat16)
    mixed = latents.astype(jnp.float32) + jnp.dot(
        attended, w_out, preferred_element_type=jnp.float32
    )
    return mixed.astype(jnp.bfloat16)


def solution(mesh):
    in_specs = (
        P(("grp", "blk"), None),
        P(("grp", "blk")),
        P("blk", None),
        P(),
        P(),
        P(),
        P(),
        P(),
        P(),
    )
    out_specs = P(("grp", "blk"), None)
    return jax.shard_map(local, mesh=mesh, in_specs=in_specs, out_specs=out_specs, check_vma=False)
```

time: 181 us -> 123 us (0.68)
  waiting for transfers between devices: 115 us -> 0.01 us
  blocking collectives: 0 us -> 76.3 us
  starting transfers between devices: 23.6 us -> 7.44 us
  matrix products: 16.3 us -> 10.1 us
  local copies, waits for them, and re-layouts: 17.7 us -> 23.5 us
    ppermute x62 -> x0, waiting for transfers between devices: 93.7 us -> none  [shifted(): return lax.ppermute(block, axis, route)]
    all_gather x0 -> x2, blocking collectives: none -> 56.5 us  [the longest x1 33.5 us: joined_rows(): all_ids = lax.all_gather(patch_of_row, 'blk', tiled=True)]
    all_to_all x2 -> x1, waiting for transfers between devices: 21.5 us -> 0.01 us  [joined_rows(): lax.all_to_all(tokens.reshape(per_peer, cycle_size, model_width), 'blk',...]
    all_to_all x0 -> x1, blocking collectives: none -> 19.8 us  [local(): lax.all_to_all(payload, 'blk', split_axis=0, concat_axis=0, tiled=True)]
    ppermute x62 -> x0, starting transfers between devices: 11.9 us -> none  [shifted(): return lax.ppermute(block, axis, route)]
    dot_general x32 -> x2, matrix products: 9.11 us -> 4.48 us  [the longest x1 2.89 us: local(): jnp.einsum('lhk,khd->lhd', weights.astype(jnp.bfloat16), value_heads, pre...]
    all_to_all x2 -> x1, starting transfers between devices: 11.7 us -> 7.44 us  [joined_rows(): lax.all_to_all(tokens.reshape(per_peer, cycle_size, model_width), 'blk',...]
    mul x0 -> x3, local copies, waits for them, and re-layouts: none -> 4.08 us  [local(): accum = jnp.sum(part_sums * factor[..., None], axis=0)]
  transfers between devices with their start and end apart: 64 -> 1, of which waited for: 19 -> 0; matrix products, arithmetic and copies ran while one was open for 4% -> 5% of each run, Pallas kernels for 0% -> 0%
where the time goes in v1:
time: 123 us; the launch traced here: 122 us
  blocking collectives  76.3 us (62%)
  local copies, waits for them, and re-layouts  23.5 us (19%)
  matrix products  10.1 us (8%)
  starting transfers between devices  7.44 us (6%)
  other arithmetic  4.65 us (4%)
    all_gather x1, blocking collectives, joined_rows(): all_ids = lax.all_gather(patch_of_row, 'blk', tiled=True)  33.5 us
    all_gather x1, blocking collectives, local(): all_queries = lax.all_gather(queries, 'blk', tiled=True)  22.9 us
    all_to_all x1, blocking collectives, local(): lax.all_to_all(payload, 'blk', split_axis=0, concat_axis=0, tiled=True)  19.8 us
    all_to_all x1, starting transfers between devices, joined_rows(): lax.all_to_all(tokens.reshape(per_peer, cycle_size, model_width), 'blk',...  7.44 us
    mul x3, local copies, waits for them, and re-layouts, local(): accum = jnp.sum(part_sums * factor[..., None], axis=0)  4.08 us
    reshape x1, local copies, waits for them, and re-layouts, joined_rows(): tokens.reshape(per_peer, cycle_size, model_width)  2.98 us
    dot_general x1, matrix products, local(): jnp.einsum('lhk,khd->lhd', weights.astype(jnp.bfloat16), value_heads, pre...  2.89 us
    gather x1, local copies, waits for them, and re-layouts, joined_rows(): received.reshape(tok_rows, model_width)[inverse]  2.79 us
  transfers between devices with their start and end apart: 1, of which 0 were waited for; matrix products, arithmetic and copies ran while one was open for 5% of the time, Pallas kernels for 0%

profile of v1, /device:TPU:0, one launch (start us, length us, event | category | flops | bytes accessed | tf_op | source)
XLA Modules:
  0.0 122.3 jit_solution(12066292924014967609)
XLA Ops:
  0.0 3.0 %copy.62 = bf16[32,16,1024]{2,0,1:T(8,128)(2,1)} copy(bf16[32,16,1024]{2,1,0:T(8,128)(2,1)} %bitcast.59) | data formatting | bytes 2097152 | tf_op jit(solution)/shard_map/reshape | solution.py:25
  3.0 7.4 %all-to-all-start = ((bf16[32,16,1024]{2,0,1:T(8,128)(2,1)}), bf16[32,16,1024]{2,0,1:T(8,128)(2,1)}, u32[]{:S(2)}, u32[]{:S(2)}) async-start(bf16[32,16,1024]{2,0,1:T(8,128)(2,1)} %copy.62), calls=%async_computation | async-start | bytes 2097152 | tf_op jit(solution)/shard_map/all_to_all | solution.py:24
  10.5 0.0 copy-done.6
  10.5 0.0 copy-done.8
  10.5 33.5 %all-gather = s32[16,1,512]{2,1,0:T(1,128)S(1)} all-gather(s32[1,1,512]{2,1,0:T(1,128)S(1)} %bitcast.62), channel_id=1, replica_groups=mesh['grp'=2,'blk'=16] {'blk'}, dimensions={0}, use_global_device_ids=true | all-gather | bytes 34816 | tf_op jit(solution)/shard_map/all_gather | solution.py:23
  44.1 0.1 reduce.2
  44.1 0.1 reshape.140
  44.3 0.5 dynamic-slice_reduce_fusion
  44.8 0.1 fusion.16
  44.8 0.1 copy.64
  44.9 0.1 reshape.141
  45.0 2.0 %fusion.5 = bf16[16,1024]{1,0:T(8,128)(2,1)S(1)} fusion(bf16[16,1024]{1,0:T(8,128)(2,1)S(1)} %copy-done.5, bf16[1024,1024]{1,0:T(8,128)(2,1)} %param.14), kind=kOutput, calls=%fused_computation.15 | convolution fusion | flops 33587200 | bytes 2162688 | tf_op jit(solution)/shard_map/dot_general | solution.py:63
  47.0 22.9 %all_gather.7 = bf16[256,1024]{1,0:T(8,128)(2,1)S(1)} all-gather(bf16[16,1024]{1,0:T(8,128)(2,1)S(1)} %fusion.5), channel_id=1, replica_groups=mesh['grp'=2,'blk'=16] {'blk'}, dimensions={0}, use_global_device_ids=true | all-gather | bytes 557056 | tf_op jit(solution)/shard_map/all_gather | solution.py:65
  69.9 1.0 copy.67
  70.9 2.4 %scatter_custom_fusion = s32[512]{0:T(512)S(1)} fusion(s32[512]{0:T(512)S(1)} %bitcast.63, s32[512]{0:T(512)S(1)} %iota.19, s32[]{:T(128)} %constant.15.clone.1), kind=kCustom, calls=%fused_computation.59 | custom fusion | bytes 2052 | tf_op jit(solution)/shard_map/scatter | solution.py:44
  73.4 0.0 all-to-all-done
  73.4 1.8 %copy.63 = bf16[32,16,1024]{2,1,0:T(8,128)(2,1)S(1)} copy(bf16[32,16,1024]{2,0,1:T(8,128)(2,1)} %all-to-all-done) | data formatting | bytes 2097152 | tf_op jit(solution)/shard_map/all_to_all | solution.py:24
  75.2 2.8 %gather_fusion = bf16[512,1024]{1,0:T(8,128)(2,1)} fusion(bf16[512,1024]{1,0:T(8,128)(2,1)S(1)} %bitcast.53, s32[1024]{0:T(1024)S(1)} %pad_clamp_fusion), kind=kCustom, calls=%fused_computation | custom fusion | bytes 2099200 | tf_op jit(solution)/shard_map/gather | solution.py:46
  78.0 1.5 %fusion = f32[128,1024]{1,0:T(8,128)S(1)} fusion(bf16[4,128,1024]{2,1,0:T(8,128)(2,1)} %bitcast.57, f32[4,1024]{1,0:T(4,128)S(1)} %convert_element_type.140), kind=kLoop, calls=%fused_computation.3 | loop fusion | flops 1441792 | bytes 1589248 | tf_op jit(solution)/shard_map/reduce_sum | solution.py:49
  79.5 0.1 multiply_reduce_fusion.1
  79.6 0.0 copy-done
  79.6 0.5 convolution_convert_fusion.1
  80.1 0.8 copy.66
  81.0 1.6 %bitcast_reduce_fusion = (f32[256,16]{0,1:T(8,128)S(1)}, f32[16,128,256]{2,1,0:T(8,128)S(1)}) fusion(bf16[128,16,64]{0,2,1:T(8,128)(2,1)} %bitcast.60, bf16[256,16,64]{0,2,1:T(8,128)(2,1)S(1)} %bitcast.58), kind=kOutput, calls=%fused_computation.5 | convolution fusion | flops 67629056 | bytes 2899968 | tf_op jit(solution)/shard_map/lhd,khd->lhk/dot_general | solution.py:78
  82.6 0.0 copy-start.1
  82.6 1.3 %copy-done.1 = f32[16,128,256]{2,1,0:T(8,128)} copy-done((f32[16,128,256]{2,1,0:T(8,128)}, f32[16,128,256]{2,1,0:T(8,128)S(1)}, u32[]{:S(2)}) %copy-start.1) | copy-done | bytes 2097176
  83.9 0.3 fusion.2
  84.3 0.5 convolution_convert_fusion.2
  84.8 0.2 copy.65
  85.0 2.9 %fusion.4 = bf16[256,16,64]{0,2,1:T(8,128)(2,1)} fusion(bf16[128,16,64]{0,2,1:T(8,128)(2,1)S(1)} %bitcast.61, f32[16,128,256]{2,1,0:T(8,128)} %copy-done.1, f32[256,16]{0,1:T(8,128)S(1)} %convert_add_fusion), kind=kOutput, calls=%fused_computation.10 | convolution fusion | flops 68419584 | bytes 2899968 | tf_op jit(solution)/shard_map/lhk,khd->lhd/dot_general | solution.py:87
  87.9 0.1 pad_maximum_fusion.1
  88.0 0.2 reshape.146
  88.2 0.3 copy.70
  88.5 2.0 %copy.69 = bf16[256,16,64]{2,1,0:T(8,128)(2,1)S(1)} copy(bf16[256,16,64]{0,2,1:T(8,128)(2,1)} %fusion.4) | data formatting | bytes 1048576 | tf_op jit(solution)/shard_map/convert_element_type | solution.py:97
  90.5 1.5 %reshape.145 = bf16[16,16,1024]{2,1,0:T(8,128)(2,1)} reshape(bf16[256,16,64]{2,1,0:T(8,128)(2,1)S(1)} %copy.69) | data formatting | bytes 1048576 | tf_op jit(solution)/shard_map/reshape | solution.py:97
  92.0 1.1 pad_maximum_fusion
  93.1 19.8 %all_to_all.10 = bf16[16,16,1088]{2,1,0:T(8,128)(2,1)S(1)} all-to-all(bf16[16,16,1088]{2,1,0:T(8,128)(2,1)S(1)} %pad_maximum_fusion), channel_id=1, replica_groups=mesh['grp'=2,'blk'=16] {'blk'}, dimensions={0} | all-to-all | bytes 1114112 | tf_op jit(solution)/shard_map/all_to_all | solution.py:99
  112.9 0.8 copy-done.2
  113.7 0.3 copy.71
  114.1 0.1 fusion.11
  114.2 0.1 copy.72
  114.3 0.1 copy.75
  114.4 0.1 div.35
  114.5 0.1 div.36
  114.6 2.0 %mul.113 = f32[16,16,16,64]{3,2,1,0:T(8,128)} broadcast(f32[16,16,16]{2,1,0:T(8,128)S(1)} %copy.72), dimensions={0,1,2} | broadcast | bytes 1064960 | tf_op jit(solution)/shard_map/mul | solution.py:111
  116.5 2.0 %mul.114 = f32[16,16,1024]{2,1,0:T(8,128)S(1)} reshape(f32[16,16,16,64]{3,2,1,0:T(8,128)} %mul.113) | data formatting | bytes 2097152 | tf_op jit(solution)/shard_map/mul | solution.py:111
  118.5 1.2 multiply_reduce_fusion
  119.7 2.6 %fusion.6 = bf16[16,1024]{1,0:T(8,128)(2,1)} fusion(bf16[1024,1024]{1,0:T(8,128)(2,1)} %param.17, bf16[16,1024]{1,0:T(8,128)(2,1)S(1)} %copy-done.5, f32[16,1024]{1,0:T(8,128)S(1)} %multiply_reduce_fusion, f32[16,1024]{1,0:T(8,128)S(1)} %div.36), kind=kOutput, calls=%fused_computation.16 | convolution fusion | flops 33636352 | bytes 2293760 | tf_op jit(solution)/shard_map/dot_general | solution.py:113
  (28 shorter events, 0.2 us)
Async XLA Ops:
  0.0 79.6 %copy-start = (bf16[1024,1024]{1,0:T(8,128)(2,1)S(1)}, bf16[1024,1024]{1,0:T(8,128)(2,1)}, u32[]{:S(2)}) copy-start(bf16[1024,1024]{1,0:T(8,128)(2,1)} %param.15) | copy-start | bytes 6291460
  0.0 10.5 %copy-start.7 = (bf16[1024]{0:T(1024)(128)(2,1)S(1)}, bf16[1024]{0:T(1024)(128)(2,1)}, u32[]{:S(2)}) copy-start(bf16[1024]{0:T(1024)(128)(2,1)} %param.13) | copy-start | bytes 6148
  0.0 10.5 %copy-start.6 = (bf16[4,1024]{1,0:T(4,128)(2,1)S(1)}, bf16[4,1024]{1,0:T(4,128)(2,1)}, u32[]{:S(2)}) copy-start(bf16[4,1024]{1,0:T(4,128)(2,1)} %param.12) | copy-start | bytes 24580
  0.0 10.5 %copy-start.8 = (s32[512]{0:T(512)S(1)}, s32[512]{0:T(512)}, u32[]{:S(2)}) copy-start(s32[512]{0:T(512)} %param.10) | copy-start | bytes 6148
  0.0 45.0 %copy-start.5 = (bf16[16,1024]{1,0:T(8,128)(2,1)S(1)}, bf16[16,1024]{1,0:T(8,128)(2,1)}, u32[]{:S(2)}) copy-start(bf16[16,1024]{1,0:T(8,128)(2,1)} %param.11) | copy-start | bytes 98308
  3.0 70.4 %all-to-all-start = ((bf16[32,16,1024]{2,0,1:T(8,128)(2,1)}), bf16[32,16,1024]{2,0,1:T(8,128)(2,1)}, u32[]{:S(2)}, u32[]{:S(2)}) async-start(bf16[32,16,1024]{2,0,1:T(8,128)(2,1)} %copy.62), calls=%async_computation | async-start | bytes 2097152 | tf_op jit(solution)/shard_map/all_to_all | solution.py:24
  79.5 1.5 %copy-start.4 = (bf16[256,1024]{0,1:T(8,128)(2,1)S(1)}, bf16[256,1024]{0,1:T(8,128)(2,1)}, u32[]{:S(2)}) copy-start(bf16[256,1024]{0,1:T(8,128)(2,1)} %copy.67) | copy-start | bytes 1572868
  81.0 3.3 %copy-start.3 = (bf16[1024,1024]{1,0:T(8,128)(2,1)S(1)}, bf16[1024,1024]{1,0:T(8,128)(2,1)}, u32[]{:S(2)}) copy-start(bf16[1024,1024]{1,0:T(8,128)(2,1)} %param.16) | copy-start | bytes 6291460
  82.6 1.4 %copy-start.1 = (f32[16,128,256]{2,1,0:T(8,128)}, f32[16,128,256]{2,1,0:T(8,128)S(1)}, u32[]{:S(2)}) copy-start(f32[16,128,256]{2,1,0:T(8,128)S(1)} %get-tuple-element.6) | copy-start | bytes 6291460
  112.9 0.8 copy-start.2

commit v2 on v1

v2 whole, which is shorter than its diff:
```python
import jax
import jax.numpy as jnp
from jax import lax
from jax.sharding import PartitionSpec as P

HEADS = 16
CONTRASTS = 4


def joined_rows(tokens, patch_of_row, contrast_gain, cycle_size, my_index):
    tok_rows, model_width = tokens.shape
    per_peer = tok_rows // cycle_size
    patches_dev = tok_rows // CONTRASTS
    all_ids = lax.all_gather(patch_of_row, "blk", tiled=True)
    received = lax.all_to_all(
        tokens.reshape(per_peer, cycle_size, model_width),
        "blk",
        split_axis=1,
        concat_axis=1,
        tiled=True,
    )
    received_ids = jnp.transpose(
        lax.dynamic_index_in_dim(
            all_ids.reshape(cycle_size, per_peer, cycle_size), my_index, axis=2, keepdims=False
        )
    )
    source_dev = lax.broadcasted_iota(jnp.int32, (per_peer, cycle_size), 1)
    row_step = lax.broadcasted_iota(jnp.int32, (per_peer, cycle_size), 0)
    slot_index = source_dev * tok_rows + my_index + cycle_size * row_step
    contrast_id = slot_index // (patches_dev * cycle_size)
    target_row = (contrast_id * patches_dev + received_ids - my_index * patches_dev).reshape(
        tok_rows
    )
    inverse = (
        jnp.zeros((tok_rows,), jnp.int32).at[target_row].set(jnp.arange(tok_rows, dtype=jnp.int32))
    )
    arranged = received.reshape(tok_rows, model_width)[inverse].reshape(
        CONTRASTS, patches_dev, model_width
    )
    return jnp.sum(
        arranged.astype(jnp.float32) * contrast_gain.astype(jnp.float32)[:, None, :], axis=0
    )


def local(tokens, patch_of_row, latents, contrast_gain, norm_gain, w_query, w_key, w_value, w_out):
    cycle_size = lax.axis_size("blk")
    my_index = lax.axis_index("blk")
    model_width = tokens.shape[1]
    head_count = HEADS
    head_width = model_width // head_count
    lat_rows = latents.shape[0]
    copies = cycle_size // head_count
    group_start = (my_index // head_count) * head_count

    queries = (
        jnp.dot(latents, w_query, preferred_element_type=jnp.float32) * head_width ** (-0.5)
    ).astype(jnp.bfloat16)
    query_parts = jnp.transpose(queries.reshape(lat_rows, head_count, head_width), (1, 0, 2))
    got_queries = lax.all_to_all(
        jnp.tile(query_parts, (copies, 1, 1)), "blk", split_axis=0, concat_axis=0, tiled=True
    )
    head_queries = lax.dynamic_slice_in_dim(got_queries, group_start, head_count, axis=0).reshape(
        head_count * lat_rows, head_width
    )

    joined = joined_rows(tokens, patch_of_row, contrast_gain, cycle_size, my_index)
    patches_dev = joined.shape[0]
    inverse_rms = lax.rsqrt(jnp.mean(joined * joined, axis=-1, keepdims=True) + 1e-05)
    normed = (joined * inverse_rms * norm_gain.astype(jnp.float32)).astype(jnp.bfloat16)
    key_rows = jnp.dot(normed, w_key, preferred_element_type=jnp.float32).astype(jnp.bfloat16)
    value_rows = jnp.dot(normed, w_value, preferred_element_type=jnp.float32).astype(jnp.bfloat16)
    pair_parts = jnp.transpose(
        jnp.concatenate(
            [
                key_rows.reshape(patches_dev, head_count, head_width),
                value_rows.reshape(patches_dev, head_count, head_width),
            ],
            axis=-1,
        ),
        (1, 0, 2),
    )
    got_pairs = lax.all_to_all(
        jnp.tile(pair_parts, (copies, 1, 1)), "blk", split_axis=0, concat_axis=0, tiled=True
    ).reshape(cycle_size * patches_dev, 2 * head_width)
    head_keys = got_pairs[:, :head_width]
    head_values = got_pairs[:, head_width:]

    scores = jnp.einsum(
        "ld,kd->lk", head_queries, head_keys, preferred_element_type=jnp.float32
    )
    maxima = jnp.max(scores, axis=-1, keepdims=True)
    weights = jnp.exp(scores - maxima)
    totals = jnp.sum(weights, axis=-1, keepdims=True)
    summed = jnp.dot(weights.astype(jnp.bfloat16), head_values, preferred_element_type=jnp.float32)
    attended_head = (summed / totals).astype(jnp.bfloat16).reshape(head_count, lat_rows, head_width)
    got_attended = lax.all_to_all(
        jnp.tile(attended_head, (copies, 1, 1)), "blk", split_axis=0, concat_axis=0, tiled=True
    )
    attended = jnp.transpose(
        lax.dynamic_slice_in_dim(got_attended, group_start, head_count, axis=0), (1, 0, 2)
    ).reshape(lat_rows, model_width)
    mixed = latents.astype(jnp.float32) + jnp.dot(
        attended, w_out, preferred_element_type=jnp.float32
    )
    return mixed.astype(jnp.bfloat16)


def solution(mesh):
    in_specs = (
        P(("grp", "blk"), None),
        P(("grp", "blk")),
        P("blk", None),
        P(),
        P(),
        P(),
        P(),
        P(),
        P(),
    )
    out_specs = P(("grp", "blk"), None)
    return jax.shard_map(local, mesh=mesh, in_specs=in_specs, out_specs=out_specs, check_vma=False)
```

time: 123 us -> 103 us (0.84)
  blocking collectives: 76.3 us -> 44.1 us
  waiting for transfers between devices: 0.01 us -> 14.4 us
  starting transfers between devices: 7.44 us -> 19.1 us
  local copies, waits for them, and re-layouts: 23.5 us -> 14.7 us
  matrix products: 10.1 us -> 6.79 us
  other arithmetic: 4.65 us -> 3.09 us
    all_gather x1 -> x0, blocking collectives: 22.9 us -> none  [local(): all_queries = lax.all_gather(queries, 'blk', tiled=True)]
    all_to_all x0 -> x2, waiting for transfers between devices: none -> 14.4 us  [the longest x1 14.4 us: local(): lax.all_to_all(jnp.tile(pair_parts, (copies, 1, 1)), 'blk', split_axis=0,...]
    all_to_all x0 -> x2, starting transfers between devices: none -> 11.7 us  [the longest x1 6.01 us: local(): lax.all_to_all(jnp.tile(pair_parts, (copies, 1, 1)), 'blk', split_axis=0,...]
    all_to_all x1, blocking collectives: 19.8 us -> 10.5 us  [local(): lax.all_to_all(jnp.tile(attended_head, (copies, 1, 1)), 'blk', split_axis...]
    mul x3 -> x0, local copies, waits for them, and re-layouts: 4.08 us -> none  [local(): accum = jnp.sum(part_sums * factor[..., None], axis=0)]
    dot_general x2, matrix products: 4.48 us -> 1.23 us  [the longest x1 0.71 us: local(): jnp.dot(weights.astype(jnp.bfloat16), head_values, preferred_element_type...]
    reshape x4 -> x3, local copies, waits for them, and re-layouts: 2.26 us -> 0.25 us  [the longest x2 0.13 us: local(): queries.reshape(lat_rows, head_count, head_width)]
    convert_element_type x1, local copies, waits for them, and re-layouts: 2 us -> 0.11 us  [local(): (summed / totals).astype(jnp.bfloat16)]
  transfers between devices with their start and end apart: 1 -> 3, of which waited for: 0 -> 1; matrix products, arithmetic and copies ran while one was open for 5% -> 14% of each run, Pallas kernels for 0% -> 0%
where the time goes in v2:
time: 103 us; the launch traced here: 102 us
  blocking collectives  44.1 us (43%)
  starting transfers between devices  19.1 us (19%)
  local copies, waits for them, and re-layouts  14.7 us (14%)
  waiting for transfers between devices  14.4 us (14%)
  matrix products  6.79 us (7%)
  other arithmetic  3.09 us (3%)
    all_gather x1, blocking collectives, joined_rows(): all_ids = lax.all_gather(patch_of_row, 'blk', tiled=True)  33.6 us
    all_to_all x1, waiting for transfers between devices, local(): lax.all_to_all(jnp.tile(pair_parts, (copies, 1, 1)), 'blk', split_axis=0,...  14.4 us
    all_to_all x1, blocking collectives, local(): lax.all_to_all(jnp.tile(attended_head, (copies, 1, 1)), 'blk', split_axis...  10.5 us
    all_to_all x1, starting transfers between devices, joined_rows(): lax.all_to_all(tokens.reshape(per_peer, cycle_size, model_width), 'blk',...  7.39 us
    all_to_all x1, starting transfers between devices, local(): lax.all_to_all(jnp.tile(pair_parts, (copies, 1, 1)), 'blk', split_axis=0,...  6.01 us
    all_to_all x1, starting transfers between devices, local(): lax.all_to_all(jnp.tile(query_parts, (copies, 1, 1)), 'blk', split_axis=0...  5.68 us
    unnamed x18, local copies, waits for them, and re-layouts  3.01 us
    reshape x1, local copies, waits for them, and re-layouts, joined_rows(): tokens.reshape(per_peer, cycle_size, model_width)  2.94 us
  transfers between devices with their start and end apart: 3, of which 1 were waited for; matrix products, arithmetic and copies ran while one was open for 14% of the time, Pallas kernels for 0%

profile of v2, /device:TPU:0, one launch (start us, length us, event | category | flops | bytes accessed | tf_op | source)
XLA Modules:
  0.0 102.4 jit_solution(17456713454679602745)
XLA Ops:
  0.0 0.0 copy-start
  0.0 0.0 copy-start.3
  0.0 2.9 %copy.41 = bf16[32,16,1024]{2,0,1:T(8,128)(2,1)} copy(bf16[32,16,1024]{2,1,0:T(8,128)(2,1)} %bitcast.31) | data formatting | bytes 2097152 | tf_op jit(solution)/shard_map/reshape | solution.py:16
  3.0 7.4 %all-to-all-start.1 = ((bf16[32,16,1024]{2,0,1:T(8,128)(2,1)}), bf16[32,16,1024]{2,0,1:T(8,128)(2,1)S(1)}, u32[]{:S(2)}, u32[]{:S(2)}) async-start(bf16[32,16,1024]{2,0,1:T(8,128)(2,1)} %copy.41), calls=%async_computation.1 | async-start | bytes 2097152 | tf_op jit(solution)/shard_map/all_to_all | solution.py:15
  10.4 0.0 copy-done.5
  10.4 0.0 copy-done.4
  10.4 0.0 copy-done.6
  10.4 33.6 %all-gather = s32[16,1,512]{2,1,0:T(1,128)S(1)} all-gather(s32[1,1,512]{2,1,0:T(1,128)S(1)} %bitcast.38), channel_id=1, replica_groups=mesh['grp'=2,'blk'=16] {'blk'}, dimensions={0}, use_global_device_ids=true | all-gather | bytes 34816 | tf_op jit(solution)/shard_map/all_gather | solution.py:14
  44.0 0.1 reduce
  44.1 0.0 copy-done.3
  44.1 2.0 %fusion.3 = bf16[16,1024]{1,0:T(8,128)(2,1)S(1)} fusion(bf16[16,1024]{1,0:T(8,128)(2,1)S(1)} %copy-done.3, bf16[1024,1024]{1,0:T(8,128)(2,1)} %param.14), kind=kOutput, calls=%fused_computation.12 | convolution fusion | flops 33587200 | bytes 2162688 | tf_op jit(solution)/shard_map/dot_general | solution.py:56
  46.1 0.1 reshape.73
  46.2 0.7 reshape.108
  47.0 0.1 reshape.77
  47.1 0.5 dynamic-slice_reduce_fusion
  47.6 0.1 fusion.14
  47.7 0.1 copy.43
  47.7 0.1 reshape.78
  47.8 2.4 %scatter_custom_fusion = s32[512]{0:T(512)S(1)} fusion(s32[512]{0:T(512)S(1)} %bitcast.39, s32[512]{0:T(512)S(1)} %iota.19, s32[]{:T(128)} %constant.21.clone.1), kind=kCustom, calls=%fused_computation.42 | custom fusion | bytes 2052 | tf_op jit(solution)/shard_map/scatter | solution.py:35
  50.3 0.0 all-to-all-done.1
  50.3 0.0 copy-start.1
  50.3 1.0 copy-done.1
  51.3 5.7 %all-to-all-start = ((bf16[16,2,512]{2,1,0:T(2,128)(2,1)}), bf16[16,2,512]{2,1,0:T(2,128)(2,1)S(1)}, u32[]{:S(2)}, u32[]{:S(2)}) async-start(bf16[16,2,512]{2,1,0:T(2,128)(2,1)} %reshape.108), calls=%async_computation | async-start | bytes 65536 | tf_op jit(solution)/shard_map/all_to_all | solution.py:59
  57.0 1.8 %copy.42 = bf16[32,16,1024]{2,1,0:T(8,128)(2,1)S(1)} copy(bf16[32,16,1024]{2,0,1:T(8,128)(2,1)} %copy-done.1) | data formatting | bytes 2097152 | tf_op jit(solution)/shard_map/all_to_all | solution.py:15
  58.8 2.8 %gather_fusion = bf16[512,1024]{1,0:T(8,128)(2,1)} fusion(bf16[512,1024]{1,0:T(8,128)(2,1)S(1)} %bitcast.27, s32[1024]{0:T(1024)S(1)} %pad_clamp_fusion), kind=kCustom, calls=%fused_computation | custom fusion | bytes 2099200 | tf_op jit(solution)/shard_map/gather | solution.py:37
  61.6 1.5 %fusion = f32[128,1024]{1,0:T(8,128)S(1)} fusion(bf16[4,128,1024]{2,1,0:T(8,128)(2,1)} %bitcast.30, f32[4,1024]{1,0:T(4,128)S(1)} %convert_element_type.40), kind=kLoop, calls=%fused_computation.3 | loop fusion | flops 1441792 | bytes 1589248 | tf_op jit(solution)/shard_map/reduce_sum | solution.py:40
  63.1 0.0 copy-start.2
  63.1 0.1 multiply_reduce_fusion
  63.2 0.5 convolution_convert_fusion
  63.7 0.9 copy-done.2
  64.7 0.5 convolution_convert_fusion.1
  65.2 0.2 copy.44
  65.4 0.2 copy.45
  65.5 0.8 maximum_bitcast_fusion
  66.4 0.0 all-to-all-done
  66.4 6.0 %all-to-all-start.2 = ((bf16[16,128,128]{1,2,0:T(8,128)(2,1)}), bf16[16,128,128]{1,2,0:T(8,128)(2,1)S(1)}, u32[]{:S(2)}, u32[]{:S(2)}) async-start(bf16[16,128,128]{1,2,0:T(8,128)(2,1)} %maximum_bitcast_fusion), calls=%async_computation.2 | async-start | bytes 1048576 | tf_op jit(solution)/shard_map/all_to_all | solution.py:82
  72.4 0.1 reshape.109
  72.5 14.4 %all-to-all-done.2 = bf16[16,128,128]{1,2,0:T(8,128)(2,1)S(1)} async-done(((bf16[16,128,128]{1,2,0:T(8,128)(2,1)}), bf16[16,128,128]{1,2,0:T(8,128)(2,1)S(1)}, u32[]{:S(2)}, u32[]{:S(2)}) %all-to-all-start.2) | async-done | bytes 524320 | tf_op jit(solution)/shard_map/all_to_all | solution.py:82
  86.9 0.3 copy.46
  87.1 0.5 fusion.21
  87.7 0.4 fusion.1
  88.1 0.7 fusion.4
  88.8 0.1 copy.47
  88.9 0.1 reshape.110
  89.0 10.5 %all_to_all.20 = bf16[16,2,512]{2,1,0:T(2,128)(2,1)S(1)} all-to-all(bf16[16,2,512]{2,1,0:T(2,128)(2,1)S(1)} %reshape.110), channel_id=1, replica_groups=mesh['grp'=2,'blk'=16] {'blk'}, dimensions={0} | all-to-all | bytes 65536 | tf_op jit(solution)/shard_map/all_to_all | solution.py:96
  99.6 0.1 reshape.111
  99.7 0.1 reshape.82
  99.8 2.6 %fusion.5 = bf16[16,1024]{1,0:T(8,128)(2,1)} fusion(bf16[16,1024]{1,0:T(8,128)(2,1)S(1)} %reshape.82, bf16[1024,1024]{1,0:T(8,128)(2,1)} %param.17, bf16[16,1024]{1,0:T(8,128)(2,1)S(1)} %copy-done.3), kind=kOutput, calls=%fused_computation.14 | convolution fusion | flops 33603584 | bytes 2195456 | tf_op jit(solution)/shard_map/dot_general | solution.py:102
  (15 shorter events, 0.1 us)
Async XLA Ops:
  0.0 63.2 %copy-start = (bf16[1024,1024]{1,0:T(8,128)(2,1)S(1)}, bf16[1024,1024]{1,0:T(8,128)(2,1)}, u32[]{:S(2)}) copy-start(bf16[1024,1024]{1,0:T(8,128)(2,1)} %param.16) | copy-start | bytes 6291460
  0.0 10.4 %copy-start.5 = (bf16[1024]{0:T(1024)(128)(2,1)S(1)}, bf16[1024]{0:T(1024)(128)(2,1)}, u32[]{:S(2)}) copy-start(bf16[1024]{0:T(1024)(128)(2,1)} %param.13) | copy-start | bytes 6148
  0.0 10.4 %copy-start.4 = (bf16[4,1024]{1,0:T(4,128)(2,1)S(1)}, bf16[4,1024]{1,0:T(4,128)(2,1)}, u32[]{:S(2)}) copy-start(bf16[4,1024]{1,0:T(4,128)(2,1)} %param.12) | copy-start | bytes 24580
  0.0 10.4 %copy-start.6 = (s32[512]{0:T(512)S(1)}, s32[512]{0:T(512)}, u32[]{:S(2)}) copy-start(s32[512]{0:T(512)} %param.10) | copy-start | bytes 6148
  0.0 44.1 %copy-start.3 = (bf16[16,1024]{1,0:T(8,128)(2,1)S(1)}, bf16[16,1024]{1,0:T(8,128)(2,1)}, u32[]{:S(2)}) copy-start(bf16[16,1024]{1,0:T(8,128)(2,1)} %param.11) | copy-start | bytes 98308
  3.0 47.3 %all-to-all-start.1 = ((bf16[32,16,1024]{2,0,1:T(8,128)(2,1)}), bf16[32,16,1024]{2,0,1:T(8,128)(2,1)S(1)}, u32[]{:S(2)}, u32[]{:S(2)}) async-start(bf16[32,16,1024]{2,0,1:T(8,128)(2,1)} %copy.41), calls=%async_computation.1 | async-start | bytes 2097152 | tf_op jit(solution)/shard_map/all_to_all | solution.py:15
  50.3 1.0 copy-start.1
  51.3 15.1 %all-to-all-start = ((bf16[16,2,512]{2,1,0:T(2,128)(2,1)}), bf16[16,2,512]{2,1,0:T(2,128)(2,1)S(1)}, u32[]{:S(2)}, u32[]{:S(2)}) async-start(bf16[16,2,512]{2,1,0:T(2,128)(2,1)} %reshape.108), calls=%async_computation | async-start | bytes 65536 | tf_op jit(solution)/shard_map/all_to_all | solution.py:59
  63.1 1.6 %copy-start.2 = (bf16[1024,1024]{1,0:T(8,128)(2,1)S(1)}, bf16[1024,1024]{1,0:T(8,128)(2,1)}, u32[]{:S(2)}) copy-start(bf16[1024,1024]{1,0:T(8,128)(2,1)} %param.15) | copy-start | bytes 6291460
  66.4 20.5 %all-to-all-start.2 = ((bf16[16,128,128]{1,2,0:T(8,128)(2,1)}), bf16[16,128,128]{1,2,0:T(8,128)(2,1)S(1)}, u32[]{:S(2)}, u32[]{:S(2)}) async-start(bf16[16,128,128]{1,2,0:T(8,128)(2,1)} %maximum_bitcast_fusion), calls=%async_computation.2 | async-start | bytes 1048576 | tf_op jit(solution)/shard_map/all_to_all | solution.py:82

commit v3 on v2

v3 whole, which is shorter than its diff:
```python
import jax
import jax.numpy as jnp
from jax import lax
from jax.sharding import PartitionSpec as P

HEADS = 16
CONTRASTS = 4


def local(tokens, patch_of_row, latents, contrast_gain, norm_gain, w_query, w_key, w_value, w_out):
    cycle_size = lax.axis_size("blk")
    my_index = lax.axis_index("blk")
    tok_rows, model_width = tokens.shape
    head_count = HEADS
    head_width = model_width // head_count
    lat_rows = latents.shape[0]
    copies = cycle_size // head_count
    group_start = (my_index // head_count) * head_count
    per_peer = tok_rows // cycle_size
    patches_dev = tok_rows // CONTRASTS
    lanes = 128

    queries = (
        jnp.dot(latents, w_query, preferred_element_type=jnp.float32) * head_width ** (-0.5)
    ).astype(jnp.bfloat16)
    query_parts = jnp.tile(
        jnp.transpose(queries.reshape(lat_rows, head_count, head_width), (1, 0, 2)),
        (copies, 1, 1),
    ).reshape(cycle_size, -1, lanes)
    token_parts = jnp.transpose(
        tokens.reshape(per_peer, cycle_size, model_width), (1, 0, 2)
    ).reshape(cycle_size, -1, lanes)
    row_dest = lax.broadcasted_iota(jnp.int32, (tok_rows,), 0) % cycle_size
    local_ids = (patch_of_row - row_dest * patches_dev).astype(jnp.bfloat16)
    id_parts = jnp.transpose(local_ids.reshape(per_peer, cycle_size))
    id_width = -(-per_peer // lanes) * lanes
    id_parts = jnp.pad(id_parts, ((0, 0), (0, id_width - per_peer))).reshape(cycle_size, -1, lanes)
    token_len = token_parts.shape[1]
    query_len = query_parts.shape[1]
    payload = jnp.concatenate([token_parts, query_parts, id_parts], axis=1)
    got = lax.all_to_all(payload, "blk", split_axis=0, concat_axis=0, tiled=True)

    head_queries = lax.dynamic_slice_in_dim(
        got[:, token_len : token_len + query_len], group_start, head_count, axis=0
    ).reshape(head_count * lat_rows, head_width)
    recv_rows = got[:, :token_len].reshape(CONTRASTS, patches_dev, model_width)
    recv_ids = (
        got[:, token_len + query_len :].reshape(cycle_size, id_width)[:, :per_peer]
        .astype(jnp.int32)
        .reshape(CONTRASTS, 1, patches_dev)
    )
    patch_iota = lax.broadcasted_iota(jnp.int32, (CONTRASTS, patches_dev, patches_dev), 1)
    selector = (recv_ids == patch_iota).astype(jnp.bfloat16)
    arranged = jnp.einsum(
        "cpk,ckd->cpd", selector, recv_rows, preferred_element_type=jnp.float32
    )
    joined = jnp.sum(arranged * contrast_gain.astype(jnp.float32)[:, None, :], axis=0)

    inverse_rms = lax.rsqrt(jnp.mean(joined * joined, axis=-1, keepdims=True) + 1e-05)
    normed = (joined * inverse_rms * norm_gain.astype(jnp.float32)).astype(jnp.bfloat16)
    key_rows = jnp.dot(normed, w_key, preferred_element_type=jnp.float32).astype(jnp.bfloat16)
    value_rows = jnp.dot(normed, w_value, preferred_element_type=jnp.float32).astype(jnp.bfloat16)
    pair_parts = jnp.transpose(
        jnp.concatenate(
            [
                key_rows.reshape(patches_dev, head_count, head_width),
                value_rows.reshape(patches_dev, head_count, head_width),
            ],
            axis=-1,
        ),
        (1, 0, 2),
    )
    got_pairs = lax.all_to_all(
        jnp.tile(pair_parts, (copies, 1, 1)), "blk", split_axis=0, concat_axis=0, tiled=True
    ).reshape(cycle_size * patches_dev, 2 * head_width)
    head_keys = got_pairs[:, :head_width]
    head_values = got_pairs[:, head_width:]

    scores = jnp.einsum(
        "ld,kd->lk", head_queries, head_keys, preferred_element_type=jnp.float32
    )
    maxima = jnp.max(scores, axis=-1, keepdims=True)
    weights = jnp.exp(scores - maxima)
    totals = jnp.sum(weights, axis=-1, keepdims=True)
    summed = jnp.dot(weights.astype(jnp.bfloat16), head_values, preferred_element_type=jnp.float32)
    attended_head = (summed / totals).astype(jnp.bfloat16).reshape(head_count, lat_rows, head_width)
    got_attended = lax.all_to_all(
        jnp.tile(attended_head, (copies, 1, 1)), "blk", split_axis=0, concat_axis=0, tiled=True
    )
    attended = jnp.transpose(
        lax.dynamic_slice_in_dim(got_attended, group_start, head_count, axis=0), (1, 0, 2)
    ).reshape(lat_rows, model_width)
    mixed = latents.astype(jnp.float32) + jnp.dot(
        attended, w_out, preferred_element_type=jnp.float32
    )
    return mixed.astype(jnp.bfloat16)


def solution(mesh):
    in_specs = (
        P(("grp", "blk"), None),
        P(("grp", "blk")),
        P("blk", None),
        P(),
        P(),
        P(),
        P(),
        P(),
        P(),
    )
    out_specs = P(("grp", "blk"), None)
    return jax.shard_map(local, mesh=mesh, in_specs=in_specs, out_specs=out_specs, check_vma=False)
```

time: 103 us -> 90.4 us (0.88)
  blocking collectives: 44.1 us -> 10.5 us
  waiting for transfers between devices: 14.4 us -> 38.4 us
  starting transfers between devices: 19.1 us -> 14.6 us
  matrix products: 6.79 us -> 9.22 us
  local copies, waits for them, and re-layouts: 14.7 us -> 12.5 us
  other arithmetic: 3.09 us -> 4.36 us
    all_gather x1 -> x0, blocking collectives: 33.6 us -> none  [joined_rows(): all_ids = lax.all_gather(patch_of_row, 'blk', tiled=True)]
    all_to_all x2 -> x1, waiting for transfers between devices: 0.01 us -> 24 us  [local(): lax.all_to_all(payload, 'blk', split_axis=0, concat_axis=0, tiled=True)]
    all_to_all x2 -> x1, starting transfers between devices: 13.1 us -> 7.39 us  [local(): lax.all_to_all(payload, 'blk', split_axis=0, concat_axis=0, tiled=True)]
    gather x1 -> x0, local copies, waits for them, and re-layouts: 2.79 us -> none  [joined_rows(): received.reshape(tok_rows, model_width)[inverse]]
    reshape x3 -> x7, local copies, waits for them, and re-layouts: 3.14 us -> 5.65 us  [the longest x1 2.31 us: local(): recv_rows = got[:, :token_len].reshape(CONTRASTS, patches_dev, model_width)]
    scatter x1 -> x0, local copies, waits for them, and re-layouts: 2.44 us -> none  [joined_rows(): jnp.zeros((tok_rows,), jnp.int32).at[target_row]]
    unnamed x18 -> x15, local copies, waits for them, and re-layouts: 3.01 us -> 1.2 us
    all_to_all x1 -> x0, local copies, waits for them, and re-layouts: 1.81 us -> none  [joined_rows(): lax.all_to_all(tokens.reshape(per_peer, cycle_size, model_width), 'blk',...]
  transfers between devices with their start and end apart: 3 -> 2, of which waited for: 1 -> 2; matrix products, arithmetic and copies ran while one was open for 14% -> 0% of each run, Pallas kernels for 0% -> 0%
where the time goes in v3:
time: 90.4 us; the launch traced here: 89.8 us
  waiting for transfers between devices  38.4 us (42%)
  starting transfers between devices  14.6 us (16%)
  local copies, waits for them, and re-layouts  12.5 us (14%)
  blocking collectives  10.5 us (12%)
  matrix products  9.22 us (10%)
  other arithmetic  4.36 us (5%)
    all_to_all x1, waiting for transfers between devices, local(): lax.all_to_all(payload, 'blk', split_axis=0, concat_axis=0, tiled=True)  24 us
    all_to_all x1, waiting for transfers between devices, local(): lax.all_to_all(jnp.tile(pair_parts, (copies, 1, 1)), 'blk', split_axis=0,...  14.4 us
    all_to_all x1, blocking collectives, local(): lax.all_to_all(jnp.tile(attended_head, (copies, 1, 1)), 'blk', split_axis...  10.5 us
    all_to_all x1, starting transfers between devices, local(): lax.all_to_all(payload, 'blk', split_axis=0, concat_axis=0, tiled=True)  7.39 us
    all_to_all x1, starting transfers between devices, local(): lax.all_to_all(jnp.tile(pair_parts, (copies, 1, 1)), 'blk', split_axis=0,...  7.24 us
    dot_general x1, matrix products, local(): jnp.dot(attended, w_out, preferred_element_type=jnp.float32)  2.6 us
    reshape x1, local copies, waits for them, and re-layouts, local(): recv_rows = got[:, :token_len].reshape(CONTRASTS, patches_dev, model_width)  2.31 us
    dot_general x1, matrix products, local(): jnp.dot(latents, w_query, preferred_element_type=jnp.float32)  2.02 us
  transfers between devices with their start and end apart: 2, of which 2 were waited for; matrix products, arithmetic and copies ran while one was open for 0% of the time, Pallas kernels for 0%

profile of v3, /device:TPU:0, one launch (start us, length us, event | category | flops | bytes accessed | tf_op | source)
XLA Modules:
  0.0 89.8 jit_solution(12522199217976141368)
XLA Ops:
  0.0 0.0 copy-start
  0.0 0.0 copy-start.2
  0.0 0.8 fusion.13
  0.9 0.1 reshape.53
  0.9 0.1 copy.33
  1.0 2.0 %fusion.2 = bf16[16,1024]{1,0:T(8,128)(2,1)S(1)} fusion(bf16[16,1024]{1,0:T(8,128)(2,1)} %param.11, bf16[1024,1024]{1,0:T(8,128)(2,1)} %param.14), kind=kOutput, calls=%fused_computation.9 | convolution fusion | flops 33587200 | bytes 2162688 | tf_op jit(solution)/shard_map/dot_general | solution.py:24
  3.0 0.1 reshape.52
  3.2 0.1 reshape_tile.3
  3.3 0.0 copy-done.2
  3.3 1.6 %copy.45 = bf16[32,16,1024]{2,0,1:T(8,128)(2,1)} copy(bf16[32,16,1024]{2,1,0:T(8,128)(2,1)S(1)} %bitcast.31) | data formatting | bytes 2097152 | tf_op jit(solution)/shard_map/reshape | solution.py:31
  4.9 1.5 %reshape.51 = bf16[16,256,128]{2,1,0:T(8,128)(2,1)S(1)} reshape(bf16[16,32,1024]{2,1,0:T(8,128)(2,1)} %bitcast.30) | data formatting | bytes 2097152 | tf_op jit(solution)/shard_map/reshape | solution.py:32
  6.4 0.0 copy-start.5
  6.4 0.0 copy-start.4
  6.4 1.1 %pad_maximum_fusion = bf16[16,265,128]{2,1,0:T(8,128)(2,1)} fusion(bf16[16,1,128]{2,1,0:T(2,128)(2,1)S(1)} %copy.33, bf16[16,8,128]{2,1,0:T(8,128)(2,1)S(1)} %reshape_tile.3, bf16[16,256,128]{2,1,0:T(8,128)(2,1)S(1)} %reshape.51), kind=kLoop, calls=%fused_computation.12 | loop fusion | flops 3256320 | bytes 2170880 | tf_op jit(solution)/shard_map/concatenate | solution.py:40
  7.5 7.4 %all-to-all-start = ((bf16[16,265,128]{2,1,0:T(8,128)(2,1)}), bf16[16,265,128]{2,1,0:T(8,128)(2,1)S(1)}, u32[]{:S(2)}, u32[]{:S(2)}) async-start(bf16[16,265,128]{2,1,0:T(8,128)(2,1)} %pad_maximum_fusion), calls=%async_computation | async-start | bytes 2228224 | tf_op jit(solution)/shard_map/all_to_all | solution.py:41
  14.9 0.0 copy-done.5
  14.9 0.0 copy-done.4
  14.9 24.0 %all-to-all-done = bf16[16,265,128]{2,1,0:T(8,128)(2,1)S(1)} async-done(((bf16[16,265,128]{2,1,0:T(8,128)(2,1)}), bf16[16,265,128]{2,1,0:T(8,128)(2,1)S(1)}, u32[]{:S(2)}, u32[]{:S(2)}) %all-to-all-start) | async-done | bytes 1085472 | tf_op jit(solution)/shard_map/all_to_all | solution.py:41
  38.9 0.1 reshape.62
  39.0 1.1 %slice.27 = bf16[16,256,128]{2,1,0:T(8,128)(2,1)} slice(bf16[16,265,128]{2,1,0:T(8,128)(2,1)S(1)} %all-to-all-done), slice={[0:16], [0:256], [0:128]} | slice | bytes 2097152 | tf_op jit(solution)/shard_map/slice | solution.py:46
  40.1 2.3 %reshape.57 = bf16[4,128,1024]{2,1,0:T(8,128)(2,1)} reshape(bf16[16,256,128]{2,1,0:T(8,128)(2,1)} %slice.27) | data formatting | bytes 2097152 | tf_op jit(solution)/shard_map/reshape | solution.py:46
  42.4 1.7 %multiply_reduce_fusion = f32[128,1024]{1,0:T(8,128)S(1)} fusion(bf16[4,128,1024]{2,1,0:T(8,128)(2,1)} %reshape.57, f32[4,1024]{1,0:T(4,128)S(1)} %convert_element_type.40, s32[4,128]{1,0:T(4,128)S(1)} %reshape.62), kind=kOutput, calls=%fused_computation.1 | convolution fusion | flops 135200768 | bytes 1591296 | tf_op jit(solution)/shard_map/cpk,ckd->cpd/dot_general | solution.py:54
  44.1 0.0 copy-start.1
  44.1 0.1 multiply_reduce_fusion.1
  44.3 0.0 copy-done
  44.3 0.5 convolution_convert_fusion
  44.8 0.9 %copy-done.1 = bf16[1024,1024]{1,0:T(8,128)(2,1)S(1)} copy-done((bf16[1024,1024]{1,0:T(8,128)(2,1)S(1)}, bf16[1024,1024]{1,0:T(8,128)(2,1)}, u32[]{:S(2)}) %copy-start.1) | copy-done | bytes 2097176
  45.7 1.2 %convolution_convert_fusion.1 = bf16[128,1024]{1,0:T(8,128)(2,1)} fusion(bf16[1024,1024]{1,0:T(8,128)(2,1)S(1)} %copy-done.1, f32[128,1024]{1,0:T(8,128)S(1)} %multiply_reduce_fusion, f32[1024]{0:T(1024)S(1)} %convert_element_type.41, f32[128]{0:T(128)S(1)} %add_rsqrt_fusion), kind=kOutput, calls=%fused_computation.5 | convolution fusion | flops 268959744 | bytes 2888192 | tf_op jit(solution)/shard_map/dot_general | solution.py:61
  46.9 1.8 %copy.34 = bf16[128,1024]{0,1:T(8,128)(2,1)} copy(bf16[128,1024]{1,0:T(8,128)(2,1)} %convolution_convert_fusion.1) | data formatting | bytes 524288 | tf_op jit(solution)/shard_map/convert_element_type | solution.py:61
  48.7 0.8 copy.35
  49.5 1.9 %maximum_bitcast_fusion = bf16[16,128,128]{1,2,0:T(8,128)(2,1)} fusion(bf16[128,16,64]{0,2,1:T(8,128)(2,1)} %bitcast.33, bf16[128,16,64]{0,2,1:T(8,128)(2,1)} %bitcast.32), kind=kLoop, calls=%fused_computation.18 | loop fusion | flops 1048576 | bytes 1048576 | tf_op jit(solution)/shard_map/transpose | solution.py:63
  51.4 7.2 %all-to-all-start.1 = ((bf16[16,128,128]{1,2,0:T(8,128)(2,1)}), bf16[16,128,128]{1,2,0:T(8,128)(2,1)}, u32[]{:S(2)}, u32[]{:S(2)}) async-start(bf16[16,128,128]{1,2,0:T(8,128)(2,1)} %maximum_bitcast_fusion), calls=%async_computation.1 | async-start | bytes 1048576 | tf_op jit(solution)/shard_map/all_to_all | solution.py:73
  58.7 0.1 reshape.55
  58.8 14.4 %all-to-all-done.1 = bf16[16,128,128]{1,2,0:T(8,128)(2,1)} async-done(((bf16[16,128,128]{1,2,0:T(8,128)(2,1)}), bf16[16,128,128]{1,2,0:T(8,128)(2,1)}, u32[]{:S(2)}, u32[]{:S(2)}) %all-to-all-start.1) | async-done | bytes 524320 | tf_op jit(solution)/shard_map/all_to_all | solution.py:73
  73.2 1.3 %copy.36 = bf16[16,128,128]{2,1,0:T(8,128)(2,1)S(1)} copy(bf16[16,128,128]{1,2,0:T(8,128)(2,1)} %all-to-all-done.1) | data formatting | bytes 1048576 | tf_op jit(solution)/shard_map/all_to_all | solution.py:73
  74.5 0.5 fusion.17
  75.0 0.4 fusion
  75.4 0.0 copy-start.3
  75.5 0.7 fusion.3
  76.2 0.1 copy.37
  76.3 0.1 reshape.63
  76.4 10.5 %all_to_all.15 = bf16[16,2,512]{2,1,0:T(2,128)(2,1)S(1)} all-to-all(bf16[16,2,512]{2,1,0:T(2,128)(2,1)S(1)} %reshape.63), channel_id=1, replica_groups=mesh['grp'=2,'blk'=16] {'blk'}, dimensions={0} | all-to-all | bytes 65536 | tf_op jit(solution)/shard_map/all_to_all | solution.py:87
  86.9 0.1 reshape.64
  87.1 0.1 reshape.61
  87.2 0.0 copy-done.3
  87.2 2.6 %fusion.4 = bf16[16,1024]{1,0:T(8,128)(2,1)} fusion(bf16[16,1024]{1,0:T(8,128)(2,1)S(1)} %reshape.61, bf16[1024,1024]{1,0:T(8,128)(2,1)} %param.17, bf16[16,1024]{1,0:T(8,128)(2,1)S(1)} %copy-done.3), kind=kOutput, calls=%fused_computation.11 | convolution fusion | flops 33603584 | bytes 2195456 | tf_op jit(solution)/shard_map/dot_general | solution.py:93
  (10 shorter events, 0.1 us)
Async XLA Ops:
  0.0 44.3 %copy-start = (bf16[1024,1024]{1,0:T(8,128)(2,1)S(1)}, bf16[1024,1024]{1,0:T(8,128)(2,1)}, u32[]{:S(2)}) copy-start(bf16[1024,1024]{1,0:T(8,128)(2,1)} %param.16) | copy-start | bytes 6291460
  0.0 3.3 %copy-start.2 = (bf16[512,1024]{1,0:T(8,128)(2,1)S(1)}, bf16[512,1024]{1,0:T(8,128)(2,1)}, u32[]{:S(2)}) copy-start(bf16[512,1024]{1,0:T(8,128)(2,1)} %param.9) | copy-start | bytes 3145732
  6.4 8.5 %copy-start.5 = (bf16[1024]{0:T(1024)(128)(2,1)S(1)}, bf16[1024]{0:T(1024)(128)(2,1)}, u32[]{:S(2)}) copy-start(bf16[1024]{0:T(1024)(128)(2,1)} %param.13) | copy-start | bytes 6148
  6.4 8.5 %copy-start.4 = (bf16[4,1024]{1,0:T(4,128)(2,1)S(1)}, bf16[4,1024]{1,0:T(4,128)(2,1)}, u32[]{:S(2)}) copy-start(bf16[4,1024]{1,0:T(4,128)(2,1)} %param.12) | copy-start | bytes 24580
  7.5 31.4 %all-to-all-start = ((bf16[16,265,128]{2,1,0:T(8,128)(2,1)}), bf16[16,265,128]{2,1,0:T(8,128)(2,1)S(1)}, u32[]{:S(2)}, u32[]{:S(2)}) async-start(bf16[16,265,128]{2,1,0:T(8,128)(2,1)} %pad_maximum_fusion), calls=%async_computation | async-start | bytes 2228224 | tf_op jit(solution)/shard_map/all_to_all | solution.py:41
  44.1 1.6 %copy-start.1 = (bf16[1024,1024]{1,0:T(8,128)(2,1)S(1)}, bf16[1024,1024]{1,0:T(8,128)(2,1)}, u32[]{:S(2)}) copy-start(bf16[1024,1024]{1,0:T(8,128)(2,1)} %param.15) | copy-start | bytes 6291460
  51.4 21.8 %all-to-all-start.1 = ((bf16[16,128,128]{1,2,0:T(8,128)(2,1)}), bf16[16,128,128]{1,2,0:T(8,128)(2,1)}, u32[]{:S(2)}, u32[]{:S(2)}) async-start(bf16[16,128,128]{1,2,0:T(8,128)(2,1)} %maximum_bitcast_fusion), calls=%async_computation.1 | async-start | bytes 1048576 | tf_op jit(solution)/shard_map/all_to_all | solution.py:73
  75.4 11.7 %copy-start.3 = (bf16[16,1024]{1,0:T(8,128)(2,1)S(1)}, bf16[16,1024]{1,0:T(8,128)(2,1)}, u32[]{:S(2)}) copy-start(bf16[16,1024]{1,0:T(8,128)(2,1)} %param.11) | copy-start | bytes 98308

commit v4 on v3

--- a/solution.py
+++ b/solution.py
@@ -23,10 +23,6 @@
     queries = (
         jnp.dot(latents, w_query, preferred_element_type=jnp.float32) * head_width ** (-0.5)
     ).astype(jnp.bfloat16)
-    query_parts = jnp.tile(
-        jnp.transpose(queries.reshape(lat_rows, head_count, head_width), (1, 0, 2)),
-        (copies, 1, 1),
-    ).reshape(cycle_size, -1, lanes)
     token_parts = jnp.transpose(
         tokens.reshape(per_peer, cycle_size, model_width), (1, 0, 2)
     ).reshape(cycle_size, -1, lanes)
@@ -36,16 +32,12 @@
     id_width = -(-per_peer // lanes) * lanes
     id_parts = jnp.pad(id_parts, ((0, 0), (0, id_width - per_peer))).reshape(cycle_size, -1, lanes)
     token_len = token_parts.shape[1]
-    query_len = query_parts.shape[1]
-    payload = jnp.concatenate([token_parts, query_parts, id_parts], axis=1)
+    payload = jnp.concatenate([token_parts, id_parts], axis=1)
     got = lax.all_to_all(payload, "blk", split_axis=0, concat_axis=0, tiled=True)
 
-    head_queries = lax.dynamic_slice_in_dim(
-        got[:, token_len : token_len + query_len], group_start, head_count, axis=0
-    ).reshape(head_count * lat_rows, head_width)
     recv_rows = got[:, :token_len].reshape(CONTRASTS, patches_dev, model_width)
     recv_ids = (
-        got[:, token_len + query_len :].reshape(cycle_size, id_width)[:, :per_peer]
+        got[:, token_len:].reshape(cycle_size, id_width)[:, :per_peer]
         .astype(jnp.int32)
         .reshape(CONTRASTS, 1, patches_dev)
     )
@@ -58,21 +50,25 @@
 
     inverse_rms = lax.rsqrt(jnp.mean(joined * joined, axis=-1, keepdims=True) + 1e-05)
     normed = (joined * inverse_rms * norm_gain.astype(jnp.float32)).astype(jnp.bfloat16)
-    key_rows = jnp.dot(normed, w_key, preferred_element_type=jnp.float32).astype(jnp.bfloat16)
-    value_rows = jnp.dot(normed, w_value, preferred_element_type=jnp.float32).astype(jnp.bfloat16)
-    pair_parts = jnp.transpose(
-        jnp.concatenate(
-            [
-                key_rows.reshape(patches_dev, head_count, head_width),
-                value_rows.reshape(patches_dev, head_count, head_width),
-            ],
-            axis=-1,
-        ),
-        (1, 0, 2),
+    pair_weight = jnp.concatenate(
+        [
+            w_key.reshape(model_width, head_count, head_width),
+            w_value.reshape(model_width, head_count, head_width),
+        ],
+        axis=-1,
     )
-    got_pairs = lax.all_to_all(
-        jnp.tile(pair_parts, (copies, 1, 1)), "blk", split_axis=0, concat_axis=0, tiled=True
-    ).reshape(cycle_size * patches_dev, 2 * head_width)
+    pair_rows = jnp.einsum(
+        "pf,fhe->hpe", normed, pair_weight, preferred_element_type=jnp.float32
+    ).astype(jnp.bfloat16)
+    query_parts = jnp.transpose(queries.reshape(lat_rows, head_count, head_width), (1, 0, 2))
+    query_parts = query_parts.reshape(head_count, -1, 2 * head_width)
+    query_len = query_parts.shape[1]
+    pair_payload = jnp.tile(jnp.concatenate([pair_rows, query_parts], axis=1), (copies, 1, 1))
+    got_pairs = lax.all_to_all(pair_payload, "blk", split_axis=0, concat_axis=0, tiled=True)
+    head_queries = lax.dynamic_slice_in_dim(
+        got_pairs[:, patches_dev:], group_start, head_count, axis=0
+    ).reshape(head_count * lat_rows, head_width)
+    got_pairs = got_pairs[:, :patches_dev].reshape(cycle_size * patches_dev, 2 * head_width)
     head_keys = got_pairs[:, :head_width]
     head_values = got_pairs[:, head_width:]
 

time: 90.4 us -> 86.6 us (0.958)
  waiting for transfers between devices: 38.4 us -> 5.37 us
  blocking collectives: 10.5 us -> 32.9 us
  local copies, waits for them, and re-layouts: 12.5 us -> 26.5 us
  starting transfers between devices: 14.6 us -> 7.39 us
  matrix products: 9.22 us -> 11.9 us
  other arithmetic: 4.36 us -> 1.73 us
    all_to_all x0 -> x1, blocking collectives: none -> 23.6 us  [local(): lax.all_to_all(pair_payload, 'blk', split_axis=0, concat_axis=0, tiled=True)]
    all_to_all x1, waiting for transfers between devices: 24 us -> 5.37 us  [local(): lax.all_to_all(payload, 'blk', split_axis=0, concat_axis=0, tiled=True)]
    all_to_all x1 -> x0, waiting for transfers between devices: 14.4 us -> none  [local(): lax.all_to_all(jnp.tile(pair_parts, (copies, 1, 1)), 'blk', split_axis=0,...]
    reshape x1 -> x4, local copies, waits for them, and re-layouts: 0.09 us -> 9.74 us  [the longest x1 4.78 us: local(): w_key.reshape(model_width, head_count, head_width)]
    all_to_all x1 -> x0, starting transfers between devices: 7.24 us -> none  [local(): lax.all_to_all(jnp.tile(pair_parts, (copies, 1, 1)), 'blk', split_axis=0,...]
    unnamed x15, local copies, waits for them, and re-layouts: 1.2 us -> 8.13 us
    dot_general x2 -> x1, matrix products: 1.68 us -> 5.98 us  [local(): jnp.einsum('pf,fhe->hpe', normed, pair_weight, preferred_element_type=jnp...]
    convert_element_type x2 -> x0, local copies, waits for them, and re-layouts: 2.64 us -> none  [the longest x1 1.79 us: local(): jnp.dot(normed, w_key, preferred_element_type=jnp.float32)]
  transfers between devices with their start and end apart: 2 -> 1, of which waited for: 2 -> 1; matrix products, arithmetic and copies ran while one was open for 0% -> 21% of each run, Pallas kernels for 0% -> 0%
where the time goes in v4:
time: 86.6 us; the launch traced here: 85.9 us
  blocking collectives  32.9 us (38%)
  local copies, waits for them, and re-layouts  26.5 us (31%)
  matrix products  11.9 us (14%)
  starting transfers between devices  7.39 us (9%)
  waiting for transfers between devices  5.37 us (6%)
  other arithmetic  1.73 us (2%)
    all_to_all x1, blocking collectives, local(): lax.all_to_all(pair_payload, 'blk', split_axis=0, concat_axis=0, tiled=True)  23.6 us
    all_to_all x1, blocking collectives, local(): lax.all_to_all(jnp.tile(attended_head, (copies, 1, 1)), 'blk', split_axis...  9.36 us
    unnamed x15, local copies, waits for them, and re-layouts  8.13 us
    all_to_all x1, starting transfers between devices, local(): lax.all_to_all(payload, 'blk', split_axis=0, concat_axis=0, tiled=True)  7.39 us
    dot_general x1, matrix products, local(): jnp.einsum('pf,fhe->hpe', normed, pair_weight, preferred_element_type=jnp...  5.98 us
    all_to_all x1, waiting for transfers between devices, local(): lax.all_to_all(payload, 'blk', split_axis=0, concat_axis=0, tiled=True)  5.37 us
    reshape x1, local copies, waits for them, and re-layouts, local(): w_key.reshape(model_width, head_count, head_width)  4.78 us
    reshape x1, local copies, waits for them, and re-layouts, local(): w_value.reshape(model_width, head_count, head_width)  4.77 us
  transfers between devices with their start and end apart: 1, of which 1 were waited for; matrix products, arithmetic and copies ran while one was open for 21% of the time, Pallas kernels for 0%

profile of v4, /device:TPU:0, one launch (start us, length us, event | category | flops | bytes accessed | tf_op | source)
XLA Modules:
  0.0 85.9 jit_solution(16594757617664614045)
XLA Ops:
  0.0 0.0 copy-start
  0.0 0.0 copy-start.4
  0.0 3.0 %copy.37 = bf16[32,16,1024]{2,0,1:T(8,128)(2,1)} copy(bf16[32,16,1024]{2,1,0:T(8,128)(2,1)} %bitcast.34) | data formatting | bytes 2097152 | tf_op jit(solution)/shard_map/reshape | solution.py:27
  3.0 1.5 %reshape.56 = bf16[16,256,128]{2,1,0:T(8,128)(2,1)S(1)} reshape(bf16[16,32,1024]{2,1,0:T(8,128)(2,1)} %bitcast.33) | data formatting | bytes 2097152 | tf_op jit(solution)/shard_map/reshape | solution.py:28
  4.5 0.0 copy-done.4
  4.5 0.1 reshape.57
  4.6 0.1 copy.27
  4.7 0.0 copy-start.2
  4.7 1.1 %pad_maximum_fusion = bf16[16,257,128]{2,1,0:T(8,128)(2,1)} fusion(bf16[16,1,128]{2,1,0:T(2,128)(2,1)S(1)} %copy.27, bf16[16,256,128]{2,1,0:T(8,128)(2,1)S(1)} %reshape.56), kind=kLoop, calls=%fused_computation.16 | loop fusion | flops 2105344 | bytes 2105344 | tf_op jit(solution)/shard_map/concatenate | solution.py:35
  5.8 7.4 %all-to-all-start = ((bf16[16,257,128]{2,1,0:T(8,128)(2,1)}), bf16[16,257,128]{2,1,0:T(8,128)(2,1)S(1)}, u32[]{:S(2)}, u32[]{:S(2)}) async-start(bf16[16,257,128]{2,1,0:T(8,128)(2,1)} %pad_maximum_fusion), calls=%async_computation | async-start | bytes 2162688 | tf_op jit(solution)/shard_map/all_to_all | solution.py:36
  13.2 0.0 copy-done.2
  13.2 4.0 %copy.21 = bf16[1024,1024]{0,1:T(8,128)(2,1)} copy(bf16[1024,1024]{1,0:T(8,128)(2,1)} %param.15) | data formatting | bytes 4194304 | tf_op args[6]
  17.1 4.8 %copy.23 = bf16[1024,16,64]{2,0,1:T(8,128)(2,1)} copy(bf16[1024,16,64]{0,2,1:T(8,128)(2,1)} %bitcast.29) | data formatting | bytes 4194304 | tf_op jit(solution)/shard_map/reshape | solution.py:55
  21.9 3.9 %copy.22 = bf16[1024,1024]{0,1:T(8,128)(2,1)} copy(bf16[1024,1024]{1,0:T(8,128)(2,1)} %param.16) | data formatting | bytes 4194304 | tf_op args[7]
  25.9 0.0 copy-start.3
  25.9 0.0 copy-start.1
  25.9 4.8 %copy.24 = bf16[1024,16,64]{2,0,1:T(8,128)(2,1)} copy(bf16[1024,16,64]{0,2,1:T(8,128)(2,1)} %bitcast.30) | data formatting | bytes 4194304 | tf_op jit(solution)/shard_map/reshape | solution.py:56
  30.6 0.0 copy-done.3
  30.6 0.0 copy-done
  30.6 0.0 copy-done.1
  30.7 0.4 fusion.12
  31.0 0.1 reshape.61
  31.2 0.1 reshape.62
  31.3 5.4 %all-to-all-done = bf16[16,257,128]{2,1,0:T(8,128)(2,1)S(1)} async-done(((bf16[16,257,128]{2,1,0:T(8,128)(2,1)}), bf16[16,257,128]{2,1,0:T(8,128)(2,1)S(1)}, u32[]{:S(2)}, u32[]{:S(2)}) %all-to-all-start) | async-done | bytes 1052704 | tf_op jit(solution)/shard_map/all_to_all | solution.py:36
  36.7 1.2 %slice.30 = bf16[16,256,128]{2,1,0:T(8,128)(2,1)} slice(bf16[16,257,128]{2,1,0:T(8,128)(2,1)S(1)} %all-to-all-done), slice={[0:16], [0:256], [0:128]} | slice | bytes 2097152 | tf_op jit(solution)/shard_map/slice | solution.py:38
  37.8 2.3 %reshape.60 = bf16[4,128,1024]{2,1,0:T(8,128)(2,1)} reshape(bf16[16,256,128]{2,1,0:T(8,128)(2,1)} %slice.30) | data formatting | bytes 2097152 | tf_op jit(solution)/shard_map/reshape | solution.py:38
  40.2 0.1 reshape.66
  40.2 1.7 %multiply_reduce_fusion = f32[128,1024]{1,0:T(8,128)S(1)} fusion(bf16[4,128,1024]{2,1,0:T(8,128)(2,1)} %reshape.60, f32[4,1024]{1,0:T(4,128)S(1)} %convert_element_type.39, s32[4,128]{1,0:T(4,128)S(1)} %reshape.66), kind=kOutput, calls=%fused_computation.5 | convolution fusion | flops 135200768 | bytes 1591296 | tf_op jit(solution)/shard_map/cpk,ckd->cpd/dot_general | solution.py:46
  41.9 0.1 multiply_reduce_fusion.1
  42.1 6.0 %fusion.9 = bf16[16,128,128]{2,1,0:T(8,128)(2,1)S(1)} fusion(bf16[1024,16,64]{2,0,1:T(8,128)(2,1)} %copy.24, bf16[1024,16,64]{2,0,1:T(8,128)(2,1)} %copy.23, f32[128,1024]{1,0:T(8,128)S(1)} %multiply_reduce_fusion, f32[1024]{0:T(1024)S(1)} %convert_element_type.40, f32[128]{0:T(128)S(1)} %add_rsqrt_fusion), kind=kOutput, calls=%fused_computation.9 | convolution fusion | flops 545914880 | bytes 5247488 | tf_op jit(solution)/shard_map/pf,fhe->hpe/dot_general | solution.py:60
  48.1 23.6 %all_to_all.15 = bf16[16,136,128]{2,1,0:T(8,128)(2,1)S(1)} all-to-all(bf16[16,136,128]{2,1,0:T(8,128)(2,1)S(1)} %pad_maximum_fusion.1), channel_id=1, replica_groups=mesh['grp'=2,'blk'=16] {'blk'}, dimensions={0} | all-to-all | bytes 1114112 | tf_op jit(solution)/shard_map/all_to_all | solution.py:67
  71.7 0.1 reshape.63
  71.8 0.5 fusion.32
  72.3 0.4 fusion.4
  72.8 0.7 fusion.13
  73.5 0.1 copy.29
  73.6 0.1 reshape.68
  73.7 9.4 %all_to_all.16 = bf16[16,2,512]{2,1,0:T(2,128)(2,1)S(1)} all-to-all(bf16[16,2,512]{2,1,0:T(2,128)(2,1)S(1)} %reshape.68), channel_id=1, replica_groups=mesh['grp'=2,'blk'=16] {'blk'}, dimensions={0} | all-to-all | bytes 65536 | tf_op jit(solution)/shard_map/all_to_all | solution.py:83
  83.1 0.1 reshape.69
  83.2 0.1 reshape.65
  83.3 2.6 %fusion.14 = bf16[16,1024]{1,0:T(8,128)(2,1)} fusion(bf16[16,1024]{1,0:T(8,128)(2,1)S(1)} %reshape.65, bf16[1024,1024]{1,0:T(8,128)(2,1)} %param.17, bf16[16,1024]{1,0:T(8,128)(2,1)S(1)} %copy-done.1), kind=kOutput, calls=%fused_computation.15 | convolution fusion | flops 33603584 | bytes 2195456 | tf_op jit(solution)/shard_map/dot_general | solution.py:89
  (13 shorter events, 0.2 us)
Async XLA Ops:
  0.0 30.6 %copy-start = (bf16[1024,1024]{1,0:T(8,128)(2,1)S(1)}, bf16[1024,1024]{1,0:T(8,128)(2,1)}, u32[]{:S(2)}) copy-start(bf16[1024,1024]{1,0:T(8,128)(2,1)} %param.14) | copy-start | bytes 6291460
  0.0 4.5 %copy-start.4 = (s32[512]{0:T(512)S(1)}, s32[512]{0:T(512)}, u32[]{:S(2)}) copy-start(s32[512]{0:T(512)} %param.10) | copy-start | bytes 6148
  4.7 8.5 %copy-start.2 = (bf16[4,1024]{1,0:T(4,128)(2,1)S(1)}, bf16[4,1024]{1,0:T(4,128)(2,1)}, u32[]{:S(2)}) copy-start(bf16[4,1024]{1,0:T(4,128)(2,1)} %param.12) | copy-start | bytes 24580
  5.8 30.9 %all-to-all-start = ((bf16[16,257,128]{2,1,0:T(8,128)(2,1)}), bf16[16,257,128]{2,1,0:T(8,128)(2,1)S(1)}, u32[]{:S(2)}, u32[]{:S(2)}) async-start(bf16[16,257,128]{2,1,0:T(8,128)(2,1)} %pad_maximum_fusion), calls=%async_computation | async-start | bytes 2162688 | tf_op jit(solution)/shard_map/all_to_all | solution.py:36
  25.9 4.8 %copy-start.3 = (bf16[1024]{0:T(1024)(128)(2,1)S(1)}, bf16[1024]{0:T(1024)(128)(2,1)}, u32[]{:S(2)}) copy-start(bf16[1024]{0:T(1024)(128)(2,1)} %param.13) | copy-start | bytes 6148
  25.9 4.8 %copy-start.1 = (bf16[16,1024]{1,0:T(8,128)(2,1)S(1)}, bf16[16,1024]{1,0:T(8,128)(2,1)}, u32[]{:S(2)}) copy-start(bf16[16,1024]{1,0:T(8,128)(2,1)} %param.11) | copy-start | bytes 98308

commit v5 on v4

--- a/solution.py
+++ b/solution.py
@@ -57,9 +57,12 @@
         ],
         axis=-1,
     )
-    pair_rows = jnp.einsum(
-        "pf,fhe->hpe", normed, pair_weight, preferred_element_type=jnp.float32
+    pair_rows = jnp.dot(
+        normed,
+        pair_weight.reshape(model_width, 2 * model_width),
+        preferred_element_type=jnp.float32,
     ).astype(jnp.bfloat16)
+    pair_rows = jnp.transpose(pair_rows.reshape(patches_dev, head_count, 2 * head_width), (1, 0, 2))
     query_parts = jnp.transpose(queries.reshape(lat_rows, head_count, head_width), (1, 0, 2))
     query_parts = query_parts.reshape(head_count, -1, 2 * head_width)
     query_len = query_parts.shape[1]

time: 86.6 us -> 85 us (0.982)
  local copies, waits for them, and re-layouts: 26.5 us -> 16.9 us
  other arithmetic: 1.73 us -> 7.37 us
  waiting for transfers between devices: 5.37 us -> 10.1 us
  matrix products: 11.9 us -> 9.62 us
    reshape x2 -> x1, local copies, waits for them, and re-layouts: 9.55 us -> 0.13 us  [local(): pair_rows.reshape(patches_dev, head_count, 2 * head_width)]
    concatenate x0 -> x1, other arithmetic: none -> 4.76 us  [local(): jnp.concatenate([w_key.reshape(model_width, head_count, head_width), w_va...]
    all_to_all x1, waiting for transfers between devices: 5.37 us -> 10.1 us  [local(): lax.all_to_all(payload, 'blk', split_axis=0, concat_axis=0, tiled=True)]
    dot_general x1, matrix products: 5.98 us -> 3.7 us  [local(): jnp.dot(normed, pair_weight.reshape(model_width, 2 * model_width), prefer...]
    unnamed x15 -> x13, local copies, waits for them, and re-layouts: 8.13 us -> 8.18 us
  transfers between devices with their start and end apart: 1 -> 1, of which waited for: 1 -> 1; matrix products, arithmetic and copies ran while one was open for 21% -> 16% of each run, Pallas kernels for 0% -> 0%
where the time goes in v5:
time: 85 us; the launch traced here: 84.5 us
  blocking collectives  32.9 us (39%)
  local copies, waits for them, and re-layouts  16.9 us (20%)
  waiting for transfers between devices  10.1 us (12%)
  matrix products  9.62 us (11%)
  starting transfers between devices  7.39 us (9%)
  other arithmetic  7.37 us (9%)
    all_to_all x1, blocking collectives, local(): lax.all_to_all(pair_payload, 'blk', split_axis=0, concat_axis=0, tiled=True)  23.6 us
    all_to_all x1, waiting for transfers between devices, local(): lax.all_to_all(payload, 'blk', split_axis=0, concat_axis=0, tiled=True)  10.1 us
    all_to_all x1, blocking collectives, local(): lax.all_to_all(jnp.tile(attended_head, (copies, 1, 1)), 'blk', split_axis...  9.35 us
    unnamed x13, local copies, waits for them, and re-layouts  8.18 us
    all_to_all x1, starting transfers between devices, local(): lax.all_to_all(payload, 'blk', split_axis=0, concat_axis=0, tiled=True)  7.39 us
    concatenate x1, other arithmetic, local(): jnp.concatenate([w_key.reshape(model_width, head_count, head_width), w_va...  4.76 us
    dot_general x1, matrix products, local(): jnp.dot(normed, pair_weight.reshape(model_width, 2 * model_width), prefer...  3.7 us
    reshape x1, local copies, waits for them, and re-layouts, local(): tokens.reshape(per_peer, cycle_size, model_width)  2.82 us
  transfers between devices with their start and end apart: 1, of which 1 were waited for; matrix products, arithmetic and copies ran while one was open for 16% of the time, Pallas kernels for 0%

profile of v5, /device:TPU:0, one launch (start us, length us, event | category | flops | bytes accessed | tf_op | source)
XLA Modules:
  0.0 84.5 jit_solution(427703326286122410)
XLA Ops:
  0.0 0.0 copy-start
  0.0 0.8 fusion.16
  0.8 0.1 reshape.61
  0.9 0.1 copy.30
  1.0 2.8 %copy.45 = bf16[32,16,1024]{2,0,1:T(8,128)(2,1)} copy(bf16[32,16,1024]{2,1,0:T(8,128)(2,1)} %bitcast.41) | data formatting | bytes 2097152 | tf_op jit(solution)/shard_map/reshape | solution.py:27
  3.8 1.5 %reshape.60 = bf16[16,256,128]{2,1,0:T(8,128)(2,1)S(1)} reshape(bf16[16,32,1024]{2,1,0:T(8,128)(2,1)} %bitcast.39) | data formatting | bytes 2097152 | tf_op jit(solution)/shard_map/reshape | solution.py:28
  5.4 0.0 copy-start.1
  5.4 1.2 %pad_maximum_fusion.1 = bf16[16,257,128]{2,1,0:T(8,128)(2,1)} fusion(bf16[16,1,128]{2,1,0:T(2,128)(2,1)S(1)} %copy.30, bf16[16,256,128]{2,1,0:T(8,128)(2,1)S(1)} %reshape.60), kind=kLoop, calls=%fused_computation.13 | loop fusion | flops 2105344 | bytes 2105344 | tf_op jit(solution)/shard_map/concatenate | solution.py:35
  6.5 7.4 %all-to-all-start = ((bf16[16,257,128]{2,1,0:T(8,128)(2,1)}), bf16[16,257,128]{2,1,0:T(8,128)(2,1)S(1)}, u32[]{:S(2)}, u32[]{:S(2)}) async-start(bf16[16,257,128]{2,1,0:T(8,128)(2,1)} %pad_maximum_fusion.1), calls=%async_computation | async-start | bytes 2162688 | tf_op jit(solution)/shard_map/all_to_all | solution.py:36
  13.9 0.0 copy-done
  13.9 0.0 copy-done.1
  13.9 0.4 fusion.3
  14.3 0.1 reshape.69
  14.5 0.1 reshape.70
  14.6 4.0 %copy.32 = bf16[1024,1024]{0,1:T(8,128)(2,1)} copy(bf16[1024,1024]{1,0:T(8,128)(2,1)} %param.16) | data formatting | bytes 4194304 | tf_op args[7]
  18.5 0.0 copy-start.2
  18.5 0.0 copy-start.3
  18.5 4.0 %copy.31 = bf16[1024,1024]{0,1:T(8,128)(2,1)} copy(bf16[1024,1024]{1,0:T(8,128)(2,1)} %param.15) | data formatting | bytes 4194304 | tf_op args[6]
  22.5 0.0 copy-done.2
  22.5 0.0 copy-done.3
  22.5 4.8 %pad_maximum_fusion = bf16[1024,16,128]{0,2,1:T(8,128)(2,1)} fusion(bf16[1024,16,64]{0,2,1:T(8,128)(2,1)} %bitcast.35, bf16[1024,16,64]{0,2,1:T(8,128)(2,1)} %bitcast.36), kind=kLoop, calls=%fused_computation | loop fusion | flops 8388608 | bytes 8388608 | tf_op jit(solution)/shard_map/concatenate | solution.py:53
  27.3 10.1 %all-to-all-done = bf16[16,257,128]{2,1,0:T(8,128)(2,1)S(1)} async-done(((bf16[16,257,128]{2,1,0:T(8,128)(2,1)}), bf16[16,257,128]{2,1,0:T(8,128)(2,1)S(1)}, u32[]{:S(2)}, u32[]{:S(2)}) %all-to-all-start) | async-done | bytes 1052704 | tf_op jit(solution)/shard_map/all_to_all | solution.py:36
  37.4 1.1 %slice.30 = bf16[16,256,128]{2,1,0:T(8,128)(2,1)} slice(bf16[16,257,128]{2,1,0:T(8,128)(2,1)S(1)} %all-to-all-done), slice={[0:16], [0:256], [0:128]} | slice | bytes 2097152 | tf_op jit(solution)/shard_map/slice | solution.py:38
  38.5 2.3 %reshape.64 = bf16[4,128,1024]{2,1,0:T(8,128)(2,1)} reshape(bf16[16,256,128]{2,1,0:T(8,128)(2,1)} %slice.30) | data formatting | bytes 2097152 | tf_op jit(solution)/shard_map/reshape | solution.py:38
  40.8 0.1 reshape.74
  40.9 1.7 %multiply_reduce_fusion = f32[128,1024]{1,0:T(8,128)S(1)} fusion(bf16[4,128,1024]{2,1,0:T(8,128)(2,1)} %reshape.64, f32[4,1024]{1,0:T(4,128)S(1)} %convert_element_type.36, s32[4,128]{1,0:T(4,128)S(1)} %reshape.74), kind=kOutput, calls=%fused_computation.3 | convolution fusion | flops 135200768 | bytes 1591296 | tf_op jit(solution)/shard_map/cpk,ckd->cpd/dot_general | solution.py:46
  42.6 0.1 multiply_reduce_fusion.1
  42.7 3.7 %fusion.2 = bf16[16,16,8,128]{3,2,1,0:T(8,128)(2,1)S(1)} fusion(bf16[1024,2048]{0,1:T(8,128)(2,1)} %bitcast.34, f32[128,1024]{1,0:T(8,128)S(1)} %multiply_reduce_fusion, f32[1024]{0:T(1024)S(1)} %convert_element_type.37, f32[128]{0:T(128)S(1)} %add_rsqrt_fusion), kind=kOutput, calls=%fused_computation.6 | convolution fusion | flops 537526272 | bytes 5247488 | tf_op jit(solution)/shard_map/dot_general | solution.py:60
  46.5 0.1 copy.46
  46.6 23.6 %all_to_all.15 = bf16[16,136,128]{2,1,0:T(8,128)(2,1)S(1)} all-to-all(bf16[16,136,128]{2,1,0:T(8,128)(2,1)S(1)} %pad_maximum_fusion.2), channel_id=1, replica_groups=mesh['grp'=2,'blk'=16] {'blk'}, dimensions={0} | all-to-all | bytes 1114112 | tf_op jit(solution)/shard_map/all_to_all | solution.py:70
  70.2 0.1 reshape.71
  70.3 0.5 fusion.20
  70.9 0.4 fusion
  71.3 0.7 fusion.4
  72.0 0.1 copy.35
  72.1 0.1 reshape.75
  72.2 9.4 %all_to_all.16 = bf16[16,2,512]{2,1,0:T(2,128)(2,1)S(1)} all-to-all(bf16[16,2,512]{2,1,0:T(2,128)(2,1)S(1)} %reshape.75), channel_id=1, replica_groups=mesh['grp'=2,'blk'=16] {'blk'}, dimensions={0} | all-to-all | bytes 65536 | tf_op jit(solution)/shard_map/all_to_all | solution.py:86
  81.6 0.1 reshape.76
  81.7 0.1 reshape.73
  81.9 2.6 %fusion.5 = bf16[16,1024]{1,0:T(8,128)(2,1)} fusion(bf16[16,1024]{1,0:T(8,128)(2,1)S(1)} %reshape.73, bf16[1024,1024]{1,0:T(8,128)(2,1)} %param.17, bf16[16,1024]{1,0:T(8,128)(2,1)S(1)} %copy-done.1), kind=kOutput, calls=%fused_computation.12 | convolution fusion | flops 33603584 | bytes 2195456 | tf_op jit(solution)/shard_map/dot_general | solution.py:92
  (12 shorter events, 0.2 us)
Async XLA Ops:
  0.0 13.9 %copy-start = (bf16[1024,1024]{1,0:T(8,128)(2,1)S(1)}, bf16[1024,1024]{1,0:T(8,128)(2,1)}, u32[]{:S(2)}) copy-start(bf16[1024,1024]{1,0:T(8,128)(2,1)} %param.14) | copy-start | bytes 6291460
  5.4 8.6 %copy-start.1 = (bf16[16,1024]{1,0:T(8,128)(2,1)S(1)}, bf16[16,1024]{1,0:T(8,128)(2,1)}, u32[]{:S(2)}) copy-start(bf16[16,1024]{1,0:T(8,128)(2,1)} %param.11) | copy-start | bytes 98308
  6.5 30.9 %all-to-all-start = ((bf16[16,257,128]{2,1,0:T(8,128)(2,1)}), bf16[16,257,128]{2,1,0:T(8,128)(2,1)S(1)}, u32[]{:S(2)}, u32[]{:S(2)}) async-start(bf16[16,257,128]{2,1,0:T(8,128)(2,1)} %pad_maximum_fusion.1), calls=%async_computation | async-start | bytes 2162688 | tf_op jit(solution)/shard_map/all_to_all | solution.py:36
  18.5 4.0 %copy-start.2 = (bf16[4,1024]{1,0:T(4,128)(2,1)S(1)}, bf16[4,1024]{1,0:T(4,128)(2,1)}, u32[]{:S(2)}) copy-start(bf16[4,1024]{1,0:T(4,128)(2,1)} %param.12) | copy-start | bytes 24580
  18.5 4.0 %copy-start.3 = (bf16[1024]{0:T(1024)(128)(2,1)S(1)}, bf16[1024]{0:T(1024)(128)(2,1)}, u32[]{:S(2)}) copy-start(bf16[1024]{0:T(1024)(128)(2,1)} %param.13) | copy-start | bytes 6148

commit v6 on v5

--- a/solution.py
+++ b/solution.py
@@ -23,24 +23,19 @@
     queries = (
         jnp.dot(latents, w_query, preferred_element_type=jnp.float32) * head_width ** (-0.5)
     ).astype(jnp.bfloat16)
-    token_parts = jnp.transpose(
-        tokens.reshape(per_peer, cycle_size, model_width), (1, 0, 2)
-    ).reshape(cycle_size, -1, lanes)
     row_dest = lax.broadcasted_iota(jnp.int32, (tok_rows,), 0) % cycle_size
     local_ids = (patch_of_row - row_dest * patches_dev).astype(jnp.bfloat16)
-    id_parts = jnp.transpose(local_ids.reshape(per_peer, cycle_size))
-    id_width = -(-per_peer // lanes) * lanes
-    id_parts = jnp.pad(id_parts, ((0, 0), (0, id_width - per_peer))).reshape(cycle_size, -1, lanes)
-    token_len = token_parts.shape[1]
-    payload = jnp.concatenate([token_parts, id_parts], axis=1)
+    id_lanes = jnp.pad(local_ids[:, None], ((0, 0), (0, lanes - 1)))
+    payload = jnp.transpose(
+        jnp.concatenate([tokens, id_lanes], axis=1).reshape(
+            per_peer, cycle_size, model_width + lanes
+        ),
+        (1, 0, 2),
+    )
     got = lax.all_to_all(payload, "blk", split_axis=0, concat_axis=0, tiled=True)
 
-    recv_rows = got[:, :token_len].reshape(CONTRASTS, patches_dev, model_width)
-    recv_ids = (
-        got[:, token_len:].reshape(cycle_size, id_width)[:, :per_peer]
-        .astype(jnp.int32)
-        .reshape(CONTRASTS, 1, patches_dev)
-    )
+    recv_rows = got[:, :, :model_width].reshape(CONTRASTS, patches_dev, model_width)
+    recv_ids = got[:, :, model_width].astype(jnp.int32).reshape(CONTRASTS, 1, patches_dev)
     patch_iota = lax.broadcasted_iota(jnp.int32, (CONTRASTS, patches_dev, patches_dev), 1)
     selector = (recv_ids == patch_iota).astype(jnp.bfloat16)
     arranged = jnp.einsum(

time: 85 us -> 79.2 us (0.932)
  local copies, waits for them, and re-layouts: 16.9 us -> 12 us
  matrix products: 9.62 us -> 6.17 us
  waiting for transfers between devices: 10.1 us -> 11.7 us
    reshape x6 -> x0, local copies, waits for them, and re-layouts: 6.81 us -> none  [the longest x1 2.82 us: local(): tokens.reshape(per_peer, cycle_size, model_width)]
    dot_general x1, matrix products: 3.7 us -> 1.5 us  [local(): jnp.dot(normed, pair_weight.reshape(model_width, 2 * model_width), prefer...]
    all_to_all x1, waiting for transfers between devices: 10.1 us -> 11.7 us  [local(): lax.all_to_all(payload, 'blk', split_axis=0, concat_axis=0, tiled=True)]
    unnamed x13 -> x14, local copies, waits for them, and re-layouts: 8.18 us -> 9.65 us
    transpose x0 -> x1, local copies, waits for them, and re-layouts: none -> 1.31 us  [local(): jnp.transpose(jnp.concatenate([tokens, id_lanes], axis=1).reshape(per_pee...]
    dot_general x1, matrix products: 1.7 us -> 0.45 us  [local(): jnp.einsum('cpk,ckd->cpd', selector, recv_rows, preferred_element_type=jn...]
    slice x2 -> x1, local copies, waits for them, and re-layouts: 1.09 us -> 0.13 us  [local(): got[:, :, :model_width].reshape(CONTRASTS, patches_dev, model_width)]
  transfers between devices with their start and end apart: 1 -> 1, of which waited for: 1 -> 1; matrix products, arithmetic and copies ran while one was open for 16% -> 17% of each run, Pallas kernels for 0% -> 0%
where the time goes in v6:
time: 79.2 us; the launch traced here: 78.8 us
  blocking collectives  33.4 us (42%)
  local copies, waits for them, and re-layouts  12 us (15%)
  waiting for transfers between devices  11.7 us (15%)
  other arithmetic  7.88 us (10%)
  starting transfers between devices  7.39 us (9%)
  matrix products  6.17 us (8%)
    all_to_all x1, blocking collectives, local(): lax.all_to_all(pair_payload, 'blk', split_axis=0, concat_axis=0, tiled=True)  24 us
    all_to_all x1, waiting for transfers between devices, local(): lax.all_to_all(payload, 'blk', split_axis=0, concat_axis=0, tiled=True)  11.7 us
    unnamed x14, local copies, waits for them, and re-layouts  9.65 us
    all_to_all x1, blocking collectives, local(): lax.all_to_all(jnp.tile(attended_head, (copies, 1, 1)), 'blk', split_axis...  9.36 us
    all_to_all x1, starting transfers between devices, local(): lax.all_to_all(payload, 'blk', split_axis=0, concat_axis=0, tiled=True)  7.39 us
    concatenate x1, other arithmetic, local(): jnp.concatenate([w_key.reshape(model_width, head_count, head_width), w_va...  4.76 us
    dot_general x1, matrix products, local(): jnp.dot(attended, w_out, preferred_element_type=jnp.float32)  2.6 us
  transfers between devices with their start and end apart: 1, of which 1 were waited for; matrix products, arithmetic and copies ran while one was open for 17% of the time, Pallas kernels for 0%

profile of v6, /device:TPU:0, one launch (start us, length us, event | category | flops | bytes accessed | tf_op | source)
XLA Modules:
  0.0 78.8 jit_solution(2139735382872723448)
XLA Ops:
  0.0 0.0 copy-start
  0.0 0.8 %fusion.18 = bf16[512]{0:T(512)(128)(2,1)S(1)} fusion(s32[512]{0:T(512)} %param.10), kind=kLoop, calls=%fused_computation.33 | loop fusion | flops 4608 | bytes 3072 | tf_op jit(solution)/shard_map/convert_element_type | solution.py:27
  0.8 0.1 broadcast_in_dim.3
  1.0 1.3 %fusion.4 = bf16[512,1152]{1,0:T(8,128)(2,1)S(1)} fusion(bf16[512,1]{1,0:T(8,128)(2,1)S(1)} %broadcast_in_dim.3, bf16[512,1024]{1,0:T(8,128)(2,1)} %param.9), kind=kLoop, calls=%fused_computation.9 | loop fusion | flops 3538944 | bytes 2229248 | tf_op jit(solution)/shard_map/concatenate | solution.py:30
  2.3 0.0 copy-start.2
  2.3 1.3 %copy.36 = bf16[16,32,1152]{2,1,0:T(8,128)(2,1)} copy(bf16[16,32,1152]{2,0,1:T(8,128)(2,1)S(1)} %bitcast.31) | data formatting | bytes 2359296 | tf_op jit(solution)/shard_map/transpose | solution.py:29
  3.6 7.4 %all-to-all-start = ((bf16[16,32,1152]{2,1,0:T(8,128)(2,1)}), bf16[16,32,1152]{2,1,0:T(8,128)(2,1)S(1)}, u32[]{:S(2)}, u32[]{:S(2)}) async-start(bf16[16,32,1152]{2,1,0:T(8,128)(2,1)} %copy.36), calls=%async_computation | async-start | bytes 2359296 | tf_op jit(solution)/shard_map/all_to_all | solution.py:35
  11.0 0.0 copy-done
  11.0 0.0 copy-done.2
  11.0 0.4 fusion.5
  11.4 0.1 reshape.59
  11.6 0.1 reshape.60
  11.7 4.0 %copy.38 = bf16[1024,1024]{0,1:T(8,128)(2,1)} copy(bf16[1024,1024]{1,0:T(8,128)(2,1)} %param.16) | data formatting | bytes 4194304 | tf_op args[7]
  15.6 0.0 copy-start.3
  15.6 0.0 copy-start.4
  15.6 4.0 %copy.37 = bf16[1024,1024]{0,1:T(8,128)(2,1)} copy(bf16[1024,1024]{1,0:T(8,128)(2,1)} %param.15) | data formatting | bytes 4194304 | tf_op args[6]
  19.6 0.0 copy-done.3
  19.6 0.0 copy-done.4
  19.6 4.8 %pad_maximum_fusion = bf16[1024,16,128]{0,2,1:T(8,128)(2,1)} fusion(bf16[1024,16,64]{0,2,1:T(8,128)(2,1)} %bitcast.29, bf16[1024,16,64]{0,2,1:T(8,128)(2,1)} %bitcast.30), kind=kLoop, calls=%fused_computation | loop fusion | flops 8388608 | bytes 8388608 | tf_op jit(solution)/shard_map/concatenate | solution.py:48
  24.4 11.7 %all-to-all-done = bf16[16,32,1152]{2,1,0:T(8,128)(2,1)S(1)} async-done(((bf16[16,32,1152]{2,1,0:T(8,128)(2,1)}), bf16[16,32,1152]{2,1,0:T(8,128)(2,1)S(1)}, u32[]{:S(2)}, u32[]{:S(2)}) %all-to-all-start) | async-done | bytes 1179680 | tf_op jit(solution)/shard_map/all_to_all | solution.py:35
  36.2 0.3 convert_reduce_fusion
  36.5 0.1 reshape.64
  36.6 0.0 copy-start.1
  36.6 0.1 slice.25
  36.7 0.4 multiply_reduce_fusion
  37.2 0.1 multiply_reduce_fusion.1
  37.3 1.5 %copy-done.1 = bf16[1024,16,128]{0,2,1:T(8,128)(2,1)S(1)} copy-done((bf16[1024,16,128]{0,2,1:T(8,128)(2,1)S(1)}, bf16[1024,16,128]{0,2,1:T(8,128)(2,1)}, u32[]{:S(2)}) %copy-start.1) | copy-done | bytes 4194328
  38.8 1.5 %fusion.3 = bf16[16,16,8,128]{3,2,1,0:T(8,128)(2,1)S(1)} fusion(bf16[1024,2048]{0,1:T(8,128)(2,1)S(1)} %bitcast.28, f32[128,1024]{1,0:T(8,128)S(1)} %multiply_reduce_fusion, f32[1024]{0:T(1024)S(1)} %convert_element_type.48, f32[128]{0:T(128)S(1)} %add_rsqrt_fusion), kind=kOutput, calls=%fused_computation.8 | convolution fusion | flops 537526272 | bytes 5247488 | tf_op jit(solution)/shard_map/dot_general | solution.py:55
  40.3 0.1 copy.47
  40.5 24.0 %all_to_all.15 = bf16[16,136,128]{2,1,0:T(8,128)(2,1)S(1)} all-to-all(bf16[16,136,128]{2,1,0:T(8,128)(2,1)S(1)} %pad_maximum_fusion.1), channel_id=1, replica_groups=mesh['grp'=2,'blk'=16] {'blk'}, dimensions={0} | all-to-all | bytes 1114112 | tf_op jit(solution)/shard_map/all_to_all | solution.py:65
  64.5 0.1 reshape.61
  64.6 0.5 fusion.22
  65.2 0.4 fusion.1
  65.6 0.7 fusion.6
  66.3 0.1 copy.41
  66.4 0.1 reshape.66
  66.5 9.4 %all_to_all.16 = bf16[16,2,512]{2,1,0:T(2,128)(2,1)S(1)} all-to-all(bf16[16,2,512]{2,1,0:T(2,128)(2,1)S(1)} %reshape.66), channel_id=1, replica_groups=mesh['grp'=2,'blk'=16] {'blk'}, dimensions={0} | all-to-all | bytes 65536 | tf_op jit(solution)/shard_map/all_to_all | solution.py:81
  75.9 0.1 reshape.67
  76.0 0.1 reshape.63
  76.2 2.6 %fusion.7 = bf16[16,1024]{1,0:T(8,128)(2,1)} fusion(bf16[16,1024]{1,0:T(8,128)(2,1)S(1)} %reshape.63, bf16[1024,1024]{1,0:T(8,128)(2,1)} %param.17, bf16[16,1024]{1,0:T(8,128)(2,1)S(1)} %copy-done.2), kind=kOutput, calls=%fused_computation.15 | convolution fusion | flops 33603584 | bytes 2195456 | tf_op jit(solution)/shard_map/dot_general | solution.py:87
  (8 shorter events, 0.1 us)
Async XLA Ops:
  0.0 11.0 %copy-start = (bf16[1024,1024]{1,0:T(8,128)(2,1)S(1)}, bf16[1024,1024]{1,0:T(8,128)(2,1)}, u32[]{:S(2)}) copy-start(bf16[1024,1024]{1,0:T(8,128)(2,1)} %param.14) | copy-start | bytes 6291460
  2.3 8.7 %copy-start.2 = (bf16[16,1024]{1,0:T(8,128)(2,1)S(1)}, bf16[16,1024]{1,0:T(8,128)(2,1)}, u32[]{:S(2)}) copy-start(bf16[16,1024]{1,0:T(8,128)(2,1)} %param.11) | copy-start | bytes 98308
  3.6 32.5 %all-to-all-start = ((bf16[16,32,1152]{2,1,0:T(8,128)(2,1)}), bf16[16,32,1152]{2,1,0:T(8,128)(2,1)S(1)}, u32[]{:S(2)}, u32[]{:S(2)}) async-start(bf16[16,32,1152]{2,1,0:T(8,128)(2,1)} %copy.36), calls=%async_computation | async-start | bytes 2359296 | tf_op jit(solution)/shard_map/all_to_all | solution.py:35
  15.6 4.0 %copy-start.3 = (bf16[4,1024]{1,0:T(4,128)(2,1)S(1)}, bf16[4,1024]{1,0:T(4,128)(2,1)}, u32[]{:S(2)}) copy-start(bf16[4,1024]{1,0:T(4,128)(2,1)} %param.12) | copy-start | bytes 24580
  15.6 4.0 %copy-start.4 = (bf16[1024]{0:T(1024)(128)(2,1)S(1)}, bf16[1024]{0:T(1024)(128)(2,1)}, u32[]{:S(2)}) copy-start(bf16[1024]{0:T(1024)(128)(2,1)} %param.13) | copy-start | bytes 6148
  36.6 2.2 %copy-start.1 = (bf16[1024,16,128]{0,2,1:T(8,128)(2,1)S(1)}, bf16[1024,16,128]{0,2,1:T(8,128)(2,1)}, u32[]{:S(2)}) copy-start(bf16[1024,16,128]{0,2,1:T(8,128)(2,1)} %pad_maximum_fusion) | copy-start | bytes 12582916

commit v7 on v6

v7 whole, which is shorter than its diff:
```python
import jax
import jax.numpy as jnp
from jax import lax
from jax.sharding import Mesh
from jax.sharding import PartitionSpec as P

HEADS = 16
CONTRASTS = 4
SIDE = 8
BLK = ("side", "rest")


def split_exact(value, upward):
    high = value.astype(jnp.bfloat16)
    rest = value - high.astype(jnp.float32)
    if upward:
        rest = rest + jnp.abs(rest) * (2.0 ** -8)
    return high, rest.astype(jnp.bfloat16)


def local(tokens, patch_of_row, latents, contrast_gain, norm_gain, w_query, w_key, w_value, w_out):
    cycle_size = lax.axis_size(BLK)
    my_index = lax.axis_index(BLK)
    side_size = lax.axis_size("rest")
    sides = cycle_size // side_size
    tok_rows, model_width = tokens.shape
    head_count = HEADS
    head_width = model_width // head_count
    heads_dev = head_count // side_size
    pair_width = heads_dev * head_width
    lat_rows = latents.shape[0]
    all_lat = lat_rows * cycle_size
    per_peer = tok_rows // cycle_size
    patches_dev = tok_rows // CONTRASTS
    lanes = 128
    query_lanes = (lat_rows * pair_width) // per_peer

    queries = (
        jnp.dot(latents, w_query, preferred_element_type=jnp.float32) * head_width ** (-0.5)
    ).astype(jnp.bfloat16)
    query_parts = jnp.tile(
        jnp.transpose(queries.reshape(lat_rows, side_size, pair_width), (1, 0, 2)),
        (sides, 1, 1),
    )
    embed = query_lanes < lanes
    if not embed:
        query_lanes = 0
    row_dest = lax.broadcasted_iota(jnp.int32, (tok_rows,), 0) % cycle_size
    local_ids = (patch_of_row - row_dest * patches_dev).astype(jnp.bfloat16)
    id_lanes = jnp.pad(local_ids[:, None], ((0, 0), (0, lanes - query_lanes - 1)))
    payload = jnp.transpose(
        jnp.concatenate([tokens, id_lanes], axis=1).reshape(
            per_peer, cycle_size, model_width + lanes - query_lanes
        ),
        (1, 0, 2),
    )
    if embed:
        payload = jnp.concatenate(
            [payload, query_parts.reshape(cycle_size, per_peer, query_lanes)], axis=2
        )
        got = lax.all_to_all(payload, BLK, split_axis=0, concat_axis=0, tiled=True)
        got_queries = got[:, :, model_width + lanes - query_lanes :]
    else:
        got = lax.all_to_all(payload, BLK, split_axis=0, concat_axis=0, tiled=True)
        got_queries = lax.all_to_all(query_parts, BLK, split_axis=0, concat_axis=0, tiled=True)

    recv_rows = got[:, :, :model_width].reshape(CONTRASTS, patches_dev, model_width)
    recv_ids = got[:, :, model_width].astype(jnp.int32).reshape(CONTRASTS, 1, patches_dev)
    head_queries = jnp.transpose(
        got_queries.reshape(all_lat, heads_dev, head_width), (1, 0, 2)
    )
    patch_iota = lax.broadcasted_iota(jnp.int32, (CONTRASTS, patches_dev, patches_dev), 1)
    selector = (recv_ids == patch_iota).astype(jnp.bfloat16)
    arranged = jnp.einsum(
        "cpk,ckd->cpd", selector, recv_rows, preferred_element_type=jnp.float32
    )
    joined = jnp.sum(arranged * contrast_gain.astype(jnp.float32)[:, None, :], axis=0)

    inverse_rms = lax.rsqrt(jnp.mean(joined * joined, axis=-1, keepdims=True) + 1e-05)
    normed = (joined * inverse_rms * norm_gain.astype(jnp.float32)).astype(jnp.bfloat16)
    pair_weight = jnp.concatenate(
        [
            w_key.reshape(model_width, head_count, head_width),
            w_value.reshape(model_width, head_count, head_width),
        ],
        axis=-1,
    )
    pair_rows = jnp.dot(
        normed,
        pair_weight.reshape(model_width, 2 * model_width),
        preferred_element_type=jnp.float32,
    ).astype(jnp.bfloat16)
    pair_rows = jnp.transpose(
        pair_rows.reshape(patches_dev, side_size, 2 * pair_width), (1, 0, 2)
    )
    got_pairs = lax.all_to_all(pair_rows, "rest", split_axis=0, concat_axis=0, tiled=True)
    got_pairs = jnp.transpose(
        got_pairs.reshape(side_size * patches_dev, heads_dev, 2 * head_width), (1, 0, 2)
    )
    head_keys = got_pairs[:, :, :head_width]
    head_values = got_pairs[:, :, head_width:]

    scores = jnp.einsum(
        "hld,hkd->hlk", head_queries, head_keys, preferred_element_type=jnp.float32
    )
    maxima = jnp.max(scores, axis=-1)
    max_high, max_low = split_exact(maxima, True)
    shift = max_high.astype(jnp.float32) + max_low.astype(jnp.float32)
    weights = jnp.exp(scores - shift[..., None])
    totals = jnp.sum(weights, axis=-1)
    tot_high, tot_low = split_exact(totals, False)
    summed = jnp.einsum(
        "hlk,hkd->lhd", weights.astype(jnp.bfloat16), head_values, preferred_element_type=jnp.float32
    ).astype(jnp.bfloat16)
    stats = jnp.transpose(jnp.stack([max_high, max_low, tot_high, tot_low], axis=-1), (1, 0, 2))
    part_payload = jnp.concatenate(
        [summed.reshape(all_lat, pair_width), stats.reshape(all_lat, heads_dev * 4)], axis=1
    ).reshape(cycle_size, lat_rows, pair_width + heads_dev * 4)
    got_parts = lax.all_to_all(part_payload, BLK, split_axis=0, concat_axis=0, tiled=True)
    got_parts = got_parts.astype(jnp.float32).reshape(sides, side_size, lat_rows, -1)
    part_sums = got_parts[..., :pair_width].reshape(
        sides, side_size, lat_rows, heads_dev, head_width
    )
    part_stats = got_parts[..., pair_width:].reshape(sides, side_size, lat_rows, heads_dev, 4)
    part_max = part_stats[..., 0] + part_stats[..., 1]
    part_tot = part_stats[..., 2] + part_stats[..., 3]
    top = jnp.max(part_max, axis=0)
    factor = jnp.exp(part_max - top[None])
    total = jnp.sum(part_tot * factor, axis=0)
    accum = jnp.sum(part_sums * factor[..., None], axis=0)
    attended = (accum / total[..., None]).astype(jnp.bfloat16)
    attended = jnp.transpose(attended, (1, 0, 2, 3)).reshape(lat_rows, model_width)
    mixed = latents.astype(jnp.float32) + jnp.dot(
        attended, w_out, preferred_element_type=jnp.float32
    )
    return mixed.astype(jnp.bfloat16)


def solution(mesh):
    groups, blocks = mesh.devices.shape
    side_mesh = Mesh(
        mesh.devices.reshape(groups, blocks // SIDE, SIDE), ("grp",) + BLK
    )
    rows = ("grp",) + BLK
    in_specs = (
        P(rows, None),
        P(rows),
        P(BLK, None),
        P(),
        P(),
        P(),
        P(),
        P(),
        P(),
    )
    out_specs = P(rows, None)
    return jax.shard_map(
        local, mesh=side_mesh, in_specs=in_specs, out_specs=out_specs, check_vma=False
    )
```

time: 79.2 us -> 79.4 us (level)
  blocking collectives: 33.4 us -> 13.2 us
  waiting for transfers between devices: 11.7 us -> 21.1 us
  starting transfers between devices: 7.39 us -> 14 us
  local copies, waits for them, and re-layouts: 12 us -> 15.9 us
    all_to_all x2 -> x1, blocking collectives: 33.4 us -> 13.2 us  [local(): lax.all_to_all(part_payload, BLK, split_axis=0, concat_axis=0, tiled=True)]
    all_to_all x1 -> x2, waiting for transfers between devices: 11.7 us -> 21.1 us  [the longest x1 12.4 us: local(): got = lax.all_to_all(payload, BLK, split_axis=0, concat_axis=0, tiled=True)]
    all_to_all x1 -> x2, starting transfers between devices: 7.39 us -> 14 us  [the longest x1 7.39 us: local(): got = lax.all_to_all(payload, BLK, split_axis=0, concat_axis=0, tiled=True)]
    reshape x6, local copies, waits for them, and re-layouts: 0.56 us -> 2.84 us  [the longest x2 1.58 us: local(): got_pairs.reshape(side_size * patches_dev, heads_dev, 2 * head_width)]
    unnamed x14 -> x18, local copies, waits for them, and re-layouts: 9.65 us -> 11.1 us
    transpose x2 -> x1, local copies, waits for them, and re-layouts: 1.33 us -> 0.01 us  [local(): jnp.transpose(queries.reshape(lat_rows, side_size, pair_width), (1, 0, 2))]
    concatenate x1 -> x2, other arithmetic: 0.04 us -> 1.27 us  [the longest x1 1.25 us: local(): jnp.concatenate([payload, query_parts.reshape(cycle_size, per_peer, query...]
    concatenate x1, other arithmetic: 1.32 us -> 0.1 us  [local(): jnp.concatenate([tokens, id_lanes], axis=1)]
  transfers between devices with their start and end apart: 1 -> 2, of which waited for: 1 -> 2; matrix products, arithmetic and copies ran while one was open for 17% -> 16% of each run, Pallas kernels for 0% -> 0%
where the time goes in v7:
time: 79.4 us; the launch traced here: 78.7 us
  waiting for transfers between devices  21.1 us (27%)
  local copies, waits for them, and re-layouts  15.9 us (20%)
  starting transfers between devices  14 us (18%)
  blocking collectives  13.2 us (17%)
  other arithmetic  7.44 us (9%)
  matrix products  6.78 us (9%)
    all_to_all x1, blocking collectives, local(): lax.all_to_all(part_payload, BLK, split_axis=0, concat_axis=0, tiled=True)  13.2 us
    all_to_all x1, waiting for transfers between devices, local(): got = lax.all_to_all(payload, BLK, split_axis=0, concat_axis=0, tiled=True)  12.4 us
    unnamed x18, local copies, waits for them, and re-layouts  11.1 us
    all_to_all x1, waiting for transfers between devices, local(): lax.all_to_all(pair_rows, 'rest', split_axis=0, concat_axis=0, tiled=True)  8.75 us
    all_to_all x1, starting transfers between devices, local(): got = lax.all_to_all(payload, BLK, split_axis=0, concat_axis=0, tiled=True)  7.39 us
    all_to_all x1, starting transfers between devices, local(): lax.all_to_all(pair_rows, 'rest', split_axis=0, concat_axis=0, tiled=True)  6.58 us
    concatenate x1, other arithmetic, local(): jnp.concatenate([w_key.reshape(model_width, head_count, head_width), w_va...  4.76 us
    dot_general x1, matrix products, local(): jnp.dot(attended, w_out, preferred_element_type=jnp.float32)  2.6 us
  transfers between devices with their start and end apart: 2, of which 2 were waited for; matrix products, arithmetic and copies ran while one was open for 16% of the time, Pallas kernels for 0%

profile of v7, /device:TPU:0, one launch (start us, length us, event | category | flops | bytes accessed | tf_op | source)
XLA Modules:
  0.0 78.7 jit_solution(4982016061456385399)
XLA Ops:
  0.0 0.0 copy-start
  0.0 1.6 %copy-done = bf16[1024,1024]{1,0:T(8,128)(2,1)S(1)} copy-done((bf16[1024,1024]{1,0:T(8,128)(2,1)S(1)}, bf16[1024,1024]{1,0:T(8,128)(2,1)}, u32[]{:S(2)}) %copy-start) | copy-done | bytes 2097176
  1.6 1.1 %fusion.7 = bf16[2,8,8,128]{3,1,2,0:T(8,128)(2,1)S(1)} fusion(bf16[16,1024]{1,0:T(8,128)(2,1)} %param.11, bf16[1024,1024]{1,0:T(8,128)(2,1)S(1)} %copy-done), kind=kOutput, calls=%fused_computation.17 | convolution fusion | flops 33587200 | bytes 2162688 | tf_op jit(solution)/shard_map/dot_general | solution.py:39
  2.8 0.1 tile.9
  2.9 0.0 copy-done.6
  2.9 0.1 broadcast_in_dim.3
  3.1 0.0 copy-done.2
  3.1 0.1 fusion.3
  3.2 0.2 copy.75
  3.4 1.2 %pad_maximum_fusion.1 = bf16[16,32,1152]{2,1,0:T(8,128)(2,1)} fusion(bf16[16,32,64]{2,1,0:T(8,128)(2,1)S(1)} %tile.9, bf16[16,32,1088]{2,1,0:T(8,128)(2,1)S(1)} %bitcast.69), kind=kLoop, calls=%fused_computation.9 | loop fusion | flops 2359296 | bytes 2359296 | tf_op jit(solution)/shard_map/concatenate | solution.py:58
  4.6 7.4 %all-to-all-start = ((bf16[16,32,1152]{2,1,0:T(8,128)(2,1)}), bf16[16,32,1152]{2,1,0:T(8,128)(2,1)S(1)}, u32[]{:S(2)}, u32[]{:S(2)}) async-start(bf16[16,32,1152]{2,1,0:T(8,128)(2,1)} %pad_maximum_fusion.1), calls=%async_computation | async-start | bytes 2359296 | tf_op jit(solution)/shard_map/all_to_all | solution.py:61
  12.0 4.0 %copy.55 = bf16[1024,1024]{0,1:T(8,128)(2,1)} copy(bf16[1024,1024]{1,0:T(8,128)(2,1)} %param.16) | data formatting | bytes 4194304 | tf_op args[7]
  16.0 4.0 %copy.54 = bf16[1024,1024]{0,1:T(8,128)(2,1)} copy(bf16[1024,1024]{1,0:T(8,128)(2,1)} %param.15) | data formatting | bytes 4194304 | tf_op args[6]
  20.0 0.0 copy-done.4
  20.0 0.0 copy-done.5
  20.0 4.8 %pad_maximum_fusion = bf16[1024,16,128]{0,2,1:T(8,128)(2,1)} fusion(bf16[1024,16,64]{0,2,1:T(8,128)(2,1)} %bitcast.67, bf16[1024,16,64]{0,2,1:T(8,128)(2,1)} %bitcast.68), kind=kLoop, calls=%fused_computation | loop fusion | flops 8388608 | bytes 8388608 | tf_op jit(solution)/shard_map/concatenate | solution.py:81
  24.7 12.4 %all-to-all-done = bf16[16,32,1152]{2,1,0:T(8,128)(2,1)S(1)} async-done(((bf16[16,32,1152]{2,1,0:T(8,128)(2,1)}), bf16[16,32,1152]{2,1,0:T(8,128)(2,1)S(1)}, u32[]{:S(2)}, u32[]{:S(2)}) %all-to-all-start) | async-done | bytes 1179680 | tf_op jit(solution)/shard_map/all_to_all | solution.py:61
  37.2 0.3 convert_reduce_fusion
  37.5 0.1 reshape.141
  37.6 0.1 slice.45
  37.7 0.4 multiply_reduce_fusion
  38.2 0.1 multiply_reduce_fusion.1
  38.3 1.5 %copy-done.1 = bf16[1024,16,128]{0,2,1:T(8,128)(2,1)S(1)} copy-done((bf16[1024,16,128]{0,2,1:T(8,128)(2,1)S(1)}, bf16[1024,16,128]{0,2,1:T(8,128)(2,1)}, u32[]{:S(2)}) %copy-start.1) | copy-done | bytes 4194328
  39.8 1.5 %convolution_convert_fusion = bf16[128,2048]{1,0:T(8,128)(2,1)S(1)} fusion(bf16[1024,2048]{0,1:T(8,128)(2,1)S(1)} %bitcast.66, f32[128,1024]{1,0:T(8,128)S(1)} %multiply_reduce_fusion, f32[1024]{0:T(1024)S(1)} %convert_element_type.148, f32[128]{0:T(128)S(1)} %add_rsqrt_fusion), kind=kOutput, calls=%fused_computation.1 | convolution fusion | flops 537526272 | bytes 5247488 | tf_op jit(solution)/shard_map/dot_general | solution.py:88
  41.3 0.8 %copy.76 = bf16[16,8,8,256]{3,2,0,1:T(8,128)(2,1)} copy(bf16[16,8,8,256]{3,2,1,0:T(8,128)(2,1)S(1)} %bitcast.71) | data formatting | bytes 1048576 | tf_op jit(solution)/shard_map/reshape | solution.py:94
  42.1 6.6 %all-to-all-start.1 = ((bf16[8,128,256]{2,1,0:T(8,128)(2,1)}), bf16[8,128,256]{2,1,0:T(8,128)(2,1)}, u32[]{:S(2)}, u32[]{:S(2)}) async-start(bf16[8,128,256]{2,1,0:T(8,128)(2,1)} %bitcast.72), calls=%async_computation.1 | async-start | bytes 1048576 | tf_op jit(solution)/shard_map/all_to_all | solution.py:96
  48.7 0.1 slice.47
  48.8 0.1 copy.58
  48.9 8.7 %all-to-all-done.1 = bf16[8,128,256]{2,1,0:T(8,128)(2,1)} async-done(((bf16[8,128,256]{2,1,0:T(8,128)(2,1)}), bf16[8,128,256]{2,1,0:T(8,128)(2,1)}, u32[]{:S(2)}, u32[]{:S(2)}) %all-to-all-start.1) | async-done | bytes 524320 | tf_op jit(solution)/shard_map/all_to_all | solution.py:96
  57.7 1.2 %reshape.144 = bf16[1024,2,128]{2,1,0:T(2,128)(2,1)S(1)} reshape(bf16[8,128,256]{2,1,0:T(8,128)(2,1)} %all-to-all-done.1) | data formatting | bytes 1048576 | tf_op jit(solution)/shard_map/reshape | solution.py:98
  58.8 0.4 copy.65
  59.3 0.6 fusion.30
  59.8 0.5 fusion.1
  60.4 0.5 fusion.4
  61.0 0.1 concatenate.21
  61.0 0.1 copy.60
  61.2 0.1 copy.59
  61.3 0.1 concatenate.20
  61.4 13.2 %all_to_all.15 = bf16[16,16,136]{2,1,0:T(8,128)(2,1)S(1)} all-to-all(bf16[16,16,136]{2,1,0:T(8,128)(2,1)S(1)} %pad_maximum_fusion.2), channel_id=1, replica_groups=mesh['grp'=2,'side'=2,'rest'=8] {'side','rest'}, dimensions={0} | all-to-all | bytes 139264 | tf_op jit(solution)/shard_map/all_to_all | solution.py:119
  74.7 0.1 copy.66
  74.8 0.2 copy.62
  75.0 0.3 mul.91
  75.3 0.2 mul.92
  75.5 0.1 reduce_sum.56
  75.7 0.1 copy.64
  75.8 0.2 fusion.17
  76.0 0.1 reshape.140
  76.1 2.6 %fusion.6 = bf16[16,1024]{1,0:T(8,128)(2,1)} fusion(bf16[16,1024]{1,0:T(8,128)(2,1)S(1)} %reshape.140, bf16[1024,1024]{1,0:T(8,128)(2,1)} %param.17, bf16[16,1024]{1,0:T(8,128)(2,1)S(1)} %copy-done.3), kind=kOutput, calls=%fused_computation.16 | convolution fusion | flops 33603584 | bytes 2195456 | tf_op jit(solution)/shard_map/dot_general | solution.py:133
  (26 shorter events, 0.2 us)
Async XLA Ops:
  0.0 1.6 %copy-start = (bf16[1024,1024]{1,0:T(8,128)(2,1)S(1)}, bf16[1024,1024]{1,0:T(8,128)(2,1)}, u32[]{:S(2)}) copy-start(bf16[1024,1024]{1,0:T(8,128)(2,1)} %param.14) | copy-start | bytes 6291460
  0.0 2.9 %copy-start.6 = (s32[512]{0:T(512)S(1)}, s32[512]{0:T(512)}, u32[]{:S(2)}) copy-start(s32[512]{0:T(512)} %param.10) | copy-start | bytes 6148
  0.0 3.0 %copy-start.2 = (bf16[512,1024]{1,0:T(8,128)(2,1)S(1)}, bf16[512,1024]{1,0:T(8,128)(2,1)}, u32[]{:S(2)}) copy-start(bf16[512,1024]{1,0:T(8,128)(2,1)} %param.9) | copy-start | bytes 3145732
  4.6 32.5 %all-to-all-start = ((bf16[16,32,1152]{2,1,0:T(8,128)(2,1)}), bf16[16,32,1152]{2,1,0:T(8,128)(2,1)S(1)}, u32[]{:S(2)}, u32[]{:S(2)}) async-start(bf16[16,32,1152]{2,1,0:T(8,128)(2,1)} %pad_maximum_fusion.1), calls=%async_computation | async-start | bytes 2359296 | tf_op jit(solution)/shard_map/all_to_all | solution.py:61
  16.0 4.0 %copy-start.4 = (bf16[4,1024]{1,0:T(4,128)(2,1)S(1)}, bf16[4,1024]{1,0:T(4,128)(2,1)}, u32[]{:S(2)}) copy-start(bf16[4,1024]{1,0:T(4,128)(2,1)} %param.12) | copy-start | bytes 24580
  16.0 4.0 %copy-start.5 = (bf16[1024]{0:T(1024)(128)(2,1)S(1)}, bf16[1024]{0:T(1024)(128)(2,1)}, u32[]{:S(2)}) copy-start(bf16[1024]{0:T(1024)(128)(2,1)} %param.13) | copy-start | bytes 6148
  37.6 2.2 %copy-start.1 = (bf16[1024,16,128]{0,2,1:T(8,128)(2,1)S(1)}, bf16[1024,16,128]{0,2,1:T(8,128)(2,1)}, u32[]{:S(2)}) copy-start(bf16[1024,16,128]{0,2,1:T(8,128)(2,1)} %pad_maximum_fusion) | copy-start | bytes 12582916
  42.1 15.5 %all-to-all-start.1 = ((bf16[8,128,256]{2,1,0:T(8,128)(2,1)}), bf16[8,128,256]{2,1,0:T(8,128)(2,1)}, u32[]{:S(2)}, u32[]{:S(2)}) async-start(bf16[8,128,256]{2,1,0:T(8,128)(2,1)} %bitcast.72), calls=%async_computation.1 | async-start | bytes 1048576 | tf_op jit(solution)/shard_map/all_to_all | solution.py:96
  60.9 15.2 %copy-start.3 = (bf16[16,1024]{1,0:T(8,128)(2,1)S(1)}, bf16[16,1024]{1,0:T(8,128)(2,1)}, u32[]{:S(2)}) copy-start(bf16[16,1024]{1,0:T(8,128)(2,1)} %param.11) | copy-start | bytes 98308

commit v8 on v7

--- a/solution.py
+++ b/solution.py
@@ -114,14 +114,20 @@
     ).astype(jnp.bfloat16)
     stats = jnp.transpose(jnp.stack([max_high, max_low, tot_high, tot_low], axis=-1), (1, 0, 2))
     part_payload = jnp.concatenate(
-        [summed.reshape(all_lat, pair_width), stats.reshape(all_lat, heads_dev * 4)], axis=1
-    ).reshape(cycle_size, lat_rows, pair_width + heads_dev * 4)
+        [
+            summed.reshape(cycle_size, lat_rows * pair_width),
+            stats.reshape(cycle_size, lat_rows * heads_dev * 4),
+        ],
+        axis=1,
+    ).reshape(cycle_size, 1, -1)
     got_parts = lax.all_to_all(part_payload, BLK, split_axis=0, concat_axis=0, tiled=True)
-    got_parts = got_parts.astype(jnp.float32).reshape(sides, side_size, lat_rows, -1)
-    part_sums = got_parts[..., :pair_width].reshape(
+    got_parts = got_parts.astype(jnp.float32).reshape(sides, side_size, -1)
+    part_sums = got_parts[..., : lat_rows * pair_width].reshape(
         sides, side_size, lat_rows, heads_dev, head_width
     )
-    part_stats = got_parts[..., pair_width:].reshape(sides, side_size, lat_rows, heads_dev, 4)
+    part_stats = got_parts[..., lat_rows * pair_width :].reshape(
+        sides, side_size, lat_rows, heads_dev, 4
+    )
     part_max = part_stats[..., 0] + part_stats[..., 1]
     part_tot = part_stats[..., 2] + part_stats[..., 3]
     top = jnp.max(part_max, axis=0)

time: 79.4 us -> 80.3 us (1.011)
  local copies, waits for them, and re-layouts: 15.9 us -> 17 us
  blocking collectives: 13.2 us -> 12.2 us
    all_to_all x1, blocking collectives: 13.2 us -> 12.2 us  [local(): lax.all_to_all(part_payload, BLK, split_axis=0, concat_axis=0, tiled=True)]
    reshape x0 -> x3, local copies, waits for them, and re-layouts: none -> 0.88 us  [the longest x1 0.51 us: local(): part_payload = jnp.concatenate([summed.reshape(cycle_size, lat_rows * pai...]
    unnamed x18 -> x21, local copies, waits for them, and re-layouts: 11.1 us -> 11.4 us
where the time goes in v8:
time: 80.3 us; the launch traced here: 79.7 us
  waiting for transfers between devices  21.1 us (26%)
  local copies, waits for them, and re-layouts  17 us (21%)
  starting transfers between devices  14 us (17%)
  blocking collectives  12.2 us (15%)
  other arithmetic  8.17 us (10%)
  matrix products  6.78 us (8%)
    all_to_all x1, waiting for transfers between devices, local(): got = lax.all_to_all(payload, BLK, split_axis=0, concat_axis=0, tiled=True)  12.4 us
    all_to_all x1, blocking collectives, local(): lax.all_to_all(part_payload, BLK, split_axis=0, concat_axis=0, tiled=True)  12.2 us
    unnamed x21, local copies, waits for them, and re-layouts  11.4 us
    all_to_all x1, waiting for transfers between devices, local(): lax.all_to_all(pair_rows, 'rest', split_axis=0, concat_axis=0, tiled=True)  8.75 us
    all_to_all x1, starting transfers between devices, local(): got = lax.all_to_all(payload, BLK, split_axis=0, concat_axis=0, tiled=True)  7.39 us
    all_to_all x1, starting transfers between devices, local(): lax.all_to_all(pair_rows, 'rest', split_axis=0, concat_axis=0, tiled=True)  6.58 us
    concatenate x1, other arithmetic, local(): jnp.concatenate([w_key.reshape(model_width, head_count, head_width), w_va...  4.76 us
    dot_general x1, matrix products, local(): jnp.dot(attended, w_out, preferred_element_type=jnp.float32)  2.6 us
  transfers between devices with their start and end apart: 2, of which 2 were waited for; matrix products, arithmetic and copies ran while one was open for 16% of the time, Pallas kernels for 0%

profile of v8, /device:TPU:0, one launch (start us, length us, event | category | flops | bytes accessed | tf_op | source)
XLA Modules:
  0.0 79.7 jit_solution(11099862500691677117)
XLA Ops:
  0.0 1.6 %copy-done = bf16[1024,1024]{1,0:T(8,128)(2,1)S(1)} copy-done((bf16[1024,1024]{1,0:T(8,128)(2,1)S(1)}, bf16[1024,1024]{1,0:T(8,128)(2,1)}, u32[]{:S(2)}) %copy-start) | copy-done | bytes 2097176
  1.6 1.1 %fusion.7 = bf16[2,8,8,128]{3,1,2,0:T(8,128)(2,1)S(1)} fusion(bf16[16,1024]{1,0:T(8,128)(2,1)} %param.11, bf16[1024,1024]{1,0:T(8,128)(2,1)S(1)} %copy-done), kind=kOutput, calls=%fused_computation.17 | convolution fusion | flops 33587200 | bytes 2162688 | tf_op jit(solution)/shard_map/dot_general | solution.py:39
  2.8 0.1 tile.9
  2.9 0.1 broadcast_in_dim.3
  3.1 0.1 fusion.3
  3.2 0.2 copy.104
  3.4 1.2 %pad_maximum_fusion.1 = bf16[16,32,1152]{2,1,0:T(8,128)(2,1)} fusion(bf16[16,32,64]{2,1,0:T(8,128)(2,1)S(1)} %tile.9, bf16[16,32,1088]{2,1,0:T(8,128)(2,1)S(1)} %bitcast.70), kind=kLoop, calls=%fused_computation.9 | loop fusion | flops 2359296 | bytes 2359296 | tf_op jit(solution)/shard_map/concatenate | solution.py:58
  4.6 7.4 %all-to-all-start = ((bf16[16,32,1152]{2,1,0:T(8,128)(2,1)}), bf16[16,32,1152]{2,1,0:T(8,128)(2,1)S(1)}, u32[]{:S(2)}, u32[]{:S(2)}) async-start(bf16[16,32,1152]{2,1,0:T(8,128)(2,1)} %pad_maximum_fusion.1), calls=%async_computation | async-start | bytes 2359296 | tf_op jit(solution)/shard_map/all_to_all | solution.py:61
  12.0 4.0 %copy.80 = bf16[1024,1024]{0,1:T(8,128)(2,1)} copy(bf16[1024,1024]{1,0:T(8,128)(2,1)} %param.16) | data formatting | bytes 4194304 | tf_op args[7]
  16.0 4.0 %copy.79 = bf16[1024,1024]{0,1:T(8,128)(2,1)} copy(bf16[1024,1024]{1,0:T(8,128)(2,1)} %param.15) | data formatting | bytes 4194304 | tf_op args[6]
  20.0 4.8 %pad_maximum_fusion = bf16[1024,16,128]{0,2,1:T(8,128)(2,1)} fusion(bf16[1024,16,64]{0,2,1:T(8,128)(2,1)} %bitcast.68, bf16[1024,16,64]{0,2,1:T(8,128)(2,1)} %bitcast.69), kind=kLoop, calls=%fused_computation | loop fusion | flops 8388608 | bytes 8388608 | tf_op jit(solution)/shard_map/concatenate | solution.py:81
  24.7 12.4 %all-to-all-done = bf16[16,32,1152]{2,1,0:T(8,128)(2,1)S(1)} async-done(((bf16[16,32,1152]{2,1,0:T(8,128)(2,1)}), bf16[16,32,1152]{2,1,0:T(8,128)(2,1)S(1)}, u32[]{:S(2)}, u32[]{:S(2)}) %all-to-all-start) | async-done | bytes 1179680 | tf_op jit(solution)/shard_map/all_to_all | solution.py:61
  37.2 0.3 convert_reduce_fusion
  37.5 0.1 reshape.146
  37.6 0.1 slice.45
  37.7 0.4 multiply_reduce_fusion
  38.2 0.1 multiply_reduce_fusion.1
  38.3 1.5 %copy-done.1 = bf16[1024,16,128]{0,2,1:T(8,128)(2,1)S(1)} copy-done((bf16[1024,16,128]{0,2,1:T(8,128)(2,1)S(1)}, bf16[1024,16,128]{0,2,1:T(8,128)(2,1)}, u32[]{:S(2)}) %copy-start.1) | copy-done | bytes 4194328
  39.8 1.5 %convolution_convert_fusion = bf16[128,2048]{1,0:T(8,128)(2,1)S(1)} fusion(bf16[1024,2048]{0,1:T(8,128)(2,1)S(1)} %bitcast.67, f32[128,1024]{1,0:T(8,128)S(1)} %multiply_reduce_fusion, f32[1024]{0:T(1024)S(1)} %convert_element_type.148, f32[128]{0:T(128)S(1)} %add_rsqrt_fusion), kind=kOutput, calls=%fused_computation.1 | convolution fusion | flops 537526272 | bytes 5247488 | tf_op jit(solution)/shard_map/dot_general | solution.py:88
  41.3 0.8 %copy.105 = bf16[16,8,8,256]{3,2,0,1:T(8,128)(2,1)} copy(bf16[16,8,8,256]{3,2,1,0:T(8,128)(2,1)S(1)} %bitcast.72) | data formatting | bytes 1048576 | tf_op jit(solution)/shard_map/reshape | solution.py:94
  42.1 6.6 %all-to-all-start.1 = ((bf16[8,128,256]{2,1,0:T(8,128)(2,1)}), bf16[8,128,256]{2,1,0:T(8,128)(2,1)}, u32[]{:S(2)}, u32[]{:S(2)}) async-start(bf16[8,128,256]{2,1,0:T(8,128)(2,1)} %bitcast.73), calls=%async_computation.1 | async-start | bytes 1048576 | tf_op jit(solution)/shard_map/all_to_all | solution.py:96
  48.7 0.1 slice.47
  48.8 0.1 copy.83
  48.9 8.7 %all-to-all-done.1 = bf16[8,128,256]{2,1,0:T(8,128)(2,1)} async-done(((bf16[8,128,256]{2,1,0:T(8,128)(2,1)}), bf16[8,128,256]{2,1,0:T(8,128)(2,1)}, u32[]{:S(2)}, u32[]{:S(2)}) %all-to-all-start.1) | async-done | bytes 524320 | tf_op jit(solution)/shard_map/all_to_all | solution.py:96
  57.7 1.2 %reshape.149 = bf16[1024,2,128]{2,1,0:T(2,128)(2,1)S(1)} reshape(bf16[8,128,256]{2,1,0:T(8,128)(2,1)} %all-to-all-done.1) | data formatting | bytes 1048576 | tf_op jit(solution)/shard_map/reshape | solution.py:98
  58.8 0.4 copy.93
  59.3 0.6 fusion.27
  59.8 0.5 fusion.1
  60.3 0.5 fusion.4
  60.9 0.2 copy.85
  61.1 0.2 reshape.140
  61.3 0.1 copy.84
  61.4 0.2 reshape.139
  61.6 0.5 broadcast.42
  62.1 0.7 reduce.4
  62.8 0.1 reshape.151
  62.9 12.2 %all_to_all.15 = bf16[16,2,1088]{2,1,0:T(2,128)(2,1)S(1)} all-to-all(bf16[16,2,1088]{2,1,0:T(2,128)(2,1)S(1)} %reshape.151), channel_id=1, replica_groups=mesh['grp'=2,'side'=2,'rest'=8] {'side','rest'}, dimensions={0} | all-to-all | bytes 139264 | tf_op jit(solution)/shard_map/all_to_all | solution.py:123
  75.2 0.1 reshape.152
  75.3 0.1 copy.96
  75.5 0.1 fusion.26
  75.7 0.3 copy.88
  75.9 0.3 mul.91
  76.3 0.3 mul.92
  76.6 0.1 reduce_sum.56
  76.7 0.1 fusion.16
  76.9 0.1 copy.92
  76.9 0.1 reshape.145
  77.1 2.6 %fusion.6 = bf16[16,1024]{1,0:T(8,128)(2,1)} fusion(bf16[16,1024]{1,0:T(8,128)(2,1)S(1)} %reshape.145, bf16[1024,1024]{1,0:T(8,128)(2,1)} %param.17, bf16[16,1024]{1,0:T(8,128)(2,1)S(1)} %copy-done.3), kind=kOutput, calls=%fused_computation.16 | convolution fusion | flops 33603584 | bytes 2195456 | tf_op jit(solution)/shard_map/dot_general | solution.py:139
  (28 shorter events, 0.2 us)
Async XLA Ops:
  0.0 1.6 %copy-start = (bf16[1024,1024]{1,0:T(8,128)(2,1)S(1)}, bf16[1024,1024]{1,0:T(8,128)(2,1)}, u32[]{:S(2)}) copy-start(bf16[1024,1024]{1,0:T(8,128)(2,1)} %param.14) | copy-start | bytes 6291460
  0.0 2.9 %copy-start.6 = (s32[512]{0:T(512)S(1)}, s32[512]{0:T(512)}, u32[]{:S(2)}) copy-start(s32[512]{0:T(512)} %param.10) | copy-start | bytes 6148
  0.0 3.0 %copy-start.2 = (bf16[512,1024]{1,0:T(8,128)(2,1)S(1)}, bf16[512,1024]{1,0:T(8,128)(2,1)}, u32[]{:S(2)}) copy-start(bf16[512,1024]{1,0:T(8,128)(2,1)} %param.9) | copy-start | bytes 3145732
  4.6 32.5 %all-to-all-start = ((bf16[16,32,1152]{2,1,0:T(8,128)(2,1)}), bf16[16,32,1152]{2,1,0:T(8,128)(2,1)S(1)}, u32[]{:S(2)}, u32[]{:S(2)}) async-start(bf16[16,32,1152]{2,1,0:T(8,128)(2,1)} %pad_maximum_fusion.1), calls=%async_computation | async-start | bytes 2359296 | tf_op jit(solution)/shard_map/all_to_all | solution.py:61
  16.0 4.0 %copy-start.4 = (bf16[4,1024]{1,0:T(4,128)(2,1)S(1)}, bf16[4,1024]{1,0:T(4,128)(2,1)}, u32[]{:S(2)}) copy-start(bf16[4,1024]{1,0:T(4,128)(2,1)} %param.12) | copy-start | bytes 24580
  16.0 4.0 %copy-start.5 = (bf16[1024]{0:T(1024)(128)(2,1)S(1)}, bf16[1024]{0:T(1024)(128)(2,1)}, u32[]{:S(2)}) copy-start(bf16[1024]{0:T(1024)(128)(2,1)} %param.13) | copy-start | bytes 6148
  37.6 2.2 %copy-start.1 = (bf16[1024,16,128]{0,2,1:T(8,128)(2,1)S(1)}, bf16[1024,16,128]{0,2,1:T(8,128)(2,1)}, u32[]{:S(2)}) copy-start(bf16[1024,16,128]{0,2,1:T(8,128)(2,1)} %pad_maximum_fusion) | copy-start | bytes 12582916
  42.1 15.5 %all-to-all-start.1 = ((bf16[8,128,256]{2,1,0:T(8,128)(2,1)}), bf16[8,128,256]{2,1,0:T(8,128)(2,1)}, u32[]{:S(2)}, u32[]{:S(2)}) async-start(bf16[8,128,256]{2,1,0:T(8,128)(2,1)} %bitcast.73), calls=%async_computation.1 | async-start | bytes 1048576 | tf_op jit(solution)/shard_map/all_to_all | solution.py:96
  60.9 16.1 %copy-start.3 = (bf16[16,1024]{1,0:T(8,128)(2,1)S(1)}, bf16[16,1024]{1,0:T(8,128)(2,1)}, u32[]{:S(2)}) copy-start(bf16[16,1024]{1,0:T(8,128)(2,1)} %param.11) | copy-start | bytes 98308

commit v9 on v7

--- a/solution.py
+++ b/solution.py
@@ -91,12 +91,10 @@
         preferred_element_type=jnp.float32,
     ).astype(jnp.bfloat16)
     pair_rows = jnp.transpose(
-        pair_rows.reshape(patches_dev, side_size, 2 * pair_width), (1, 0, 2)
+        pair_rows.reshape(patches_dev, side_size, heads_dev, 2 * head_width), (1, 2, 0, 3)
     )
-    got_pairs = lax.all_to_all(pair_rows, "rest", split_axis=0, concat_axis=0, tiled=True)
-    got_pairs = jnp.transpose(
-        got_pairs.reshape(side_size * patches_dev, heads_dev, 2 * head_width), (1, 0, 2)
-    )
+    got_pairs = lax.all_to_all(pair_rows, "rest", split_axis=0, concat_axis=2, tiled=True)
+    got_pairs = got_pairs.reshape(heads_dev, side_size * patches_dev, 2 * head_width)
     head_keys = got_pairs[:, :, :head_width]
     head_values = got_pairs[:, :, head_width:]
 

time: 79.4 us -> 87.3 us (1.099)
  local copies, waits for them, and re-layouts: 15.9 us -> 21.4 us
  matrix products: 6.78 us -> 9.19 us
    slice x0 -> x1, local copies, waits for them, and re-layouts: none -> 2.14 us  [local(): head_values = got_pairs[:, :, head_width:]]
    reshape x3 -> x2, local copies, waits for them, and re-layouts: 2.43 us -> 4.4 us  [local(): pair_rows.reshape(patches_dev, side_size, heads_dev, 2 * head_width)]
    dot_general x1, matrix products: 0.53 us -> 2.11 us  [local(): jnp.einsum('hlk,hkd->lhd', weights.astype(jnp.bfloat16), head_values, pre...]
    unnamed x18 -> x20, local copies, waits for them, and re-layouts: 11.1 us -> 12.5 us
  transfers between devices with their start and end apart: 2 -> 2, of which waited for: 2 -> 2; matrix products, arithmetic and copies ran while one was open for 16% -> 15% of each run, Pallas kernels for 0% -> 0%
where the time goes in v9:
time: 87.3 us; the launch traced here: 86.6 us
  local copies, waits for them, and re-layouts  21.4 us (25%)
  waiting for transfers between devices  21.1 us (24%)
  starting transfers between devices  14 us (16%)
  blocking collectives  13.2 us (15%)
  matrix products  9.19 us (11%)
  other arithmetic  7.43 us (9%)
    all_to_all x1, blocking collectives, local(): lax.all_to_all(part_payload, BLK, split_axis=0, concat_axis=0, tiled=True)  13.2 us
    unnamed x20, local copies, waits for them, and re-layouts  12.5 us
    all_to_all x1, waiting for transfers between devices, local(): got = lax.all_to_all(payload, BLK, split_axis=0, concat_axis=0, tiled=True)  12.4 us
    all_to_all x1, waiting for transfers between devices, local(): lax.all_to_all(pair_rows, 'rest', split_axis=0, concat_axis=2, tiled=True)  8.75 us
    all_to_all x1, starting transfers between devices, local(): got = lax.all_to_all(payload, BLK, split_axis=0, concat_axis=0, tiled=True)  7.39 us
    all_to_all x1, starting transfers between devices, local(): lax.all_to_all(pair_rows, 'rest', split_axis=0, concat_axis=2, tiled=True)  6.58 us
    concatenate x1, other arithmetic, local(): jnp.concatenate([w_key.reshape(model_width, head_count, head_width), w_va...  4.76 us
    reshape x2, local copies, waits for them, and re-layouts, local(): pair_rows.reshape(patches_dev, side_size, heads_dev, 2 * head_width)  4.4 us
  transfers between devices with their start and end apart: 2, of which 2 were waited for; matrix products, arithmetic and copies ran while one was open for 15% of the time, Pallas kernels for 0%

profile of v9, /device:TPU:0, one launch (start us, length us, event | category | flops | bytes accessed | tf_op | source)
XLA Modules:
  0.0 86.6 jit_solution(8680234325976144197)
XLA Ops:
  0.0 0.0 copy-start
  0.0 1.6 %copy-done = bf16[1024,1024]{1,0:T(8,128)(2,1)S(1)} copy-done((bf16[1024,1024]{1,0:T(8,128)(2,1)S(1)}, bf16[1024,1024]{1,0:T(8,128)(2,1)}, u32[]{:S(2)}) %copy-start) | copy-done | bytes 2097176
  1.6 1.1 %fusion.7 = bf16[2,8,8,128]{3,1,2,0:T(8,128)(2,1)S(1)} fusion(bf16[16,1024]{1,0:T(8,128)(2,1)} %param.11, bf16[1024,1024]{1,0:T(8,128)(2,1)S(1)} %copy-done), kind=kOutput, calls=%fused_computation.17 | convolution fusion | flops 33587200 | bytes 2162688 | tf_op jit(solution)/shard_map/dot_general | solution.py:39
  2.8 0.1 tile.9
  2.9 0.0 copy-done.7
  2.9 0.1 broadcast_in_dim.3
  3.1 0.1 fusion.3
  3.2 0.2 copy.82
  3.4 1.2 %pad_maximum_fusion.1 = bf16[16,32,1152]{2,1,0:T(8,128)(2,1)} fusion(bf16[16,32,64]{2,1,0:T(8,128)(2,1)S(1)} %tile.9, bf16[16,32,1088]{2,1,0:T(8,128)(2,1)S(1)} %bitcast.69), kind=kLoop, calls=%fused_computation.9 | loop fusion | flops 2359296 | bytes 2359296 | tf_op jit(solution)/shard_map/concatenate | solution.py:58
  4.6 7.4 %all-to-all-start = ((bf16[16,32,1152]{2,1,0:T(8,128)(2,1)}), bf16[16,32,1152]{2,1,0:T(8,128)(2,1)S(1)}, u32[]{:S(2)}, u32[]{:S(2)}) async-start(bf16[16,32,1152]{2,1,0:T(8,128)(2,1)} %pad_maximum_fusion.1), calls=%async_computation | async-start | bytes 2359296 | tf_op jit(solution)/shard_map/all_to_all | solution.py:61
  12.0 4.0 %copy.55 = bf16[1024,1024]{0,1:T(8,128)(2,1)} copy(bf16[1024,1024]{1,0:T(8,128)(2,1)} %param.16) | data formatting | bytes 4194304 | tf_op args[7]
  16.0 4.0 %copy.54 = bf16[1024,1024]{0,1:T(8,128)(2,1)} copy(bf16[1024,1024]{1,0:T(8,128)(2,1)} %param.15) | data formatting | bytes 4194304 | tf_op args[6]
  20.0 0.0 copy-done.5
  20.0 4.8 %pad_maximum_fusion = bf16[1024,16,128]{0,2,1:T(8,128)(2,1)} fusion(bf16[1024,16,64]{0,2,1:T(8,128)(2,1)} %bitcast.67, bf16[1024,16,64]{0,2,1:T(8,128)(2,1)} %bitcast.68), kind=kLoop, calls=%fused_computation | loop fusion | flops 8388608 | bytes 8388608 | tf_op jit(solution)/shard_map/concatenate | solution.py:81
  24.7 12.4 %all-to-all-done = bf16[16,32,1152]{2,1,0:T(8,128)(2,1)S(1)} async-done(((bf16[16,32,1152]{2,1,0:T(8,128)(2,1)}), bf16[16,32,1152]{2,1,0:T(8,128)(2,1)S(1)}, u32[]{:S(2)}, u32[]{:S(2)}) %all-to-all-start) | async-done | bytes 1179680 | tf_op jit(solution)/shard_map/all_to_all | solution.py:61
  37.2 0.3 convert_reduce_fusion
  37.5 0.1 reshape.142
  37.6 0.1 slice.45
  37.7 0.4 multiply_reduce_fusion
  38.2 0.1 multiply_reduce_fusion.1
  38.3 1.5 %copy-done.2 = bf16[1024,16,128]{0,2,1:T(8,128)(2,1)S(1)} copy-done((bf16[1024,16,128]{0,2,1:T(8,128)(2,1)S(1)}, bf16[1024,16,128]{0,2,1:T(8,128)(2,1)}, u32[]{:S(2)}) %copy-start.2) | copy-done | bytes 4194328
  39.8 2.3 %convolution_convert_fusion = bf16[128,2048]{1,0:T(8,128)(2,1)} fusion(bf16[1024,2048]{0,1:T(8,128)(2,1)S(1)} %bitcast.66, f32[128,1024]{1,0:T(8,128)S(1)} %multiply_reduce_fusion, f32[1024]{0:T(1024)S(1)} %convert_element_type.148, f32[128]{0:T(128)S(1)} %add_rsqrt_fusion), kind=kOutput, calls=%fused_computation.1 | convolution fusion | flops 537526272 | bytes 5247488 | tf_op jit(solution)/shard_map/dot_general | solution.py:88
  42.1 2.2 %reshape.135 = bf16[128,8,2,128]{3,2,1,0:T(2,128)(2,1)} reshape(bf16[128,2048]{1,0:T(8,128)(2,1)} %convolution_convert_fusion) | data formatting | bytes 1048576 | tf_op jit(solution)/shard_map/reshape | solution.py:94
  44.3 2.2 %copy.83 = bf16[128,8,2,128]{3,2,0,1:T(2,128)(2,1)} copy(bf16[128,8,2,128]{3,2,1,0:T(2,128)(2,1)} %reshape.135) | data formatting | bytes 1048576 | tf_op jit(solution)/shard_map/reshape | solution.py:94
  46.5 6.6 %all-to-all-start.1 = ((bf16[8,2,128,128]{3,1,2,0:T(2,128)(2,1)}), bf16[8,2,128,128]{3,1,2,0:T(2,128)(2,1)}, u32[]{:S(2)}, u32[]{:S(2)}) async-start(bf16[8,2,128,128]{3,1,2,0:T(2,128)(2,1)} %bitcast.71), calls=%async_computation.1 | async-start | bytes 1048576 | tf_op jit(solution)/shard_map/all_to_all | solution.py:96
  53.1 0.1 slice.47
  53.2 0.1 copy.58
  53.3 8.7 %all-to-all-done.1 = bf16[8,2,128,128]{3,1,2,0:T(2,128)(2,1)} async-done(((bf16[8,2,128,128]{3,1,2,0:T(2,128)(2,1)}), bf16[8,2,128,128]{3,1,2,0:T(2,128)(2,1)}, u32[]{:S(2)}, u32[]{:S(2)}) %all-to-all-start.1) | async-done | bytes 524320 | tf_op jit(solution)/shard_map/all_to_all | solution.py:96
  62.0 2.1 %fusion.30 = (bf16[2,1024,64]{2,0,1:T(2,128)(2,1)S(1)}, bf16[2,1024,64]{2,0,1:T(2,128)(2,1)S(1)}) fusion(bf16[2,1024,128]{2,0,1:T(2,128)(2,1)} %bitcast.10), kind=kLoop, calls=%fused_computation.63 | loop fusion | bytes 1048576 | tf_op jit(solution)/shard_map/slice | solution.py:99
  64.2 0.6 fusion.31
  64.8 1.3 %copy-done.1 = f32[2,256,1024]{2,1,0:T(8,128)} copy-done((f32[2,256,1024]{2,1,0:T(8,128)}, f32[2,256,1024]{2,1,0:T(8,128)S(1)}, u32[]{:S(2)}) %copy-start.1) | copy-done | bytes 2097176
  66.1 0.5 fusion.1
  66.7 0.1 concatenate.21
  66.8 0.1 copy.60
  66.9 2.1 %fusion.4 = bf16[256,2,64]{0,2,1:T(8,128)(2,1)S(1)} fusion(f32[2,256,1024]{2,1,0:T(8,128)} %copy-done.1, f32[2,256]{1,0:T(2,128)S(1)} %convert_add_fusion, bf16[2,1024,64]{2,0,1:T(2,128)(2,1)S(1)} %get-tuple-element.5), kind=kOutput, calls=%fused_computation.12 | convolution fusion | flops 68190208 | bytes 2426880 | tf_op jit(solution)/shard_map/hlk,hkd->lhd/dot_general | solution.py:110
  69.0 0.0 copy-start.4
  69.0 0.1 copy.59
  69.1 0.1 concatenate.20
  69.3 13.2 %all_to_all.25 = bf16[16,16,136]{2,1,0:T(8,128)(2,1)S(1)} all-to-all(bf16[16,16,136]{2,1,0:T(8,128)(2,1)S(1)} %pad_maximum_fusion.2), channel_id=1, replica_groups=mesh['grp'=2,'side'=2,'rest'=8] {'side','rest'}, dimensions={0} | all-to-all | bytes 139264 | tf_op jit(solution)/shard_map/all_to_all | solution.py:117
  82.5 0.1 copy.68
  82.7 0.2 copy.62
  82.8 0.3 mul.91
  83.2 0.2 mul.92
  83.4 0.1 reduce_sum.56
  83.5 0.1 copy.64
  83.7 0.2 fusion.17
  83.9 0.1 reshape.141
  84.0 2.6 %fusion.6 = bf16[16,1024]{1,0:T(8,128)(2,1)} fusion(bf16[16,1024]{1,0:T(8,128)(2,1)S(1)} %reshape.141, bf16[1024,1024]{1,0:T(8,128)(2,1)} %param.17, bf16[16,1024]{1,0:T(8,128)(2,1)S(1)} %copy-done.4), kind=kOutput, calls=%fused_computation.16 | convolution fusion | flops 33603584 | bytes 2195456 | tf_op jit(solution)/shard_map/dot_general | solution.py:131
  (28 shorter events, 0.2 us)
Async XLA Ops:
  0.0 1.6 %copy-start = (bf16[1024,1024]{1,0:T(8,128)(2,1)S(1)}, bf16[1024,1024]{1,0:T(8,128)(2,1)}, u32[]{:S(2)}) copy-start(bf16[1024,1024]{1,0:T(8,128)(2,1)} %param.14) | copy-start | bytes 6291460
  0.0 2.9 %copy-start.7 = (s32[512]{0:T(512)S(1)}, s32[512]{0:T(512)}, u32[]{:S(2)}) copy-start(s32[512]{0:T(512)} %param.10) | copy-start | bytes 6148
  0.0 3.0 %copy-start.3 = (bf16[512,1024]{1,0:T(8,128)(2,1)S(1)}, bf16[512,1024]{1,0:T(8,128)(2,1)}, u32[]{:S(2)}) copy-start(bf16[512,1024]{1,0:T(8,128)(2,1)} %param.9) | copy-start | bytes 3145732
  4.6 32.5 %all-to-all-start = ((bf16[16,32,1152]{2,1,0:T(8,128)(2,1)}), bf16[16,32,1152]{2,1,0:T(8,128)(2,1)S(1)}, u32[]{:S(2)}, u32[]{:S(2)}) async-start(bf16[16,32,1152]{2,1,0:T(8,128)(2,1)} %pad_maximum_fusion.1), calls=%async_computation | async-start | bytes 2359296 | tf_op jit(solution)/shard_map/all_to_all | solution.py:61
  16.0 4.0 %copy-start.5 = (bf16[4,1024]{1,0:T(4,128)(2,1)S(1)}, bf16[4,1024]{1,0:T(4,128)(2,1)}, u32[]{:S(2)}) copy-start(bf16[4,1024]{1,0:T(4,128)(2,1)} %param.12) | copy-start | bytes 24580
  16.0 4.0 %copy-start.6 = (bf16[1024]{0:T(1024)(128)(2,1)S(1)}, bf16[1024]{0:T(1024)(128)(2,1)}, u32[]{:S(2)}) copy-start(bf16[1024]{0:T(1024)(128)(2,1)} %param.13) | copy-start | bytes 6148
  37.6 2.2 %copy-start.2 = (bf16[1024,16,128]{0,2,1:T(8,128)(2,1)S(1)}, bf16[1024,16,128]{0,2,1:T(8,128)(2,1)}, u32[]{:S(2)}) copy-start(bf16[1024,16,128]{0,2,1:T(8,128)(2,1)} %pad_maximum_fusion) | copy-start | bytes 12582916
  46.5 15.5 %all-to-all-start.1 = ((bf16[8,2,128,128]{3,1,2,0:T(2,128)(2,1)}), bf16[8,2,128,128]{3,1,2,0:T(2,128)(2,1)}, u32[]{:S(2)}, u32[]{:S(2)}) async-start(bf16[8,2,128,128]{3,1,2,0:T(2,128)(2,1)} %bitcast.71), calls=%async_computation.1 | async-start | bytes 1048576 | tf_op jit(solution)/shard_map/all_to_all | solution.py:96
  64.7 1.4 %copy-start.1 = (f32[2,256,1024]{2,1,0:T(8,128)}, f32[2,256,1024]{2,1,0:T(8,128)S(1)}, u32[]{:S(2)}) copy-start(f32[2,256,1024]{2,1,0:T(8,128)S(1)} %get-tuple-element.8) | copy-start | bytes 6291460
  69.0 15.0 %copy-start.4 = (bf16[16,1024]{1,0:T(8,128)(2,1)S(1)}, bf16[16,1024]{1,0:T(8,128)(2,1)}, u32[]{:S(2)}) copy-start(bf16[16,1024]{1,0:T(8,128)(2,1)} %param.11) | copy-start | bytes 98308

commit v10 on v6

--- a/solution.py
+++ b/solution.py
@@ -5,6 +5,11 @@
 
 HEADS = 16
 CONTRASTS = 4
+
+
+def shifted(block, axis, distance):
+    size = lax.axis_size(axis)
+    return lax.ppermute(block, axis, [(i, (i + distance) % size) for i in range(size)])
 
 
 def local(tokens, patch_of_row, latents, contrast_gain, norm_gain, w_query, w_key, w_value, w_out):
@@ -62,10 +67,20 @@
     query_parts = query_parts.reshape(head_count, -1, 2 * head_width)
     query_len = query_parts.shape[1]
     pair_payload = jnp.tile(jnp.concatenate([pair_rows, query_parts], axis=1), (copies, 1, 1))
-    got_pairs = lax.all_to_all(pair_payload, "blk", split_axis=0, concat_axis=0, tiled=True)
-    head_queries = lax.dynamic_slice_in_dim(
-        got_pairs[:, patches_dev:], group_start, head_count, axis=0
-    ).reshape(head_count * lat_rows, head_width)
+    if copies == 1:
+        blocks = [pair_payload[my_index]]
+        for step in range(1, cycle_size):
+            sent = lax.dynamic_index_in_dim(
+                pair_payload, (my_index + step) % cycle_size, axis=0, keepdims=False
+            )
+            blocks.append(shifted(sent, "blk", step))
+        got_pairs = jnp.stack(blocks)
+        head_queries = got_pairs[:, patches_dev:].reshape(head_count * lat_rows, head_width)
+    else:
+        got_pairs = lax.all_to_all(pair_payload, "blk", split_axis=0, concat_axis=0, tiled=True)
+        head_queries = lax.dynamic_slice_in_dim(
+            got_pairs[:, patches_dev:], group_start, head_count, axis=0
+        ).reshape(head_count * lat_rows, head_width)
     got_pairs = got_pairs[:, :patches_dev].reshape(cycle_size * patches_dev, 2 * head_width)
     head_keys = got_pairs[:, :head_width]
     head_values = got_pairs[:, head_width:]
@@ -78,6 +93,8 @@
     totals = jnp.sum(weights, axis=-1, keepdims=True)
     summed = jnp.dot(weights.astype(jnp.bfloat16), head_values, preferred_element_type=jnp.float32)
     attended_head = (summed / totals).astype(jnp.bfloat16).reshape(head_count, lat_rows, head_width)
+    if copies == 1:
+        attended_head = jnp.take(attended_head, (my_index - lax.broadcasted_iota(jnp.int32, (cycle_size,), 0)) % cycle_size, axis=0)
     got_attended = lax.all_to_all(
         jnp.tile(attended_head, (copies, 1, 1)), "blk", split_axis=0, concat_axis=0, tiled=True
     )

time: 79.2 us -> 86.9 us (1.097)
  starting transfers between devices: 7.39 us -> 33.8 us
  blocking collectives: 33.4 us -> 12.3 us
  waiting for transfers between devices: 11.7 us -> 12.9 us
    ppermute x0 -> x15, starting transfers between devices: none -> 26.4 us  [shifted(): lax.ppermute(block, axis, [(i, (i + distance) % size) for i in range(size)])]
    all_to_all x1 -> x0, blocking collectives: 24 us -> none  [local(): lax.all_to_all(pair_payload, 'blk', split_axis=0, concat_axis=0, tiled=True)]
    all_to_all x1, blocking collectives: 9.36 us -> 12.3 us  [local(): lax.all_to_all(jnp.tile(attended_head, (copies, 1, 1)), 'blk', split_axis...]
    ppermute x0 -> x15, waiting for transfers between devices: none -> 1.54 us  [shifted(): lax.ppermute(block, axis, [(i, (i + distance) % size) for i in range(size)])]
    unnamed x14 -> x28, local copies, waits for them, and re-layouts: 9.65 us -> 9.8 us
  transfers between devices with their start and end apart: 1 -> 16, of which waited for: 1 -> 2; matrix products, arithmetic and copies ran while one was open for 17% -> 16% of each run, Pallas kernels for 0% -> 0%
where the time goes in v10:
time: 86.9 us; the launch traced here: 86.5 us
  starting transfers between devices  33.8 us (39%)
  waiting for transfers between devices  12.9 us (15%)
  local copies, waits for them, and re-layouts  12.8 us (15%)
  blocking collectives  12.3 us (14%)
  other arithmetic  8.05 us (9%)
  matrix products  6.16 us (7%)
    ppermute x15, starting transfers between devices, shifted(): lax.ppermute(block, axis, [(i, (i + distance) % size) for i in range(size)])  26.4 us
    all_to_all x1, blocking collectives, local(): lax.all_to_all(jnp.tile(attended_head, (copies, 1, 1)), 'blk', split_axis...  12.3 us
    all_to_all x1, waiting for transfers between devices, local(): lax.all_to_all(payload, 'blk', split_axis=0, concat_axis=0, tiled=True)  11.4 us
    unnamed x28, local copies, waits for them, and re-layouts  9.8 us
    all_to_all x1, starting transfers between devices, local(): lax.all_to_all(payload, 'blk', split_axis=0, concat_axis=0, tiled=True)  7.39 us
    concatenate x1, other arithmetic, local(): jnp.concatenate([w_key.reshape(model_width, head_count, head_width), w_va...  4.78 us
    dot_general x1, matrix products, local(): jnp.dot(attended, w_out, preferred_element_type=jnp.float32)  2.6 us
  transfers between devices with their start and end apart: 16, of which 2 were waited for; matrix products, arithmetic and copies ran while one was open for 16% of the time, Pallas kernels for 0%

profile of v10, /device:TPU:0, one launch (start us, length us, event | category | flops | bytes accessed | tf_op | source)
XLA Modules:
  0.0 86.5 jit_solution(7752378049112809497)
XLA Ops:
  0.0 0.8 fusion.50
  0.8 0.1 broadcast_in_dim.21
  1.0 1.3 %fusion.4 = bf16[512,1152]{1,0:T(8,128)(2,1)S(1)} fusion(bf16[512,1]{1,0:T(8,128)(2,1)S(1)} %broadcast_in_dim.21, bf16[512,1024]{1,0:T(8,128)(2,1)} %param.9), kind=kLoop, calls=%fused_computation.26 | loop fusion | flops 3538944 | bytes 2229248 | tf_op jit(solution)/shard_map/concatenate | solution.py:35
  2.3 1.3 %copy.36 = bf16[16,32,1152]{2,1,0:T(8,128)(2,1)} copy(bf16[16,32,1152]{2,0,1:T(8,128)(2,1)S(1)} %bitcast.97) | data formatting | bytes 2359296 | tf_op jit(solution)/shard_map/transpose | solution.py:34
  3.6 7.4 %all-to-all-start = ((bf16[16,32,1152]{2,1,0:T(8,128)(2,1)}), bf16[16,32,1152]{2,1,0:T(8,128)(2,1)S(1)}, u32[]{:S(2)}, u32[]{:S(2)}) async-start(bf16[16,32,1152]{2,1,0:T(8,128)(2,1)} %copy.36), calls=%async_computation | async-start | bytes 2359296 | tf_op jit(solution)/shard_map/all_to_all | solution.py:40
  11.2 0.4 fusion.5
  11.6 0.1 reshape.116
  11.8 0.1 reshape.117
  11.9 3.9 %copy.38 = bf16[1024,1024]{0,1:T(8,128)(2,1)} copy(bf16[1024,1024]{1,0:T(8,128)(2,1)} %param.16) | data formatting | bytes 4194304 | tf_op args[7]
  15.8 4.0 %copy.37 = bf16[1024,1024]{0,1:T(8,128)(2,1)} copy(bf16[1024,1024]{1,0:T(8,128)(2,1)} %param.15) | data formatting | bytes 4194304 | tf_op args[6]
  20.0 4.8 %pad_maximum_fusion = bf16[1024,16,128]{0,2,1:T(8,128)(2,1)} fusion(bf16[1024,16,64]{0,2,1:T(8,128)(2,1)} %bitcast.95, bf16[1024,16,64]{0,2,1:T(8,128)(2,1)} %bitcast.96), kind=kLoop, calls=%fused_computation.1 | loop fusion | flops 8388608 | bytes 8388608 | tf_op jit(solution)/shard_map/concatenate | solution.py:53
  24.8 11.4 %all-to-all-done = bf16[16,32,1152]{2,1,0:T(8,128)(2,1)S(1)} async-done(((bf16[16,32,1152]{2,1,0:T(8,128)(2,1)}), bf16[16,32,1152]{2,1,0:T(8,128)(2,1)S(1)}, u32[]{:S(2)}, u32[]{:S(2)}) %all-to-all-start) | async-done | bytes 1179680 | tf_op jit(solution)/shard_map/all_to_all | solution.py:40
  36.2 0.3 convert_reduce_fusion
  36.5 0.1 reshape.122
  36.6 0.1 slice.27
  36.7 0.4 multiply_reduce_fusion
  37.2 0.1 multiply_reduce_fusion.1
  37.3 1.5 %copy-done.1 = bf16[1024,16,128]{0,2,1:T(8,128)(2,1)S(1)} copy-done((bf16[1024,16,128]{0,2,1:T(8,128)(2,1)S(1)}, bf16[1024,16,128]{0,2,1:T(8,128)(2,1)}, u32[]{:S(2)}) %copy-start.1) | copy-done | bytes 4194328
  38.8 1.5 %fusion.3 = bf16[16,16,8,128]{3,2,1,0:T(8,128)(2,1)S(1)} fusion(bf16[1024,2048]{0,1:T(8,128)(2,1)S(1)} %bitcast.90, f32[128,1024]{1,0:T(8,128)S(1)} %multiply_reduce_fusion, f32[1024]{0:T(1024)S(1)} %convert_element_type.48, f32[128]{0:T(128)S(1)} %add_rsqrt_fusion), kind=kOutput, calls=%fused_computation.25 | convolution fusion | flops 537526272 | bytes 5247488 | tf_op jit(solution)/shard_map/dot_general | solution.py:60
  40.3 0.1 copy.47
  40.5 0.8 collective-permute-start
  41.3 2.1 %collective-permute-start.1 = (bf16[136,128]{1,0:T(8,128)(2,1)S(1)}, bf16[136,128]{1,0:T(8,128)(2,1)S(1)}, u32[]{:S(2)}, u32[]{:S(2)}) collective-permute-start(bf16[136,128]{1,0:T(8,128)(2,1)S(1)} %get-tuple-element.8), channel_id=1, source_target_pairs={{0,2},{1,3},{2,4},{3,5},{4,6},{5,7},{6,8},{7,9},{8,10},{9,11},{10,... | collective-permute-start | bytes 104456 | tf_op jit(solution)/shard_map/ppermute | solution.py:12
  43.4 3.9 %collective-permute-start.2 = (bf16[136,128]{1,0:T(8,128)(2,1)S(1)}, bf16[136,128]{1,0:T(8,128)(2,1)S(1)}, u32[]{:S(2)}, u32[]{:S(2)}) collective-permute-start(bf16[136,128]{1,0:T(8,128)(2,1)S(1)} %get-tuple-element.10), channel_id=1, source_target_pairs={{0,3},{1,4},{2,5},{3,6},{4,7},{5,8},{6,9},{7,10},{8,11},{9,12},{10... | collective-permute-start | bytes 104456 | tf_op jit(solution)/shard_map/ppermute | solution.py:12
  47.4 0.7 collective-permute-start.3
  48.0 0.1 collective-permute-start.4
  48.2 2.3 %collective-permute-start.5 = (bf16[136,128]{1,0:T(8,128)(2,1)S(1)}, bf16[136,128]{1,0:T(8,128)(2,1)S(1)}, u32[]{:S(2)}, u32[]{:S(2)}) collective-permute-start(bf16[136,128]{1,0:T(8,128)(2,1)S(1)} %get-tuple-element.14), channel_id=1, source_target_pairs={{0,6},{1,7},{2,8},{3,9},{4,10},{5,11},{6,12},{7,13},{8,14},{9,15},... | collective-permute-start | bytes 104456 | tf_op jit(solution)/shard_map/ppermute | solution.py:12
  50.5 3.0 %collective-permute-start.6 = (bf16[136,128]{1,0:T(8,128)(2,1)S(1)}, bf16[136,128]{1,0:T(8,128)(2,1)S(1)}, u32[]{:S(2)}, u32[]{:S(2)}) collective-permute-start(bf16[136,128]{1,0:T(8,128)(2,1)S(1)} %get-tuple-element.15), channel_id=1, source_target_pairs={{0,7},{1,8},{2,9},{3,10},{4,11},{5,12},{6,13},{7,14},{8,15},{9,0},... | collective-permute-start | bytes 104456 | tf_op jit(solution)/shard_map/ppermute | solution.py:12
  53.6 1.0 %collective-permute-start.7 = (bf16[136,128]{1,0:T(8,128)(2,1)S(1)}, bf16[136,128]{1,0:T(8,128)(2,1)S(1)}, u32[]{:S(2)}, u32[]{:S(2)}) collective-permute-start(bf16[136,128]{1,0:T(8,128)(2,1)S(1)} %get-tuple-element.16), channel_id=1, source_target_pairs={{0,8},{1,9},{2,10},{3,11},{4,12},{5,13},{6,14},{7,15},{8,0},{9,1},... | collective-permute-start | bytes 104456 | tf_op jit(solution)/shard_map/ppermute | solution.py:12
  54.6 1.1 %collective-permute-start.8 = (bf16[136,128]{1,0:T(8,128)(2,1)S(1)}, bf16[136,128]{1,0:T(8,128)(2,1)S(1)}, u32[]{:S(2)}, u32[]{:S(2)}) collective-permute-start(bf16[136,128]{1,0:T(8,128)(2,1)S(1)} %get-tuple-element.18), channel_id=1, source_target_pairs={{0,9},{1,10},{2,11},{3,12},{4,13},{5,14},{6,15},{7,0},{8,1},{9,2},... | collective-permute-start | bytes 104456 | tf_op jit(solution)/shard_map/ppermute | solution.py:12
  55.7 1.4 %collective-permute-start.9 = (bf16[136,128]{1,0:T(8,128)(2,1)S(1)}, bf16[136,128]{1,0:T(8,128)(2,1)S(1)}, u32[]{:S(2)}, u32[]{:S(2)}) collective-permute-start(bf16[136,128]{1,0:T(8,128)(2,1)S(1)} %get-tuple-element.19), channel_id=1, source_target_pairs={{0,10},{1,11},{2,12},{3,13},{4,14},{5,15},{6,0},{7,1},{8,2},{9,3},... | collective-permute-start | bytes 104456 | tf_op jit(solution)/shard_map/ppermute | solution.py:12
  57.2 3.1 %collective-permute-start.10 = (bf16[136,128]{1,0:T(8,128)(2,1)S(1)}, bf16[136,128]{1,0:T(8,128)(2,1)S(1)}, u32[]{:S(2)}, u32[]{:S(2)}) collective-permute-start(bf16[136,128]{1,0:T(8,128)(2,1)S(1)} %get-tuple-element.20), channel_id=1, source_target_pairs={{0,11},{1,12},{2,13},{3,14},{4,15},{5,0},{6,1},{7,2},{8,3},{9,4},{... | collective-permute-start | bytes 104456 | tf_op jit(solution)/shard_map/ppermute | solution.py:12
  60.3 1.5 %collective-permute-start.11 = (bf16[136,128]{1,0:T(8,128)(2,1)S(1)}, bf16[136,128]{1,0:T(8,128)(2,1)S(1)}, u32[]{:S(2)}, u32[]{:S(2)}) collective-permute-start(bf16[136,128]{1,0:T(8,128)(2,1)S(1)} %get-tuple-element.17), channel_id=1, source_target_pairs={{0,12},{1,13},{2,14},{3,15},{4,0},{5,1},{6,2},{7,3},{8,4},{9,5},{1... | collective-permute-start | bytes 104456 | tf_op jit(solution)/shard_map/ppermute | solution.py:12
  61.8 0.4 collective-permute-start.12
  62.3 1.3 %collective-permute-start.13 = (bf16[136,128]{1,0:T(8,128)(2,1)S(1)}, bf16[136,128]{1,0:T(8,128)(2,1)S(1)}, u32[]{:S(2)}, u32[]{:S(2)}) collective-permute-start(bf16[136,128]{1,0:T(8,128)(2,1)S(1)} %get-tuple-element.9), channel_id=1, source_target_pairs={{0,14},{1,15},{2,0},{3,1},{4,2},{5,3},{6,4},{7,5},{8,6},{9,7},{10,... | collective-permute-start | bytes 104456 | tf_op jit(solution)/shard_map/ppermute | solution.py:12
  63.6 3.5 %collective-permute-start.14 = (bf16[136,128]{1,0:T(8,128)(2,1)S(1)}, bf16[136,128]{1,0:T(8,128)(2,1)S(1)}, u32[]{:S(2)}, u32[]{:S(2)}) collective-permute-start(bf16[136,128]{1,0:T(8,128)(2,1)S(1)} %get-tuple-element.5), channel_id=1, source_target_pairs={{0,15},{1,0},{2,1},{3,2},{4,3},{5,4},{6,5},{7,6},{8,7},{9,8},{10,9... | collective-permute-start | bytes 104456 | tf_op jit(solution)/shard_map/ppermute | solution.py:12
  67.1 1.5 %collective-permute-done.14 = bf16[136,128]{1,0:T(8,128)(2,1)S(1)} collective-permute-done((bf16[136,128]{1,0:T(8,128)(2,1)S(1)}, bf16[136,128]{1,0:T(8,128)(2,1)S(1)}, u32[]{:S(2)}, u32[]{:S(2)}) %collective-permute-start.14) | collective-permute-done | bytes 34848 | tf_op jit(solution)/shard_map/ppermute | solution.py:12
  68.7 0.1 reshape.118
  68.8 0.5 fusion.57
  69.3 0.4 fusion.1
  69.8 0.7 fusion.6
  70.5 0.1 copy.41
  70.6 0.6 gather_fusion
  71.2 0.1 broadcast_select_fusion
  71.3 0.1 reshape.132
  71.4 12.3 %all_to_all.10 = bf16[16,2,512]{2,1,0:T(2,128)(2,1)S(1)} all-to-all(bf16[16,2,512]{2,1,0:T(2,128)(2,1)S(1)} %reshape.132), channel_id=1, replica_groups=mesh['grp'=2,'blk'=16] {'blk'}, dimensions={0} | all-to-all | bytes 65536 | tf_op jit(solution)/shard_map/all_to_all | solution.py:98
  83.6 0.1 reshape.133
  83.8 0.1 reshape.121
  83.9 2.6 %fusion.7 = bf16[16,1024]{1,0:T(8,128)(2,1)} fusion(bf16[16,1024]{1,0:T(8,128)(2,1)S(1)} %reshape.121, bf16[1024,1024]{1,0:T(8,128)(2,1)} %param.17, bf16[16,1024]{1,0:T(8,128)(2,1)S(1)} %copy-done.2), kind=kOutput, calls=%fused_computation.32 | convolution fusion | flops 33603584 | bytes 2195456 | tf_op jit(solution)/shard_map/dot_general | solution.py:104
  (52 shorter events, 0.4 us)
Async XLA Ops:
  0.0 11.2 %copy-start = (bf16[1024,1024]{1,0:T(8,128)(2,1)S(1)}, bf16[1024,1024]{1,0:T(8,128)(2,1)}, u32[]{:S(2)}) copy-start(bf16[1024,1024]{1,0:T(8,128)(2,1)} %param.14) | copy-start | bytes 6291460
  2.3 8.9 %copy-start.2 = (bf16[16,1024]{1,0:T(8,128)(2,1)S(1)}, bf16[16,1024]{1,0:T(8,128)(2,1)}, u32[]{:S(2)}) copy-start(bf16[16,1024]{1,0:T(8,128)(2,1)} %param.11) | copy-start | bytes 98308
  3.6 32.5 %all-to-all-start = ((bf16[16,32,1152]{2,1,0:T(8,128)(2,1)}), bf16[16,32,1152]{2,1,0:T(8,128)(2,1)S(1)}, u32[]{:S(2)}, u32[]{:S(2)}) async-start(bf16[16,32,1152]{2,1,0:T(8,128)(2,1)} %copy.36), calls=%async_computation | async-start | bytes 2359296 | tf_op jit(solution)/shard_map/all_to_all | solution.py:40
  15.8 4.0 %copy-start.3 = (bf16[4,1024]{1,0:T(4,128)(2,1)S(1)}, bf16[4,1024]{1,0:T(4,128)(2,1)}, u32[]{:S(2)}) copy-start(bf16[4,1024]{1,0:T(4,128)(2,1)} %param.12) | copy-start | bytes 24580
  15.8 4.0 %copy-start.4 = (bf16[1024]{0:T(1024)(128)(2,1)S(1)}, bf16[1024]{0:T(1024)(128)(2,1)}, u32[]{:S(2)}) copy-start(bf16[1024]{0:T(1024)(128)(2,1)} %param.13) | copy-start | bytes 6148
  36.6 2.2 %copy-start.1 = (bf16[1024,16,128]{0,2,1:T(8,128)(2,1)S(1)}, bf16[1024,16,128]{0,2,1:T(8,128)(2,1)}, u32[]{:S(2)}) copy-start(bf16[1024,16,128]{0,2,1:T(8,128)(2,1)} %pad_maximum_fusion) | copy-start | bytes 12582916
  40.5 7.7 %collective-permute-start = (bf16[136,128]{1,0:T(8,128)(2,1)S(1)}, bf16[136,128]{1,0:T(8,128)(2,1)S(1)}, u32[]{:S(2)}, u32[]{:S(2)}) collective-permute-start(bf16[136,128]{1,0:T(8,128)(2,1)S(1)} %get-tuple-element.7), channel_id=1, source_target_pairs={{0,1},{1,2},{2,3},{3,4},{4,5},{5,6},{6,7},{7,8},{8,9},{9,10},{10,1... | collective-permute-start | bytes 104456 | tf_op jit(solution)/shard_map/ppermute | solution.py:12
  41.3 9.2 %collective-permute-start.1 = (bf16[136,128]{1,0:T(8,128)(2,1)S(1)}, bf16[136,128]{1,0:T(8,128)(2,1)S(1)}, u32[]{:S(2)}, u32[]{:S(2)}) collective-permute-start(bf16[136,128]{1,0:T(8,128)(2,1)S(1)} %get-tuple-element.8), channel_id=1, source_target_pairs={{0,2},{1,3},{2,4},{3,5},{4,6},{5,7},{6,8},{7,9},{8,10},{9,11},{10,... | collective-permute-start | bytes 104456 | tf_op jit(solution)/shard_map/ppermute | solution.py:12
  43.4 10.1 %collective-permute-start.2 = (bf16[136,128]{1,0:T(8,128)(2,1)S(1)}, bf16[136,128]{1,0:T(8,128)(2,1)S(1)}, u32[]{:S(2)}, u32[]{:S(2)}) collective-permute-start(bf16[136,128]{1,0:T(8,128)(2,1)S(1)} %get-tuple-element.10), channel_id=1, source_target_pairs={{0,3},{1,4},{2,5},{3,6},{4,7},{5,8},{6,9},{7,10},{8,11},{9,12},{10... | collective-permute-start | bytes 104456 | tf_op jit(solution)/shard_map/ppermute | solution.py:12
  47.4 7.2 %collective-permute-start.3 = (bf16[136,128]{1,0:T(8,128)(2,1)S(1)}, bf16[136,128]{1,0:T(8,128)(2,1)S(1)}, u32[]{:S(2)}, u32[]{:S(2)}) collective-permute-start(bf16[136,128]{1,0:T(8,128)(2,1)S(1)} %get-tuple-element.11), channel_id=1, source_target_pairs={{0,4},{1,5},{2,6},{3,7},{4,8},{5,9},{6,10},{7,11},{8,12},{9,13},{1... | collective-permute-start | bytes 104456 | tf_op jit(solution)/shard_map/ppermute | solution.py:12
  48.0 7.7 %collective-permute-start.4 = (bf16[136,128]{1,0:T(8,128)(2,1)S(1)}, bf16[136,128]{1,0:T(8,128)(2,1)S(1)}, u32[]{:S(2)}, u32[]{:S(2)}) collective-permute-start(bf16[136,128]{1,0:T(8,128)(2,1)S(1)} %get-tuple-element.12), channel_id=1, source_target_pairs={{0,5},{1,6},{2,7},{3,8},{4,9},{5,10},{6,11},{7,12},{8,13},{9,14},{... | collective-permute-start | bytes 104456 | tf_op jit(solution)/shard_map/ppermute | solution.py:12
  48.2 9.0 %collective-permute-start.5 = (bf16[136,128]{1,0:T(8,128)(2,1)S(1)}, bf16[136,128]{1,0:T(8,128)(2,1)S(1)}, u32[]{:S(2)}, u32[]{:S(2)}) collective-permute-start(bf16[136,128]{1,0:T(8,128)(2,1)S(1)} %get-tuple-element.14), channel_id=1, source_target_pairs={{0,6},{1,7},{2,8},{3,9},{4,10},{5,11},{6,12},{7,13},{8,14},{9,15},... | collective-permute-start | bytes 104456 | tf_op jit(solution)/shard_map/ppermute | solution.py:12
  50.5 9.8 %collective-permute-start.6 = (bf16[136,128]{1,0:T(8,128)(2,1)S(1)}, bf16[136,128]{1,0:T(8,128)(2,1)S(1)}, u32[]{:S(2)}, u32[]{:S(2)}) collective-permute-start(bf16[136,128]{1,0:T(8,128)(2,1)S(1)} %get-tuple-element.15), channel_id=1, source_target_pairs={{0,7},{1,8},{2,9},{3,10},{4,11},{5,12},{6,13},{7,14},{8,15},{9,0},... | collective-permute-start | bytes 104456 | tf_op jit(solution)/shard_map/ppermute | solution.py:12
  53.6 8.3 %collective-permute-start.7 = (bf16[136,128]{1,0:T(8,128)(2,1)S(1)}, bf16[136,128]{1,0:T(8,128)(2,1)S(1)}, u32[]{:S(2)}, u32[]{:S(2)}) collective-permute-start(bf16[136,128]{1,0:T(8,128)(2,1)S(1)} %get-tuple-element.16), channel_id=1, source_target_pairs={{0,8},{1,9},{2,10},{3,11},{4,12},{5,13},{6,14},{7,15},{8,0},{9,1},... | collective-permute-start | bytes 104456 | tf_op jit(solution)/shard_map/ppermute | solution.py:12
  54.6 7.7 %collective-permute-start.8 = (bf16[136,128]{1,0:T(8,128)(2,1)S(1)}, bf16[136,128]{1,0:T(8,128)(2,1)S(1)}, u32[]{:S(2)}, u32[]{:S(2)}) collective-permute-start(bf16[136,128]{1,0:T(8,128)(2,1)S(1)} %get-tuple-element.18), channel_id=1, source_target_pairs={{0,9},{1,10},{2,11},{3,12},{4,13},{5,14},{6,15},{7,0},{8,1},{9,2},... | collective-permute-start | bytes 104456 | tf_op jit(solution)/shard_map/ppermute | solution.py:12
  55.7 7.8 %collective-permute-start.9 = (bf16[136,128]{1,0:T(8,128)(2,1)S(1)}, bf16[136,128]{1,0:T(8,128)(2,1)S(1)}, u32[]{:S(2)}, u32[]{:S(2)}) collective-permute-start(bf16[136,128]{1,0:T(8,128)(2,1)S(1)} %get-tuple-element.19), channel_id=1, source_target_pairs={{0,10},{1,11},{2,12},{3,13},{4,14},{5,15},{6,0},{7,1},{8,2},{9,3},... | collective-permute-start | bytes 104456 | tf_op jit(solution)/shard_map/ppermute | solution.py:12
  57.2 9.9 %collective-permute-start.10 = (bf16[136,128]{1,0:T(8,128)(2,1)S(1)}, bf16[136,128]{1,0:T(8,128)(2,1)S(1)}, u32[]{:S(2)}, u32[]{:S(2)}) collective-permute-start(bf16[136,128]{1,0:T(8,128)(2,1)S(1)} %get-tuple-element.20), channel_id=1, source_target_pairs={{0,11},{1,12},{2,13},{3,14},{4,15},{5,0},{6,1},{7,2},{8,3},{9,4},{... | collective-permute-start | bytes 104456 | tf_op jit(solution)/shard_map/ppermute | solution.py:12
  60.3 6.7 %collective-permute-start.11 = (bf16[136,128]{1,0:T(8,128)(2,1)S(1)}, bf16[136,128]{1,0:T(8,128)(2,1)S(1)}, u32[]{:S(2)}, u32[]{:S(2)}) collective-permute-start(bf16[136,128]{1,0:T(8,128)(2,1)S(1)} %get-tuple-element.17), channel_id=1, source_target_pairs={{0,12},{1,13},{2,14},{3,15},{4,0},{5,1},{6,2},{7,3},{8,4},{9,5},{1... | collective-permute-start | bytes 104456 | tf_op jit(solution)/shard_map/ppermute | solution.py:12
  61.8 5.2 %collective-permute-start.12 = (bf16[136,128]{1,0:T(8,128)(2,1)S(1)}, bf16[136,128]{1,0:T(8,128)(2,1)S(1)}, u32[]{:S(2)}, u32[]{:S(2)}) collective-permute-start(bf16[136,128]{1,0:T(8,128)(2,1)S(1)} %get-tuple-element.13), channel_id=1, source_target_pairs={{0,13},{1,14},{2,15},{3,0},{4,1},{5,2},{6,3},{7,4},{8,5},{9,6},{10... | collective-permute-start | bytes 104456 | tf_op jit(solution)/shard_map/ppermute | solution.py:12
  62.3 4.8 %collective-permute-start.13 = (bf16[136,128]{1,0:T(8,128)(2,1)S(1)}, bf16[136,128]{1,0:T(8,128)(2,1)S(1)}, u32[]{:S(2)}, u32[]{:S(2)}) collective-permute-start(bf16[136,128]{1,0:T(8,128)(2,1)S(1)} %get-tuple-element.9), channel_id=1, source_target_pairs={{0,14},{1,15},{2,0},{3,1},{4,2},{5,3},{6,4},{7,5},{8,6},{9,7},{10,... | collective-permute-start | bytes 104456 | tf_op jit(solution)/shard_map/ppermute | solution.py:12
  63.6 5.1 %collective-permute-start.14 = (bf16[136,128]{1,0:T(8,128)(2,1)S(1)}, bf16[136,128]{1,0:T(8,128)(2,1)S(1)}, u32[]{:S(2)}, u32[]{:S(2)}) collective-permute-start(bf16[136,128]{1,0:T(8,128)(2,1)S(1)} %get-tuple-element.5), channel_id=1, source_target_pairs={{0,15},{1,0},{2,1},{3,2},{4,3},{5,4},{6,5},{7,6},{8,7},{9,8},{10,9... | collective-permute-start | bytes 104456 | tf_op jit(solution)/shard_map/ppermute | solution.py:12

commit v11 on v8

--- a/solution.py
+++ b/solution.py
@@ -94,25 +94,31 @@
         pair_rows.reshape(patches_dev, side_size, 2 * pair_width), (1, 0, 2)
     )
     got_pairs = lax.all_to_all(pair_rows, "rest", split_axis=0, concat_axis=0, tiled=True)
-    got_pairs = jnp.transpose(
-        got_pairs.reshape(side_size * patches_dev, heads_dev, 2 * head_width), (1, 0, 2)
-    )
-    head_keys = got_pairs[:, :, :head_width]
-    head_values = got_pairs[:, :, head_width:]
-
-    scores = jnp.einsum(
-        "hld,hkd->hlk", head_queries, head_keys, preferred_element_type=jnp.float32
-    )
-    maxima = jnp.max(scores, axis=-1)
-    max_high, max_low = split_exact(maxima, True)
-    shift = max_high.astype(jnp.float32) + max_low.astype(jnp.float32)
-    weights = jnp.exp(scores - shift[..., None])
-    totals = jnp.sum(weights, axis=-1)
-    tot_high, tot_low = split_exact(totals, False)
-    summed = jnp.einsum(
-        "hlk,hkd->lhd", weights.astype(jnp.bfloat16), head_values, preferred_element_type=jnp.float32
-    ).astype(jnp.bfloat16)
-    stats = jnp.transpose(jnp.stack([max_high, max_low, tot_high, tot_low], axis=-1), (1, 0, 2))
+    got_pairs = got_pairs.reshape(side_size * patches_dev, heads_dev * 2 * head_width)
+    maxima, totals, summed = [], [], []
+    for head in range(heads_dev):
+        base = head * 2 * head_width
+        scores = jnp.dot(
+            head_queries[head],
+            jnp.transpose(got_pairs[:, base : base + head_width]),
+            preferred_element_type=jnp.float32,
+        )
+        head_max = jnp.max(scores, axis=-1)
+        max_high, max_low = split_exact(head_max, True)
+        shift = max_high.astype(jnp.float32) + max_low.astype(jnp.float32)
+        weights = jnp.exp(scores - shift[:, None])
+        head_tot = jnp.sum(weights, axis=-1)
+        tot_high, tot_low = split_exact(head_tot, False)
+        summed.append(
+            jnp.dot(
+                weights.astype(jnp.bfloat16),
+                got_pairs[:, base + head_width : base + 2 * head_width],
+                preferred_element_type=jnp.float32,
+            ).astype(jnp.bfloat16)
+        )
+        maxima.append(jnp.stack([max_high, max_low, tot_high, tot_low], axis=-1))
+    summed = jnp.stack(summed, axis=1)
+    stats = jnp.stack(maxima, axis=1)
     part_payload = jnp.concatenate(
         [
             summed.reshape(cycle_size, lat_rows * pair_width),

time: 80.3 us -> 83.4 us (1.039)
  matrix products: 6.78 us -> 11.2 us
  local copies, waits for them, and re-layouts: 17 us -> 15.7 us
    dot_general x2 -> x4, matrix products: 1.08 us -> 5.53 us  [the longest x2 2.82 us: local(): jnp.dot(weights.astype(jnp.bfloat16), got_pairs[:, base + head_width:base...]
    reshape x4 -> x0, local copies, waits for them, and re-layouts: 1.88 us -> none  [the longest x2 1.58 us: local(): got_pairs.reshape(side_size * patches_dev, heads_dev, 2 * head_width)]
where the time goes in v11:
time: 83.4 us; the launch traced here: 82.7 us
  waiting for transfers between devices  20.8 us (25%)
  local copies, waits for them, and re-layouts  15.7 us (19%)
  starting transfers between devices  14 us (17%)
  blocking collectives  12.3 us (15%)
  matrix products  11.2 us (13%)
  other arithmetic  8.34 us (10%)
    all_to_all x1, waiting for transfers between devices, local(): got = lax.all_to_all(payload, BLK, split_axis=0, concat_axis=0, tiled=True)  12.4 us
    all_to_all x1, blocking collectives, local(): lax.all_to_all(part_payload, BLK, split_axis=0, concat_axis=0, tiled=True)  12.3 us
    unnamed x21, local copies, waits for them, and re-layouts  11.4 us
    all_to_all x1, waiting for transfers between devices, local(): lax.all_to_all(pair_rows, 'rest', split_axis=0, concat_axis=0, tiled=True)  8.45 us
    all_to_all x1, starting transfers between devices, local(): got = lax.all_to_all(payload, BLK, split_axis=0, concat_axis=0, tiled=True)  7.39 us
    all_to_all x1, starting transfers between devices, local(): lax.all_to_all(pair_rows, 'rest', split_axis=0, concat_axis=0, tiled=True)  6.58 us
    concatenate x1, other arithmetic, local(): jnp.concatenate([w_key.reshape(model_width, head_count, head_width), w_va...  4.76 us
    dot_general x2, matrix products, local(): jnp.dot(weights.astype(jnp.bfloat16), got_pairs[:, base + head_width:base...  2.82 us
  transfers between devices with their start and end apart: 2, of which 2 were waited for; matrix products, arithmetic and copies ran while one was open for 16% of the time, Pallas kernels for 0%

profile of v11, /device:TPU:0, one launch (start us, length us, event | category | flops | bytes accessed | tf_op | source)
XLA Modules:
  0.0 82.7 jit_solution(4566829589830360928)
XLA Ops:
  0.0 1.6 %copy-done = bf16[1024,1024]{1,0:T(8,128)(2,1)S(1)} copy-done((bf16[1024,1024]{1,0:T(8,128)(2,1)S(1)}, bf16[1024,1024]{1,0:T(8,128)(2,1)}, u32[]{:S(2)}) %copy-start) | copy-done | bytes 2097176
  1.6 1.1 %fusion.6 = bf16[2,8,8,128]{3,1,2,0:T(8,128)(2,1)S(1)} fusion(bf16[16,1024]{1,0:T(8,128)(2,1)} %param.11, bf16[1024,1024]{1,0:T(8,128)(2,1)S(1)} %copy-done), kind=kOutput, calls=%fused_computation.15 | convolution fusion | flops 33587200 | bytes 2162688 | tf_op jit(solution)/shard_map/dot_general | solution.py:39
  2.8 0.1 tile.9
  2.9 0.1 broadcast_in_dim.3
  3.1 0.1 fusion.1
  3.2 0.2 copy.98
  3.4 1.2 %pad_maximum_fusion.1 = bf16[16,32,1152]{2,1,0:T(8,128)(2,1)} fusion(bf16[16,32,64]{2,1,0:T(8,128)(2,1)S(1)} %tile.9, bf16[16,32,1088]{2,1,0:T(8,128)(2,1)S(1)} %copy.98), kind=kLoop, calls=%fused_computation.6 | loop fusion | flops 2359296 | bytes 2359296 | tf_op jit(solution)/shard_map/concatenate | solution.py:58
  4.6 7.4 %all-to-all-start = ((bf16[16,32,1152]{2,1,0:T(8,128)(2,1)}), bf16[16,32,1152]{2,1,0:T(8,128)(2,1)S(1)}, u32[]{:S(2)}, u32[]{:S(2)}) async-start(bf16[16,32,1152]{2,1,0:T(8,128)(2,1)} %pad_maximum_fusion.1), calls=%async_computation | async-start | bytes 2359296 | tf_op jit(solution)/shard_map/all_to_all | solution.py:61
  12.0 4.0 %copy.101 = bf16[1024,1024]{0,1:T(8,128)(2,1)} copy(bf16[1024,1024]{1,0:T(8,128)(2,1)} %param.16) | data formatting | bytes 4194304 | tf_op args[7]
  16.0 4.0 %copy.100 = bf16[1024,1024]{0,1:T(8,128)(2,1)} copy(bf16[1024,1024]{1,0:T(8,128)(2,1)} %param.15) | data formatting | bytes 4194304 | tf_op args[6]
  20.0 4.8 %pad_maximum_fusion = bf16[1024,16,128]{0,2,1:T(8,128)(2,1)} fusion(bf16[1024,16,64]{0,2,1:T(8,128)(2,1)} %bitcast.70, bf16[1024,16,64]{0,2,1:T(8,128)(2,1)} %bitcast.71), kind=kLoop, calls=%fused_computation | loop fusion | flops 8388608 | bytes 8388608 | tf_op jit(solution)/shard_map/concatenate | solution.py:81
  24.7 12.4 %all-to-all-done = bf16[16,32,1152]{2,1,0:T(8,128)(2,1)S(1)} async-done(((bf16[16,32,1152]{2,1,0:T(8,128)(2,1)}), bf16[16,32,1152]{2,1,0:T(8,128)(2,1)S(1)}, u32[]{:S(2)}, u32[]{:S(2)}) %all-to-all-start) | async-done | bytes 1179680 | tf_op jit(solution)/shard_map/all_to_all | solution.py:61
  37.2 0.3 convert_reduce_fusion
  37.6 0.1 slice.63
  37.7 0.4 multiply_reduce_fusion
  38.2 0.1 multiply_reduce_fusion.1
  38.3 1.5 %copy-done.1 = bf16[1024,16,128]{0,2,1:T(8,128)(2,1)S(1)} copy-done((bf16[1024,16,128]{0,2,1:T(8,128)(2,1)S(1)}, bf16[1024,16,128]{0,2,1:T(8,128)(2,1)}, u32[]{:S(2)}) %copy-start.1) | copy-done | bytes 4194328
  39.8 1.5 %convolution_convert_fusion = bf16[128,2048]{1,0:T(8,128)(2,1)S(1)} fusion(bf16[1024,2048]{0,1:T(8,128)(2,1)S(1)} %bitcast.69, f32[128,1024]{1,0:T(8,128)S(1)} %multiply_reduce_fusion, f32[1024]{0:T(1024)S(1)} %convert_element_type.242, f32[128]{0:T(128)S(1)} %add_rsqrt_fusion), kind=kOutput, calls=%fused_computation.1 | convolution fusion | flops 537526272 | bytes 5247488 | tf_op jit(solution)/shard_map/dot_general | solution.py:88
  41.3 0.8 %copy.122 = bf16[16,8,8,256]{3,2,0,1:T(8,128)(2,1)} copy(bf16[16,8,8,256]{3,2,1,0:T(8,128)(2,1)S(1)} %bitcast.73) | data formatting | bytes 1048576 | tf_op jit(solution)/shard_map/reshape | solution.py:94
  42.1 6.6 %all-to-all-start.1 = ((bf16[8,128,256]{2,1,0:T(8,128)(2,1)}), bf16[8,128,256]{2,1,0:T(8,128)(2,1)}, u32[]{:S(2)}, u32[]{:S(2)}) async-start(bf16[8,128,256]{2,1,0:T(8,128)(2,1)} %bitcast.74), calls=%async_computation.1 | async-start | bytes 1048576 | tf_op jit(solution)/shard_map/all_to_all | solution.py:96
  48.7 0.1 slice.60
  48.8 0.2 fusion.35
  49.0 0.1 copy.103
  49.2 8.4 %all-to-all-done.1 = bf16[8,128,256]{2,1,0:T(8,128)(2,1)} async-done(((bf16[8,128,256]{2,1,0:T(8,128)(2,1)}), bf16[8,128,256]{2,1,0:T(8,128)(2,1)}, u32[]{:S(2)}, u32[]{:S(2)}) %all-to-all-start.1) | async-done | bytes 524320 | tf_op jit(solution)/shard_map/all_to_all | solution.py:96
  57.7 1.4 %fusion.36 = (f32[256]{0:T(256)S(1)}, f32[256,1024]{1,0:T(8,128)S(1)}) fusion(bf16[1024,256]{1,0:T(8,128)(2,1)} %bitcast.11, bf16[1,256,64]{1,2,0:T(8,128)(2,1)S(1)} %copy.103), kind=kOutput, calls=%fused_computation.75 | convolution fusion | flops 33816320 | bytes 1344512 | tf_op jit(solution)/shard_map/dot_general | solution.py:101
  59.0 0.3 fusion.9
  59.4 1.4 %fusion.37 = (f32[256]{0:T(256)S(1)}, f32[256,1024]{1,0:T(8,128)S(1)}) fusion(bf16[1024,256]{1,0:T(8,128)(2,1)} %bitcast.11, bf16[1,256,64]{1,2,0:T(8,128)(2,1)S(1)} %copy.99), kind=kOutput, calls=%fused_computation.76 | convolution fusion | flops 33816320 | bytes 1344512 | tf_op jit(solution)/shard_map/dot_general | solution.py:101
  60.7 0.3 fusion.7
  61.1 1.4 %fusion.5 = bf16[256,1,64]{0,2,1:T(8,128)(2,1)S(1)} fusion(f32[256,1024]{1,0:T(8,128)S(1)} %get-tuple-element.11, f32[256]{0:T(256)S(1)} %convert_add_fusion, bf16[1024,256]{1,0:T(8,128)(2,1)} %bitcast.11), kind=kOutput, calls=%fused_computation.14 | convolution fusion | flops 34095104 | bytes 1344512 | tf_op jit(solution)/shard_map/dot_general | solution.py:113
  62.5 1.4 %fusion.4 = bf16[256,1,64]{0,2,1:T(8,128)(2,1)S(1)} fusion(f32[256,1024]{1,0:T(8,128)S(1)} %get-tuple-element.13, f32[256]{0:T(256)S(1)} %convert_add_fusion.1, bf16[1024,256]{1,0:T(8,128)(2,1)} %bitcast.11), kind=kOutput, calls=%fused_computation.13 | convolution fusion | flops 34095104 | bytes 1344512 | tf_op jit(solution)/shard_map/dot_general | solution.py:113
  64.0 0.2 copy.105
  64.2 0.2 reshape.193
  64.4 0.1 copy.104
  64.5 0.2 reshape.192
  64.7 0.5 broadcast.63
  65.2 0.7 reduce.4
  65.9 0.1 reshape.203
  66.0 12.3 %all_to_all.15 = bf16[16,2,1088]{2,1,0:T(2,128)(2,1)S(1)} all-to-all(bf16[16,2,1088]{2,1,0:T(2,128)(2,1)S(1)} %reshape.203), channel_id=1, replica_groups=mesh['grp'=2,'side'=2,'rest'=8] {'side','rest'}, dimensions={0} | all-to-all | bytes 139264 | tf_op jit(solution)/shard_map/all_to_all | solution.py:129
  78.3 0.1 reshape.204
  78.4 0.1 copy.115
  78.5 0.1 fusion.34
  78.7 0.3 copy.108
  79.0 0.3 mul.101
  79.3 0.3 mul.102
  79.6 0.1 reduce_sum.69
  79.8 0.1 fusion.24
  80.0 0.1 reshape.198
  80.1 2.6 %fusion.3 = bf16[16,1024]{1,0:T(8,128)(2,1)} fusion(bf16[16,1024]{1,0:T(8,128)(2,1)S(1)} %reshape.198, bf16[1024,1024]{1,0:T(8,128)(2,1)} %param.17, bf16[16,1024]{1,0:T(8,128)(2,1)S(1)} %copy-done.3), kind=kOutput, calls=%fused_computation.10 | convolution fusion | flops 33603584 | bytes 2195456 | tf_op jit(solution)/shard_map/dot_general | solution.py:145
  (40 shorter events, 0.5 us)
Async XLA Ops:
  0.0 1.6 %copy-start = (bf16[1024,1024]{1,0:T(8,128)(2,1)S(1)}, bf16[1024,1024]{1,0:T(8,128)(2,1)}, u32[]{:S(2)}) copy-start(bf16[1024,1024]{1,0:T(8,128)(2,1)} %param.14) | copy-start | bytes 6291460
  0.0 2.9 %copy-start.6 = (s32[512]{0:T(512)S(1)}, s32[512]{0:T(512)}, u32[]{:S(2)}) copy-start(s32[512]{0:T(512)} %param.10) | copy-start | bytes 6148
  0.0 3.0 %copy-start.2 = (bf16[512,1024]{1,0:T(8,128)(2,1)S(1)}, bf16[512,1024]{1,0:T(8,128)(2,1)}, u32[]{:S(2)}) copy-start(bf16[512,1024]{1,0:T(8,128)(2,1)} %param.9) | copy-start | bytes 3145732
  4.6 32.5 %all-to-all-start = ((bf16[16,32,1152]{2,1,0:T(8,128)(2,1)}), bf16[16,32,1152]{2,1,0:T(8,128)(2,1)S(1)}, u32[]{:S(2)}, u32[]{:S(2)}) async-start(bf16[16,32,1152]{2,1,0:T(8,128)(2,1)} %pad_maximum_fusion.1), calls=%async_computation | async-start | bytes 2359296 | tf_op jit(solution)/shard_map/all_to_all | solution.py:61
  16.0 4.0 %copy-start.4 = (bf16[4,1024]{1,0:T(4,128)(2,1)S(1)}, bf16[4,1024]{1,0:T(4,128)(2,1)}, u32[]{:S(2)}) copy-start(bf16[4,1024]{1,0:T(4,128)(2,1)} %param.12) | copy-start | bytes 24580
  16.0 4.0 %copy-start.5 = (bf16[1024]{0:T(1024)(128)(2,1)S(1)}, bf16[1024]{0:T(1024)(128)(2,1)}, u32[]{:S(2)}) copy-start(bf16[1024]{0:T(1024)(128)(2,1)} %param.13) | copy-start | bytes 6148
  37.6 2.2 %copy-start.1 = (bf16[1024,16,128]{0,2,1:T(8,128)(2,1)S(1)}, bf16[1024,16,128]{0,2,1:T(8,128)(2,1)}, u32[]{:S(2)}) copy-start(bf16[1024,16,128]{0,2,1:T(8,128)(2,1)} %pad_maximum_fusion) | copy-start | bytes 12582916
  42.1 15.5 %all-to-all-start.1 = ((bf16[8,128,256]{2,1,0:T(8,128)(2,1)}), bf16[8,128,256]{2,1,0:T(8,128)(2,1)}, u32[]{:S(2)}, u32[]{:S(2)}) async-start(bf16[8,128,256]{2,1,0:T(8,128)(2,1)} %bitcast.74), calls=%async_computation.1 | async-start | bytes 1048576 | tf_op jit(solution)/shard_map/all_to_all | solution.py:96
  64.2 16.0 %copy-start.3 = (bf16[16,1024]{1,0:T(8,128)(2,1)S(1)}, bf16[16,1024]{1,0:T(8,128)(2,1)}, u32[]{:S(2)}) copy-start(bf16[16,1024]{1,0:T(8,128)(2,1)} %param.11) | copy-start | bytes 98308

commit v12 on v6

--- a/solution.py
+++ b/solution.py
@@ -23,16 +23,35 @@
     queries = (
         jnp.dot(latents, w_query, preferred_element_type=jnp.float32) * head_width ** (-0.5)
     ).astype(jnp.bfloat16)
+    query_parts = jnp.tile(
+        jnp.transpose(queries.reshape(lat_rows, head_count, head_width), (1, 0, 2)),
+        (copies, 1, 1),
+    )
+    query_lanes = (lat_rows * head_width) // per_peer
+    embed = query_lanes < lanes
+    if not embed:
+        query_lanes = 0
     row_dest = lax.broadcasted_iota(jnp.int32, (tok_rows,), 0) % cycle_size
     local_ids = (patch_of_row - row_dest * patches_dev).astype(jnp.bfloat16)
-    id_lanes = jnp.pad(local_ids[:, None], ((0, 0), (0, lanes - 1)))
+    id_lanes = jnp.pad(local_ids[:, None], ((0, 0), (0, lanes - query_lanes - 1)))
     payload = jnp.transpose(
         jnp.concatenate([tokens, id_lanes], axis=1).reshape(
-            per_peer, cycle_size, model_width + lanes
+            per_peer, cycle_size, model_width + lanes - query_lanes
         ),
         (1, 0, 2),
     )
-    got = lax.all_to_all(payload, "blk", split_axis=0, concat_axis=0, tiled=True)
+    if embed:
+        payload = jnp.concatenate(
+            [payload, query_parts.reshape(cycle_size, per_peer, query_lanes)], axis=2
+        )
+        got = lax.all_to_all(payload, "blk", split_axis=0, concat_axis=0, tiled=True)
+        got_queries = got[:, :, model_width + lanes - query_lanes :]
+    else:
+        got = lax.all_to_all(payload, "blk", split_axis=0, concat_axis=0, tiled=True)
+        got_queries = lax.all_to_all(query_parts, "blk", split_axis=0, concat_axis=0, tiled=True)
+    head_queries = lax.dynamic_slice_in_dim(
+        got_queries, group_start, head_count, axis=0
+    ).reshape(head_count * lat_rows, head_width)
 
     recv_rows = got[:, :, :model_width].reshape(CONTRASTS, patches_dev, model_width)
     recv_ids = got[:, :, model_width].astype(jnp.int32).reshape(CONTRASTS, 1, patches_dev)
@@ -58,15 +77,9 @@
         preferred_element_type=jnp.float32,
     ).astype(jnp.bfloat16)
     pair_rows = jnp.transpose(pair_rows.reshape(patches_dev, head_count, 2 * head_width), (1, 0, 2))
-    query_parts = jnp.transpose(queries.reshape(lat_rows, head_count, head_width), (1, 0, 2))
-    query_parts = query_parts.reshape(head_count, -1, 2 * head_width)
-    query_len = query_parts.shape[1]
-    pair_payload = jnp.tile(jnp.concatenate([pair_rows, query_parts], axis=1), (copies, 1, 1))
-    got_pairs = lax.all_to_all(pair_payload, "blk", split_axis=0, concat_axis=0, tiled=True)
-    head_queries = lax.dynamic_slice_in_dim(
-        got_pairs[:, patches_dev:], group_start, head_count, axis=0
-    ).reshape(head_count * lat_rows, head_width)
-    got_pairs = got_pairs[:, :patches_dev].reshape(cycle_size * patches_dev, 2 * head_width)
+    got_pairs = lax.all_to_all(
+        jnp.tile(pair_rows, (copies, 1, 1)), "blk", split_axis=0, concat_axis=0, tiled=True
+    ).reshape(cycle_size * patches_dev, 2 * head_width)
     head_keys = got_pairs[:, :head_width]
     head_values = got_pairs[:, head_width:]
 

time: 79.2 us -> 82.5 us (1.042)
  blocking collectives: 33.4 us -> 10.5 us
  waiting for transfers between devices: 11.7 us -> 26.7 us
  starting transfers between devices: 7.39 us -> 14.9 us
  matrix products: 6.17 us -> 9.01 us
    all_to_all x1 -> x0, blocking collectives: 24 us -> none  [local(): lax.all_to_all(pair_payload, 'blk', split_axis=0, concat_axis=0, tiled=True)]
    all_to_all x0 -> x1, waiting for transfers between devices: none -> 14.3 us  [local(): lax.all_to_all(jnp.tile(pair_rows, (copies, 1, 1)), 'blk', split_axis=0,...]
    all_to_all x0 -> x1, starting transfers between devices: none -> 7.53 us  [local(): lax.all_to_all(jnp.tile(pair_rows, (copies, 1, 1)), 'blk', split_axis=0,...]
    concatenate x1, other arithmetic: 1.32 us -> 0.1 us  [local(): jnp.concatenate([tokens, id_lanes], axis=1)]
    concatenate x1, other arithmetic: 0.04 us -> 1.25 us  [local(): jnp.concatenate([payload, query_parts.reshape(cycle_size, per_peer, query...]
    all_to_all x1, blocking collectives: 9.36 us -> 10.5 us  [local(): lax.all_to_all(jnp.tile(attended_head, (copies, 1, 1)), 'blk', split_axis...]
    transpose x1, local copies, waits for them, and re-layouts: 1.31 us -> 0.21 us  [local(): jnp.transpose(jnp.concatenate([tokens, id_lanes], axis=1).reshape(per_pee...]
    dot_general x1, matrix products: 0.71 us -> 1.76 us  [local(): jnp.dot(weights.astype(jnp.bfloat16), head_values, preferred_element_type...]
  transfers between devices with their start and end apart: 1 -> 2, of which waited for: 1 -> 2; matrix products, arithmetic and copies ran while one was open for 17% -> 16% of each run, Pallas kernels for 0% -> 0%
where the time goes in v12:
time: 82.5 us; the launch traced here: 81.8 us
  waiting for transfers between devices  26.7 us (32%)
  starting transfers between devices  14.9 us (18%)
  local copies, waits for them, and re-layouts  12.6 us (15%)
  blocking collectives  10.5 us (13%)
  matrix products  9.01 us (11%)
  other arithmetic  7.85 us (10%)
    all_to_all x1, waiting for transfers between devices, local(): lax.all_to_all(jnp.tile(pair_rows, (copies, 1, 1)), 'blk', split_axis=0,...  14.3 us
    all_to_all x1, waiting for transfers between devices, local(): lax.all_to_all(payload, 'blk', split_axis=0, concat_axis=0, tiled=True)  12.4 us
    all_to_all x1, blocking collectives, local(): lax.all_to_all(jnp.tile(attended_head, (copies, 1, 1)), 'blk', split_axis...  10.5 us
    unnamed x16, local copies, waits for them, and re-layouts  10.4 us
    all_to_all x1, starting transfers between devices, local(): lax.all_to_all(jnp.tile(pair_rows, (copies, 1, 1)), 'blk', split_axis=0,...  7.53 us
    all_to_all x1, starting transfers between devices, local(): lax.all_to_all(payload, 'blk', split_axis=0, concat_axis=0, tiled=True)  7.39 us
    concatenate x1, other arithmetic, local(): jnp.concatenate([w_key.reshape(model_width, head_count, head_width), w_va...  4.75 us
    dot_general x1, matrix products, local(): jnp.dot(attended, w_out, preferred_element_type=jnp.float32)  2.6 us
  transfers between devices with their start and end apart: 2, of which 2 were waited for; matrix products, arithmetic and copies ran while one was open for 16% of the time, Pallas kernels for 0%

profile of v12, /device:TPU:0, one launch (start us, length us, event | category | flops | bytes accessed | tf_op | source)
XLA Modules:
  0.0 81.8 jit_solution(13189302905594196264)
XLA Ops:
  0.0 0.0 copy-start
  0.0 0.0 copy-start.2
  0.0 0.8 %fusion.18 = bf16[512]{0:T(512)(128)(2,1)S(1)} fusion(s32[512]{0:T(512)} %param.10), kind=kLoop, calls=%fused_computation.33 | loop fusion | flops 4608 | bytes 3072 | tf_op jit(solution)/shard_map/convert_element_type | solution.py:35
  0.8 0.8 copy-done
  1.6 1.1 %fusion.5 = bf16[16,1024]{1,0:T(8,128)(2,1)S(1)} fusion(bf16[16,1024]{1,0:T(8,128)(2,1)} %param.11, bf16[1024,1024]{1,0:T(8,128)(2,1)S(1)} %copy-done), kind=kOutput, calls=%fused_computation.14 | convolution fusion | flops 33587200 | bytes 2162688 | tf_op jit(solution)/shard_map/dot_general | solution.py:24
  2.8 0.1 reshape.51
  2.9 0.1 reshape_tile.3
  3.0 0.1 broadcast_in_dim.3
  3.1 0.0 copy-done.2
  3.2 0.1 fusion.4
  3.3 0.2 copy.39
  3.5 0.0 copy-start.5
  3.5 0.0 copy-start.4
  3.5 1.2 %pad_maximum_fusion.1 = bf16[16,32,1152]{2,1,0:T(8,128)(2,1)} fusion(bf16[16,32,32]{2,1,0:T(8,128)(2,1)S(1)} %reshape_tile.3, bf16[16,32,1120]{2,1,0:T(8,128)(2,1)S(1)} %copy.39), kind=kLoop, calls=%fused_computation.10 | loop fusion | flops 2359296 | bytes 2359296 | tf_op jit(solution)/shard_map/concatenate | solution.py:44
  4.7 7.4 %all-to-all-start = ((bf16[16,32,1152]{2,1,0:T(8,128)(2,1)}), bf16[16,32,1152]{2,1,0:T(8,128)(2,1)S(1)}, u32[]{:S(2)}, u32[]{:S(2)}) async-start(bf16[16,32,1152]{2,1,0:T(8,128)(2,1)} %pad_maximum_fusion.1), calls=%async_computation | async-start | bytes 2359296 | tf_op jit(solution)/shard_map/all_to_all | solution.py:47
  12.1 0.0 copy-done.5
  12.2 0.0 copy-done.4
  12.2 4.0 %copy.40 = bf16[1024,1024]{0,1:T(8,128)(2,1)} copy(bf16[1024,1024]{1,0:T(8,128)(2,1)} %param.15) | data formatting | bytes 4194304 | tf_op args[6]
  16.1 3.9 %copy.41 = bf16[1024,1024]{0,1:T(8,128)(2,1)} copy(bf16[1024,1024]{1,0:T(8,128)(2,1)} %param.16) | data formatting | bytes 4194304 | tf_op args[7]
  20.1 4.8 %pad_maximum_fusion = bf16[1024,16,128]{0,2,1:T(8,128)(2,1)} fusion(bf16[1024,16,64]{0,2,1:T(8,128)(2,1)} %bitcast.30, bf16[1024,16,64]{0,2,1:T(8,128)(2,1)} %bitcast.29), kind=kLoop, calls=%fused_computation | loop fusion | flops 8388608 | bytes 8388608 | tf_op jit(solution)/shard_map/concatenate | solution.py:67
  24.8 12.4 %all-to-all-done = bf16[16,32,1152]{2,1,0:T(8,128)(2,1)S(1)} async-done(((bf16[16,32,1152]{2,1,0:T(8,128)(2,1)}), bf16[16,32,1152]{2,1,0:T(8,128)(2,1)S(1)}, u32[]{:S(2)}, u32[]{:S(2)}) %all-to-all-start) | async-done | bytes 1179680 | tf_op jit(solution)/shard_map/all_to_all | solution.py:47
  37.3 0.3 convert_reduce_fusion
  37.6 0.1 reshape.60
  37.7 0.0 copy-start.1
  37.7 0.1 slice.22
  37.8 0.4 multiply_reduce_fusion
  38.3 0.1 multiply_reduce_fusion.1
  38.4 1.5 %copy-done.1 = bf16[1024,16,128]{0,2,1:T(8,128)(2,1)S(1)} copy-done((bf16[1024,16,128]{0,2,1:T(8,128)(2,1)S(1)}, bf16[1024,16,128]{0,2,1:T(8,128)(2,1)}, u32[]{:S(2)}) %copy-start.1) | copy-done | bytes 4194328
  39.9 1.5 %fusion.3 = bf16[16,16,8,128]{3,2,1,0:T(8,128)(2,1)S(1)} fusion(bf16[1024,2048]{0,1:T(8,128)(2,1)S(1)} %bitcast.28, f32[128,1024]{1,0:T(8,128)S(1)} %multiply_reduce_fusion, f32[1024]{0:T(1024)S(1)} %convert_element_type.49, f32[128]{0:T(128)S(1)} %add_rsqrt_fusion), kind=kOutput, calls=%fused_computation.8 | convolution fusion | flops 537526272 | bytes 5247488 | tf_op jit(solution)/shard_map/dot_general | solution.py:74
  41.4 0.9 %copy.49 = bf16[16,16,8,128]{3,2,0,1:T(8,128)(2,1)} copy(bf16[16,16,8,128]{3,2,1,0:T(8,128)(2,1)S(1)} %fusion.3) | data formatting | bytes 1048576 | tf_op jit(solution)/shard_map/reshape | solution.py:79
  42.4 7.5 %all-to-all-start.1 = ((bf16[16,128,128]{2,1,0:T(8,128)(2,1)}), bf16[16,128,128]{2,1,0:T(8,128)(2,1)}, u32[]{:S(2)}, u32[]{:S(2)}) async-start(bf16[16,128,128]{2,1,0:T(8,128)(2,1)} %bitcast.32), calls=%async_computation.1 | async-start | bytes 1048576 | tf_op jit(solution)/shard_map/all_to_all | solution.py:80
  49.9 0.1 slice.20
  50.0 0.1 reshape.52
  50.1 14.3 %all-to-all-done.1 = bf16[16,128,128]{2,1,0:T(8,128)(2,1)} async-done(((bf16[16,128,128]{2,1,0:T(8,128)(2,1)}), bf16[16,128,128]{2,1,0:T(8,128)(2,1)}, u32[]{:S(2)}, u32[]{:S(2)}) %all-to-all-start.1) | async-done | bytes 524320 | tf_op jit(solution)/shard_map/all_to_all | solution.py:80
  64.4 1.6 %fusion.22 = (f32[256]{0:T(256)S(1)}, f32[256,2048]{1,0:T(8,128)S(1)}) fusion(bf16[256,64]{1,0:T(8,128)(2,1)S(1)} %reshape.52, bf16[2048,128]{1,0:T(8,128)(2,1)} %bitcast.8), kind=kOutput, calls=%fused_computation.39 | convolution fusion | flops 67632896 | bytes 2655232 | tf_op jit(solution)/shard_map/ld,kd->lk/dot_general | solution.py:86
  66.0 0.4 fusion.1
  66.4 0.0 copy-start.3
  66.4 1.8 %fusion.6 = bf16[256,64]{0,1:T(8,128)(2,1)S(1)} fusion(f32[256,2048]{1,0:T(8,128)S(1)} %get-tuple-element.6, f32[256]{0:T(256)S(1)} %get-tuple-element.5, bf16[2048,128]{1,0:T(8,128)(2,1)} %bitcast.8, f32[256]{0:T(256)S(1)} %fusion.1), kind=kOutput, calls=%fused_computation.15 | convolution fusion | flops 68190208 | bytes 2656256 | tf_op jit(solution)/shard_map/dot_general | solution.py:92
  68.2 0.1 copy.43
  68.3 0.1 reshape.62
  68.4 10.5 %all_to_all.15 = bf16[16,2,512]{2,1,0:T(2,128)(2,1)S(1)} all-to-all(bf16[16,2,512]{2,1,0:T(2,128)(2,1)S(1)} %reshape.62), channel_id=1, replica_groups=mesh['grp'=2,'blk'=16] {'blk'}, dimensions={0} | all-to-all | bytes 65536 | tf_op jit(solution)/shard_map/all_to_all | solution.py:94
  79.0 0.1 reshape.63
  79.1 0.1 reshape.59
  79.2 0.0 copy-done.3
  79.2 2.6 %fusion.7 = bf16[16,1024]{1,0:T(8,128)(2,1)} fusion(bf16[16,1024]{1,0:T(8,128)(2,1)S(1)} %reshape.59, bf16[1024,1024]{1,0:T(8,128)(2,1)} %param.17, bf16[16,1024]{1,0:T(8,128)(2,1)S(1)} %copy-done.3), kind=kOutput, calls=%fused_computation.16 | convolution fusion | flops 33603584 | bytes 2195456 | tf_op jit(solution)/shard_map/dot_general | solution.py:100
  (5 shorter events, 0.1 us)
Async XLA Ops:
  0.0 1.6 %copy-start = (bf16[1024,1024]{1,0:T(8,128)(2,1)S(1)}, bf16[1024,1024]{1,0:T(8,128)(2,1)}, u32[]{:S(2)}) copy-start(bf16[1024,1024]{1,0:T(8,128)(2,1)} %param.14) | copy-start | bytes 6291460
  0.0 3.1 %copy-start.2 = (bf16[512,1024]{1,0:T(8,128)(2,1)S(1)}, bf16[512,1024]{1,0:T(8,128)(2,1)}, u32[]{:S(2)}) copy-start(bf16[512,1024]{1,0:T(8,128)(2,1)} %param.9) | copy-start | bytes 3145732
  3.5 8.7 %copy-start.5 = (bf16[1024]{0:T(1024)(128)(2,1)S(1)}, bf16[1024]{0:T(1024)(128)(2,1)}, u32[]{:S(2)}) copy-start(bf16[1024]{0:T(1024)(128)(2,1)} %param.13) | copy-start | bytes 6148
  3.5 8.7 %copy-start.4 = (bf16[4,1024]{1,0:T(4,128)(2,1)S(1)}, bf16[4,1024]{1,0:T(4,128)(2,1)}, u32[]{:S(2)}) copy-start(bf16[4,1024]{1,0:T(4,128)(2,1)} %param.12) | copy-start | bytes 24580
  4.7 32.5 %all-to-all-start = ((bf16[16,32,1152]{2,1,0:T(8,128)(2,1)}), bf16[16,32,1152]{2,1,0:T(8,128)(2,1)S(1)}, u32[]{:S(2)}, u32[]{:S(2)}) async-start(bf16[16,32,1152]{2,1,0:T(8,128)(2,1)} %pad_maximum_fusion.1), calls=%async_computation | async-start | bytes 2359296 | tf_op jit(solution)/shard_map/all_to_all | solution.py:47
  37.7 2.2 %copy-start.1 = (bf16[1024,16,128]{0,2,1:T(8,128)(2,1)S(1)}, bf16[1024,16,128]{0,2,1:T(8,128)(2,1)}, u32[]{:S(2)}) copy-start(bf16[1024,16,128]{0,2,1:T(8,128)(2,1)} %pad_maximum_fusion) | copy-start | bytes 12582916
  42.4 22.1 %all-to-all-start.1 = ((bf16[16,128,128]{2,1,0:T(8,128)(2,1)}), bf16[16,128,128]{2,1,0:T(8,128)(2,1)}, u32[]{:S(2)}, u32[]{:S(2)}) async-start(bf16[16,128,128]{2,1,0:T(8,128)(2,1)} %bitcast.32), calls=%async_computation.1 | async-start | bytes 1048576 | tf_op jit(solution)/shard_map/all_to_all | solution.py:80
  66.4 12.8 %copy-start.3 = (bf16[16,1024]{1,0:T(8,128)(2,1)S(1)}, bf16[16,1024]{1,0:T(8,128)(2,1)}, u32[]{:S(2)}) copy-start(bf16[16,1024]{1,0:T(8,128)(2,1)} %param.11) | copy-start | bytes 98308

commit v13 on v9

--- a/solution.py
+++ b/solution.py
@@ -92,9 +92,11 @@
     ).astype(jnp.bfloat16)
     pair_rows = jnp.transpose(
         pair_rows.reshape(patches_dev, side_size, heads_dev, 2 * head_width), (1, 2, 0, 3)
-    )
-    got_pairs = lax.all_to_all(pair_rows, "rest", split_axis=0, concat_axis=2, tiled=True)
-    got_pairs = got_pairs.reshape(heads_dev, side_size * patches_dev, 2 * head_width)
+    ).reshape(side_size, heads_dev * patches_dev, 2 * head_width)
+    got_pairs = lax.all_to_all(pair_rows, "rest", split_axis=0, concat_axis=0, tiled=True)
+    got_pairs = jnp.transpose(
+        got_pairs.reshape(side_size, heads_dev, patches_dev, 2 * head_width), (1, 0, 2, 3)
+    ).reshape(heads_dev, side_size * patches_dev, 2 * head_width)
     head_keys = got_pairs[:, :, :head_width]
     head_values = got_pairs[:, :, head_width:]
 

time: 87.3 us -> 83.6 us (0.958)
  local copies, waits for them, and re-layouts: 21.4 us -> 19.2 us
  matrix products: 9.19 us -> 7.59 us
    slice x1 -> x0, local copies, waits for them, and re-layouts: 2.14 us -> none  [local(): head_values = got_pairs[:, :, head_width:]]
    dot_general x1, matrix products: 2.11 us -> 0.53 us  [local(): jnp.einsum('hlk,hkd->lhd', weights.astype(jnp.bfloat16), head_values, pre...]
    unnamed x20 -> x18, local copies, waits for them, and re-layouts: 12.5 us -> 11.1 us
    transpose x0 -> x1, local copies, waits for them, and re-layouts: none -> 1.34 us  [local(): jnp.transpose(got_pairs.reshape(side_size, heads_dev, patches_dev, 2 * he...]
  transfers between devices with their start and end apart: 2 -> 2, of which waited for: 2 -> 2; matrix products, arithmetic and copies ran while one was open for 15% -> 16% of each run, Pallas kernels for 0% -> 0%
where the time goes in v13:
time: 83.6 us; the launch traced here: 82.9 us
  waiting for transfers between devices  21.1 us (25%)
  local copies, waits for them, and re-layouts  19.2 us (23%)
  starting transfers between devices  14 us (17%)
  blocking collectives  13.2 us (16%)
  matrix products  7.59 us (9%)
  other arithmetic  7.44 us (9%)
    all_to_all x1, blocking collectives, local(): lax.all_to_all(part_payload, BLK, split_axis=0, concat_axis=0, tiled=True)  13.2 us
    all_to_all x1, waiting for transfers between devices, local(): got = lax.all_to_all(payload, BLK, split_axis=0, concat_axis=0, tiled=True)  12.4 us
    unnamed x18, local copies, waits for them, and re-layouts  11.1 us
    all_to_all x1, waiting for transfers between devices, local(): lax.all_to_all(pair_rows, 'rest', split_axis=0, concat_axis=0, tiled=True)  8.75 us
    all_to_all x1, starting transfers between devices, local(): got = lax.all_to_all(payload, BLK, split_axis=0, concat_axis=0, tiled=True)  7.39 us
    all_to_all x1, starting transfers between devices, local(): lax.all_to_all(pair_rows, 'rest', split_axis=0, concat_axis=0, tiled=True)  6.58 us
    concatenate x1, other arithmetic, local(): jnp.concatenate([w_key.reshape(model_width, head_count, head_width), w_va...  4.76 us
    reshape x2, local copies, waits for them, and re-layouts, local(): pair_rows.reshape(patches_dev, side_size, heads_dev, 2 * head_width)  4.18 us
  transfers between devices with their start and end apart: 2, of which 2 were waited for; matrix products, arithmetic and copies ran while one was open for 16% of the time, Pallas kernels for 0%

profile of v13, /device:TPU:0, one launch (start us, length us, event | category | flops | bytes accessed | tf_op | source)
XLA Modules:
  0.0 82.9 jit_solution(16897534570136903860)
XLA Ops:
  0.0 0.0 copy-start
  0.0 1.6 %copy-done = bf16[1024,1024]{1,0:T(8,128)(2,1)S(1)} copy-done((bf16[1024,1024]{1,0:T(8,128)(2,1)S(1)}, bf16[1024,1024]{1,0:T(8,128)(2,1)}, u32[]{:S(2)}) %copy-start) | copy-done | bytes 2097176
  1.6 1.1 %fusion.7 = bf16[2,8,8,128]{3,1,2,0:T(8,128)(2,1)S(1)} fusion(bf16[16,1024]{1,0:T(8,128)(2,1)} %param.11, bf16[1024,1024]{1,0:T(8,128)(2,1)S(1)} %copy-done), kind=kOutput, calls=%fused_computation.17 | convolution fusion | flops 33587200 | bytes 2162688 | tf_op jit(solution)/shard_map/dot_general | solution.py:39
  2.8 0.1 tile.9
  2.9 0.0 copy-done.6
  2.9 0.1 broadcast_in_dim.3
  3.1 0.1 fusion.3
  3.2 0.2 copy.73
  3.4 1.2 %pad_maximum_fusion.1 = bf16[16,32,1152]{2,1,0:T(8,128)(2,1)} fusion(bf16[16,32,64]{2,1,0:T(8,128)(2,1)S(1)} %tile.9, bf16[16,32,1088]{2,1,0:T(8,128)(2,1)S(1)} %bitcast.71), kind=kLoop, calls=%fused_computation.9 | loop fusion | flops 2359296 | bytes 2359296 | tf_op jit(solution)/shard_map/concatenate | solution.py:58
  4.6 7.4 %all-to-all-start = ((bf16[16,32,1152]{2,1,0:T(8,128)(2,1)}), bf16[16,32,1152]{2,1,0:T(8,128)(2,1)S(1)}, u32[]{:S(2)}, u32[]{:S(2)}) async-start(bf16[16,32,1152]{2,1,0:T(8,128)(2,1)} %pad_maximum_fusion.1), calls=%async_computation | async-start | bytes 2359296 | tf_op jit(solution)/shard_map/all_to_all | solution.py:61
  12.0 4.0 %copy.56 = bf16[1024,1024]{0,1:T(8,128)(2,1)} copy(bf16[1024,1024]{1,0:T(8,128)(2,1)} %param.16) | data formatting | bytes 4194304 | tf_op args[7]
  16.0 4.0 %copy.55 = bf16[1024,1024]{0,1:T(8,128)(2,1)} copy(bf16[1024,1024]{1,0:T(8,128)(2,1)} %param.15) | data formatting | bytes 4194304 | tf_op args[6]
  20.0 0.0 copy-done.4
  20.0 4.8 %pad_maximum_fusion = bf16[1024,16,128]{0,2,1:T(8,128)(2,1)} fusion(bf16[1024,16,64]{0,2,1:T(8,128)(2,1)} %bitcast.69, bf16[1024,16,64]{0,2,1:T(8,128)(2,1)} %bitcast.70), kind=kLoop, calls=%fused_computation | loop fusion | flops 8388608 | bytes 8388608 | tf_op jit(solution)/shard_map/concatenate | solution.py:81
  24.7 12.4 %all-to-all-done = bf16[16,32,1152]{2,1,0:T(8,128)(2,1)S(1)} async-done(((bf16[16,32,1152]{2,1,0:T(8,128)(2,1)}), bf16[16,32,1152]{2,1,0:T(8,128)(2,1)S(1)}, u32[]{:S(2)}, u32[]{:S(2)}) %all-to-all-start) | async-done | bytes 1179680 | tf_op jit(solution)/shard_map/all_to_all | solution.py:61
  37.2 0.3 convert_reduce_fusion
  37.5 0.1 reshape.149
  37.6 0.1 slice.45
  37.7 0.4 multiply_reduce_fusion
  38.2 0.1 multiply_reduce_fusion.1
  38.3 1.5 %copy-done.1 = bf16[1024,16,128]{0,2,1:T(8,128)(2,1)S(1)} copy-done((bf16[1024,16,128]{0,2,1:T(8,128)(2,1)S(1)}, bf16[1024,16,128]{0,2,1:T(8,128)(2,1)}, u32[]{:S(2)}) %copy-start.1) | copy-done | bytes 4194328
  39.8 2.3 %convolution_convert_fusion = bf16[128,2048]{1,0:T(8,128)(2,1)} fusion(bf16[1024,2048]{0,1:T(8,128)(2,1)S(1)} %bitcast.68, f32[128,1024]{1,0:T(8,128)S(1)} %multiply_reduce_fusion, f32[1024]{0:T(1024)S(1)} %convert_element_type.148, f32[128]{0:T(128)S(1)} %add_rsqrt_fusion), kind=kOutput, calls=%fused_computation.1 | convolution fusion | flops 537526272 | bytes 5247488 | tf_op jit(solution)/shard_map/dot_general | solution.py:88
  42.1 2.2 %reshape.140 = bf16[128,8,2,128]{3,2,1,0:T(2,128)(2,1)} reshape(bf16[128,2048]{1,0:T(8,128)(2,1)} %convolution_convert_fusion) | data formatting | bytes 1048576 | tf_op jit(solution)/shard_map/reshape | solution.py:94
  44.3 2.0 %copy.57 = bf16[128,8,2,128]{3,0,2,1:T(8,128)(2,1)} copy(bf16[128,8,2,128]{3,2,1,0:T(2,128)(2,1)} %reshape.140) | data formatting | bytes 1048576 | tf_op jit(solution)/shard_map/reshape | solution.py:94
  46.3 6.6 %all-to-all-start.1 = ((bf16[8,256,128]{2,1,0:T(8,128)(2,1)}), bf16[8,256,128]{2,1,0:T(8,128)(2,1)}, u32[]{:S(2)}, u32[]{:S(2)}) async-start(bf16[8,256,128]{2,1,0:T(8,128)(2,1)} %bitcast.73), calls=%async_computation.1 | async-start | bytes 1048576 | tf_op jit(solution)/shard_map/all_to_all | solution.py:96
  52.9 0.1 slice.47
  53.0 0.1 copy.59
  53.1 8.7 %all-to-all-done.1 = bf16[8,256,128]{2,1,0:T(8,128)(2,1)} async-done(((bf16[8,256,128]{2,1,0:T(8,128)(2,1)}), bf16[8,256,128]{2,1,0:T(8,128)(2,1)}, u32[]{:S(2)}, u32[]{:S(2)}) %all-to-all-start.1) | async-done | bytes 524320 | tf_op jit(solution)/shard_map/all_to_all | solution.py:96
  61.8 1.3 %copy.58 = bf16[2,8,128,128]{2,1,3,0:T(8,128)(2,1)S(1)} copy(bf16[2,8,128,128]{3,2,0,1:T(8,128)(2,1)} %bitcast.10) | data formatting | bytes 1048576 | tf_op jit(solution)/shard_map/transpose | solution.py:97
  63.1 0.2 reshape.143
  63.4 0.6 fusion.30
  63.9 0.5 fusion.1
  64.5 0.5 fusion.4
  65.0 0.0 copy-start.3
  65.1 0.1 concatenate.21
  65.2 0.1 copy.61
  65.3 0.1 copy.60
  65.4 0.1 concatenate.20
  65.6 13.2 %all_to_all.15 = bf16[16,16,136]{2,1,0:T(8,128)(2,1)S(1)} all-to-all(bf16[16,16,136]{2,1,0:T(8,128)(2,1)S(1)} %pad_maximum_fusion.2), channel_id=1, replica_groups=mesh['grp'=2,'side'=2,'rest'=8] {'side','rest'}, dimensions={0} | all-to-all | bytes 139264 | tf_op jit(solution)/shard_map/all_to_all | solution.py:119
  78.8 0.1 copy.66
  78.9 0.2 copy.63
  79.1 0.3 mul.91
  79.4 0.2 mul.92
  79.6 0.1 reduce_sum.56
  79.8 0.1 copy.65
  79.9 0.2 fusion.17
  80.1 0.1 reshape.148
  80.3 2.6 %fusion.6 = bf16[16,1024]{1,0:T(8,128)(2,1)} fusion(bf16[16,1024]{1,0:T(8,128)(2,1)S(1)} %reshape.148, bf16[1024,1024]{1,0:T(8,128)(2,1)} %param.17, bf16[16,1024]{1,0:T(8,128)(2,1)S(1)} %copy-done.3), kind=kOutput, calls=%fused_computation.16 | convolution fusion | flops 33603584 | bytes 2195456 | tf_op jit(solution)/shard_map/dot_general | solution.py:133
  (27 shorter events, 0.2 us)
Async XLA Ops:
  0.0 1.6 %copy-start = (bf16[1024,1024]{1,0:T(8,128)(2,1)S(1)}, bf16[1024,1024]{1,0:T(8,128)(2,1)}, u32[]{:S(2)}) copy-start(bf16[1024,1024]{1,0:T(8,128)(2,1)} %param.14) | copy-start | bytes 6291460
  0.0 2.9 %copy-start.6 = (s32[512]{0:T(512)S(1)}, s32[512]{0:T(512)}, u32[]{:S(2)}) copy-start(s32[512]{0:T(512)} %param.10) | copy-start | bytes 6148
  0.0 3.0 %copy-start.2 = (bf16[512,1024]{1,0:T(8,128)(2,1)S(1)}, bf16[512,1024]{1,0:T(8,128)(2,1)}, u32[]{:S(2)}) copy-start(bf16[512,1024]{1,0:T(8,128)(2,1)} %param.9) | copy-start | bytes 3145732
  4.6 32.5 %all-to-all-start = ((bf16[16,32,1152]{2,1,0:T(8,128)(2,1)}), bf16[16,32,1152]{2,1,0:T(8,128)(2,1)S(1)}, u32[]{:S(2)}, u32[]{:S(2)}) async-start(bf16[16,32,1152]{2,1,0:T(8,128)(2,1)} %pad_maximum_fusion.1), calls=%async_computation | async-start | bytes 2359296 | tf_op jit(solution)/shard_map/all_to_all | solution.py:61
  16.0 4.0 %copy-start.4 = (bf16[4,1024]{1,0:T(4,128)(2,1)S(1)}, bf16[4,1024]{1,0:T(4,128)(2,1)}, u32[]{:S(2)}) copy-start(bf16[4,1024]{1,0:T(4,128)(2,1)} %param.12) | copy-start | bytes 24580
  16.0 4.0 %copy-start.5 = (bf16[1024]{0:T(1024)(128)(2,1)S(1)}, bf16[1024]{0:T(1024)(128)(2,1)}, u32[]{:S(2)}) copy-start(bf16[1024]{0:T(1024)(128)(2,1)} %param.13) | copy-start | bytes 6148
  37.6 2.2 %copy-start.1 = (bf16[1024,16,128]{0,2,1:T(8,128)(2,1)S(1)}, bf16[1024,16,128]{0,2,1:T(8,128)(2,1)}, u32[]{:S(2)}) copy-start(bf16[1024,16,128]{0,2,1:T(8,128)(2,1)} %pad_maximum_fusion) | copy-start | bytes 12582916
  46.3 15.5 %all-to-all-start.1 = ((bf16[8,256,128]{2,1,0:T(8,128)(2,1)}), bf16[8,256,128]{2,1,0:T(8,128)(2,1)}, u32[]{:S(2)}, u32[]{:S(2)}) async-start(bf16[8,256,128]{2,1,0:T(8,128)(2,1)} %bitcast.73), calls=%async_computation.1 | async-start | bytes 1048576 | tf_op jit(solution)/shard_map/all_to_all | solution.py:96
  65.0 15.2 %copy-start.3 = (bf16[16,1024]{1,0:T(8,128)(2,1)S(1)}, bf16[16,1024]{1,0:T(8,128)(2,1)}, u32[]{:S(2)}) copy-start(bf16[16,1024]{1,0:T(8,128)(2,1)} %param.11) | copy-start | bytes 98308

commit v14 on v12

--- a/solution.py
+++ b/solution.py
@@ -27,8 +27,8 @@
         jnp.transpose(queries.reshape(lat_rows, head_count, head_width), (1, 0, 2)),
         (copies, 1, 1),
     )
-    query_lanes = (lat_rows * head_width) // per_peer
-    embed = query_lanes < lanes
+    query_lanes = head_width
+    embed = per_peer >= lat_rows and query_lanes < lanes
     if not embed:
         query_lanes = 0
     row_dest = lax.broadcasted_iota(jnp.int32, (tok_rows,), 0) % cycle_size
@@ -41,11 +41,10 @@
         (1, 0, 2),
     )
     if embed:
-        payload = jnp.concatenate(
-            [payload, query_parts.reshape(cycle_size, per_peer, query_lanes)], axis=2
-        )
+        query_rows = jnp.pad(query_parts, ((0, 0), (0, per_peer - lat_rows), (0, 0)))
+        payload = jnp.concatenate([payload, query_rows], axis=2)
         got = lax.all_to_all(payload, "blk", split_axis=0, concat_axis=0, tiled=True)
-        got_queries = got[:, :, model_width + lanes - query_lanes :]
+        got_queries = got[:, :lat_rows, model_width + lanes - query_lanes :]
     else:
         got = lax.all_to_all(payload, "blk", split_axis=0, concat_axis=0, tiled=True)
         got_queries = lax.all_to_all(query_parts, "blk", split_axis=0, concat_axis=0, tiled=True)

time: 82.5 us -> 82.4 us (level)
  no operation moved by 1% of the time
where the time goes in v14:
time: 82.4 us; the launch traced here: 81.7 us
  waiting for transfers between devices  26.9 us (33%)
  starting transfers between devices  14.9 us (18%)
  local copies, waits for them, and re-layouts  12.4 us (15%)
  blocking collectives  10.5 us (13%)
  matrix products  9.01 us (11%)
  other arithmetic  7.85 us (10%)
    all_to_all x1, waiting for transfers between devices, local(): lax.all_to_all(jnp.tile(pair_rows, (copies, 1, 1)), 'blk', split_axis=0,...  14.4 us
    all_to_all x1, waiting for transfers between devices, local(): lax.all_to_all(payload, 'blk', split_axis=0, concat_axis=0, tiled=True)  12.4 us
    all_to_all x1, blocking collectives, local(): lax.all_to_all(jnp.tile(attended_head, (copies, 1, 1)), 'blk', split_axis...  10.5 us
    unnamed x16, local copies, waits for them, and re-layouts  10.4 us
    all_to_all x1, starting transfers between devices, local(): lax.all_to_all(jnp.tile(pair_rows, (copies, 1, 1)), 'blk', split_axis=0,...  7.54 us
    all_to_all x1, starting transfers between devices, local(): lax.all_to_all(payload, 'blk', split_axis=0, concat_axis=0, tiled=True)  7.39 us
    concatenate x1, other arithmetic, local(): jnp.concatenate([w_key.reshape(model_width, head_count, head_width), w_va...  4.75 us
    dot_general x1, matrix products, local(): jnp.dot(attended, w_out, preferred_element_type=jnp.float32)  2.6 us
  transfers between devices with their start and end apart: 2, of which 2 were waited for; matrix products, arithmetic and copies ran while one was open for 16% of the time, Pallas kernels for 0%

profile of v14, /device:TPU:0, one launch (start us, length us, event | category | flops | bytes accessed | tf_op | source)
XLA Modules:
  0.0 81.7 jit_solution(18248234688358710472)
XLA Ops:
  0.0 0.0 copy-start
  0.0 0.0 copy-start.2
  0.0 0.8 %fusion.20 = bf16[512]{0:T(512)(128)(2,1)S(1)} fusion(s32[512]{0:T(512)} %param.10), kind=kLoop, calls=%fused_computation.35 | loop fusion | flops 4608 | bytes 3072 | tf_op jit(solution)/shard_map/convert_element_type | solution.py:35
  0.8 0.8 copy-done
  1.6 1.1 %fusion.7 = bf16[16,1024]{1,0:T(8,128)(2,1)S(1)} fusion(bf16[16,1024]{1,0:T(8,128)(2,1)} %param.11, bf16[1024,1024]{1,0:T(8,128)(2,1)S(1)} %copy-done), kind=kOutput, calls=%fused_computation.16 | convolution fusion | flops 33587200 | bytes 2162688 | tf_op jit(solution)/shard_map/dot_general | solution.py:24
  2.8 0.1 reshape.51
  2.9 0.1 broadcast_in_dim.3
  3.0 0.0 copy-done.2
  3.0 0.1 fusion.6
  3.1 0.2 copy.48
  3.4 0.0 copy-start.5
  3.4 0.0 copy-start.4
  3.4 1.2 %fusion.5 = bf16[16,32,1152]{2,1,0:T(8,128)(2,1)} fusion(bf16[16,16,64]{2,1,0:T(8,128)(2,1)S(1)} %bitcast.36, bf16[16,32,1088]{2,1,0:T(8,128)(2,1)S(1)} %copy.48), kind=kLoop, calls=%fused_computation.11 | loop fusion | flops 3538944 | bytes 2326528 | tf_op jit(solution)/shard_map/concatenate | solution.py:45
  4.6 7.4 %all-to-all-start = ((bf16[16,32,1152]{2,1,0:T(8,128)(2,1)}), bf16[16,32,1152]{2,1,0:T(8,128)(2,1)S(1)}, u32[]{:S(2)}, u32[]{:S(2)}) async-start(bf16[16,32,1152]{2,1,0:T(8,128)(2,1)} %fusion.5), calls=%async_computation | async-start | bytes 2359296 | tf_op jit(solution)/shard_map/all_to_all | solution.py:46
  12.0 0.0 copy-done.5
  12.0 0.0 copy-done.4
  12.1 4.0 %copy.49 = bf16[1024,1024]{0,1:T(8,128)(2,1)} copy(bf16[1024,1024]{1,0:T(8,128)(2,1)} %param.15) | data formatting | bytes 4194304 | tf_op args[6]
  16.0 3.9 %copy.50 = bf16[1024,1024]{0,1:T(8,128)(2,1)} copy(bf16[1024,1024]{1,0:T(8,128)(2,1)} %param.16) | data formatting | bytes 4194304 | tf_op args[7]
  20.0 4.8 %pad_maximum_fusion = bf16[1024,16,128]{0,2,1:T(8,128)(2,1)} fusion(bf16[1024,16,64]{0,2,1:T(8,128)(2,1)} %bitcast.31, bf16[1024,16,64]{0,2,1:T(8,128)(2,1)} %bitcast.30), kind=kLoop, calls=%fused_computation | loop fusion | flops 8388608 | bytes 8388608 | tf_op jit(solution)/shard_map/concatenate | solution.py:66
  24.7 12.4 %all-to-all-done = bf16[16,32,1152]{2,1,0:T(8,128)(2,1)S(1)} async-done(((bf16[16,32,1152]{2,1,0:T(8,128)(2,1)}), bf16[16,32,1152]{2,1,0:T(8,128)(2,1)S(1)}, u32[]{:S(2)}, u32[]{:S(2)}) %all-to-all-start) | async-done | bytes 1179680 | tf_op jit(solution)/shard_map/all_to_all | solution.py:46
  37.2 0.3 convert_reduce_fusion
  37.5 0.1 reshape.60
  37.6 0.0 copy-start.1
  37.6 0.1 slice.22
  37.7 0.4 multiply_reduce_fusion
  38.2 0.1 multiply_reduce_fusion.1
  38.3 1.5 %copy-done.1 = bf16[1024,16,128]{0,2,1:T(8,128)(2,1)S(1)} copy-done((bf16[1024,16,128]{0,2,1:T(8,128)(2,1)S(1)}, bf16[1024,16,128]{0,2,1:T(8,128)(2,1)}, u32[]{:S(2)}) %copy-start.1) | copy-done | bytes 4194328
  39.8 1.5 %fusion.4 = bf16[16,16,8,128]{3,2,1,0:T(8,128)(2,1)S(1)} fusion(bf16[1024,2048]{0,1:T(8,128)(2,1)S(1)} %bitcast.29, f32[128,1024]{1,0:T(8,128)S(1)} %multiply_reduce_fusion, f32[1024]{0:T(1024)S(1)} %convert_element_type.51, f32[128]{0:T(128)S(1)} %add_rsqrt_fusion), kind=kOutput, calls=%fused_computation.10 | convolution fusion | flops 537526272 | bytes 5247488 | tf_op jit(solution)/shard_map/dot_general | solution.py:73
  41.3 0.9 %copy.58 = bf16[16,16,8,128]{3,2,0,1:T(8,128)(2,1)} copy(bf16[16,16,8,128]{3,2,1,0:T(8,128)(2,1)S(1)} %fusion.4) | data formatting | bytes 1048576 | tf_op jit(solution)/shard_map/reshape | solution.py:78
  42.2 7.5 %all-to-all-start.1 = ((bf16[16,128,128]{2,1,0:T(8,128)(2,1)}), bf16[16,128,128]{2,1,0:T(8,128)(2,1)}, u32[]{:S(2)}, u32[]{:S(2)}) async-start(bf16[16,128,128]{2,1,0:T(8,128)(2,1)} %bitcast.33), calls=%async_computation.1 | async-start | bytes 1048576 | tf_op jit(solution)/shard_map/all_to_all | solution.py:79
  49.8 0.1 slice.20
  49.9 14.4 %all-to-all-done.1 = bf16[16,128,128]{2,1,0:T(8,128)(2,1)} async-done(((bf16[16,128,128]{2,1,0:T(8,128)(2,1)}), bf16[16,128,128]{2,1,0:T(8,128)(2,1)}, u32[]{:S(2)}, u32[]{:S(2)}) %all-to-all-start.1) | async-done | bytes 524320 | tf_op jit(solution)/shard_map/all_to_all | solution.py:79
  64.3 1.6 %fusion.24 = (f32[256]{0:T(256)S(1)}, f32[256,2048]{1,0:T(8,128)S(1)}) fusion(bf16[256,64]{1,0:T(8,128)(2,1)S(1)} %bitcast.35, bf16[2048,128]{1,0:T(8,128)(2,1)} %bitcast.9), kind=kOutput, calls=%fused_computation.41 | convolution fusion | flops 67632896 | bytes 2655232 | tf_op jit(solution)/shard_map/ld,kd->lk/dot_general | solution.py:85
  65.9 0.4 fusion.2
  66.3 0.0 copy-start.3
  66.3 1.8 %fusion.8 = bf16[256,64]{0,1:T(8,128)(2,1)S(1)} fusion(f32[256,2048]{1,0:T(8,128)S(1)} %get-tuple-element.6, f32[256]{0:T(256)S(1)} %get-tuple-element.5, bf16[2048,128]{1,0:T(8,128)(2,1)} %bitcast.9, f32[256]{0:T(256)S(1)} %fusion.2), kind=kOutput, calls=%fused_computation.17 | convolution fusion | flops 68190208 | bytes 2656256 | tf_op jit(solution)/shard_map/dot_general | solution.py:91
  68.1 0.1 copy.52
  68.2 0.1 reshape.62
  68.3 10.5 %all_to_all.15 = bf16[16,2,512]{2,1,0:T(2,128)(2,1)S(1)} all-to-all(bf16[16,2,512]{2,1,0:T(2,128)(2,1)S(1)} %reshape.62), channel_id=1, replica_groups=mesh['grp'=2,'blk'=16] {'blk'}, dimensions={0} | all-to-all | bytes 65536 | tf_op jit(solution)/shard_map/all_to_all | solution.py:93
  78.8 0.1 reshape.63
  79.0 0.1 reshape.59
  79.1 0.0 copy-done.3
  79.1 2.6 %fusion.9 = bf16[16,1024]{1,0:T(8,128)(2,1)} fusion(bf16[16,1024]{1,0:T(8,128)(2,1)S(1)} %reshape.59, bf16[1024,1024]{1,0:T(8,128)(2,1)} %param.17, bf16[16,1024]{1,0:T(8,128)(2,1)S(1)} %copy-done.3), kind=kOutput, calls=%fused_computation.18 | convolution fusion | flops 33603584 | bytes 2195456 | tf_op jit(solution)/shard_map/dot_general | solution.py:99
  (5 shorter events, 0.1 us)
Async XLA Ops:
  0.0 1.6 %copy-start = (bf16[1024,1024]{1,0:T(8,128)(2,1)S(1)}, bf16[1024,1024]{1,0:T(8,128)(2,1)}, u32[]{:S(2)}) copy-start(bf16[1024,1024]{1,0:T(8,128)(2,1)} %param.14) | copy-start | bytes 6291460
  0.0 3.0 %copy-start.2 = (bf16[512,1024]{1,0:T(8,128)(2,1)S(1)}, bf16[512,1024]{1,0:T(8,128)(2,1)}, u32[]{:S(2)}) copy-start(bf16[512,1024]{1,0:T(8,128)(2,1)} %param.9) | copy-start | bytes 3145732
  3.4 8.7 %copy-start.5 = (bf16[1024]{0:T(1024)(128)(2,1)S(1)}, bf16[1024]{0:T(1024)(128)(2,1)}, u32[]{:S(2)}) copy-start(bf16[1024]{0:T(1024)(128)(2,1)} %param.13) | copy-start | bytes 6148
  3.4 8.7 %copy-start.4 = (bf16[4,1024]{1,0:T(4,128)(2,1)S(1)}, bf16[4,1024]{1,0:T(4,128)(2,1)}, u32[]{:S(2)}) copy-start(bf16[4,1024]{1,0:T(4,128)(2,1)} %param.12) | copy-start | bytes 24580
  4.6 32.5 %all-to-all-start = ((bf16[16,32,1152]{2,1,0:T(8,128)(2,1)}), bf16[16,32,1152]{2,1,0:T(8,128)(2,1)S(1)}, u32[]{:S(2)}, u32[]{:S(2)}) async-start(bf16[16,32,1152]{2,1,0:T(8,128)(2,1)} %fusion.5), calls=%async_computation | async-start | bytes 2359296 | tf_op jit(solution)/shard_map/all_to_all | solution.py:46
  37.6 2.2 %copy-start.1 = (bf16[1024,16,128]{0,2,1:T(8,128)(2,1)S(1)}, bf16[1024,16,128]{0,2,1:T(8,128)(2,1)}, u32[]{:S(2)}) copy-start(bf16[1024,16,128]{0,2,1:T(8,128)(2,1)} %pad_maximum_fusion) | copy-start | bytes 12582916
  42.2 22.1 %all-to-all-start.1 = ((bf16[16,128,128]{2,1,0:T(8,128)(2,1)}), bf16[16,128,128]{2,1,0:T(8,128)(2,1)}, u32[]{:S(2)}, u32[]{:S(2)}) async-start(bf16[16,128,128]{2,1,0:T(8,128)(2,1)} %bitcast.33), calls=%async_computation.1 | async-start | bytes 1048576 | tf_op jit(solution)/shard_map/all_to_all | solution.py:79
  66.3 12.8 %copy-start.3 = (bf16[16,1024]{1,0:T(8,128)(2,1)S(1)}, bf16[16,1024]{1,0:T(8,128)(2,1)}, u32[]{:S(2)}) copy-start(bf16[16,1024]{1,0:T(8,128)(2,1)} %param.11) | copy-start | bytes 98308

commit v15 on v6

--- a/solution.py
+++ b/solution.py
@@ -1,10 +1,35 @@
 import jax
 import jax.numpy as jnp
 from jax import lax
+from jax.experimental import pallas as pl
+from jax.experimental.pallas import tpu as pltpu
 from jax.sharding import PartitionSpec as P
 
 HEADS = 16
 CONTRASTS = 4
+
+
+def pair_kernel(normed_ref, weight_ref, query_ref, out_ref):
+    rows = normed_ref.shape[0]
+    width = out_ref.shape[2]
+    pairs = jnp.dot(
+        normed_ref[...], weight_ref[...], preferred_element_type=jnp.float32
+    ).astype(out_ref.dtype)
+    for head in range(out_ref.shape[0]):
+        out_ref[head, :rows, :] = pairs[:, head * width : (head + 1) * width]
+        out_ref[head, rows:, :] = query_ref[head]
+
+
+def pair_payload_of(normed, weight, query_parts):
+    rows = normed.shape[0]
+    heads, query_len, width = query_parts.shape
+    in_vmem = pl.BlockSpec(memory_space=pltpu.VMEM)
+    return pl.pallas_call(
+        pair_kernel,
+        out_shape=jax.ShapeDtypeStruct((heads, rows + query_len, width), normed.dtype),
+        in_specs=[in_vmem, in_vmem, in_vmem],
+        out_specs=in_vmem,
+    )(normed, weight, query_parts)
 
 
 def local(tokens, patch_of_row, latents, contrast_gain, norm_gain, w_query, w_key, w_value, w_out):
@@ -52,16 +77,12 @@
         ],
         axis=-1,
     )
-    pair_rows = jnp.dot(
-        normed,
-        pair_weight.reshape(model_width, 2 * model_width),
-        preferred_element_type=jnp.float32,
-    ).astype(jnp.bfloat16)
-    pair_rows = jnp.transpose(pair_rows.reshape(patches_dev, head_count, 2 * head_width), (1, 0, 2))
     query_parts = jnp.transpose(queries.reshape(lat_rows, head_count, head_width), (1, 0, 2))
     query_parts = query_parts.reshape(head_count, -1, 2 * head_width)
-    query_len = query_parts.shape[1]
-    pair_payload = jnp.tile(jnp.concatenate([pair_rows, query_parts], axis=1), (copies, 1, 1))
+    pair_payload = jnp.tile(
+        pair_payload_of(normed, pair_weight.reshape(model_width, 2 * model_width), query_parts),
+        (copies, 1, 1),
+    )
     got_pairs = lax.all_to_all(pair_payload, "blk", split_axis=0, concat_axis=0, tiled=True)
     head_queries = lax.dynamic_slice_in_dim(
         got_pairs[:, patches_dev:], group_start, head_count, axis=0

time: 79.2 us -> 81 us (1.023)
  waiting for transfers between devices: 11.7 us -> 4.62 us
  local copies, waits for them, and re-layouts: 12 us -> 17.5 us
  Pallas kernels: 0 us -> 3.75 us
  matrix products: 6.17 us -> 4.66 us
  other arithmetic: 7.88 us -> 8.7 us
    all_to_all x1, waiting for transfers between devices: 11.7 us -> 4.62 us  [local(): lax.all_to_all(payload, 'blk', split_axis=0, concat_axis=0, tiled=True)]
    reshape x1, local copies, waits for them, and re-layouts: 0.13 us -> 6.5 us  [local(): pair_weight.reshape(model_width, 2 * model_width)]
    pallas_call x0 -> x1, Pallas kernels: none -> 3.75 us  [pair_payload_of(): pl.pallas_call(pair_kernel, out_shape=jax.ShapeDtypeStruct((heads, rows +...]
    dot_general x1 -> x0, matrix products: 1.5 us -> none  [local(): jnp.dot(normed, pair_weight.reshape(model_width, 2 * model_width), prefer...]
    unnamed x14 -> x12, local copies, waits for them, and re-layouts: 9.65 us -> 8.15 us
    convert_element_type x0 -> x1, other arithmetic: none -> 0.82 us  [local(): (joined * inverse_rms * norm_gain.astype(jnp.float32)).astype(jnp.bfloat16)]
  transfers between devices with their start and end apart: 1 -> 1, of which waited for: 1 -> 1; matrix products, arithmetic and copies ran while one was open for 17% -> 25% of each run, Pallas kernels for 0% -> 0%
where the time goes in v15:
time: 81 us; the launch traced here: 80.4 us
  blocking collectives  33.6 us (41%)
  local copies, waits for them, and re-layouts  17.5 us (22%)
  other arithmetic  8.7 us (11%)
  starting transfers between devices  7.39 us (9%)
  matrix products  4.66 us (6%)
  waiting for transfers between devices  4.62 us (6%)
  Pallas kernels  3.75 us (5%)
    all_to_all x1, blocking collectives, local(): lax.all_to_all(pair_payload, 'blk', split_axis=0, concat_axis=0, tiled=True)  24.2 us
    all_to_all x1, blocking collectives, local(): lax.all_to_all(jnp.tile(attended_head, (copies, 1, 1)), 'blk', split_axis...  9.36 us
    unnamed x12, local copies, waits for them, and re-layouts  8.15 us
    all_to_all x1, starting transfers between devices, local(): lax.all_to_all(payload, 'blk', split_axis=0, concat_axis=0, tiled=True)  7.39 us
    reshape x1, local copies, waits for them, and re-layouts, local(): pair_weight.reshape(model_width, 2 * model_width)  6.5 us
    concatenate x1, other arithmetic, local(): jnp.concatenate([w_key.reshape(model_width, head_count, head_width), w_va...  4.8 us
    all_to_all x1, waiting for transfers between devices, local(): lax.all_to_all(payload, 'blk', split_axis=0, concat_axis=0, tiled=True)  4.62 us
    pallas_call x1, Pallas kernels, pair_payload_of(): pl.pallas_call(pair_kernel, out_shape=jax.ShapeDtypeStruct((heads, rows +...  3.75 us
  transfers between devices with their start and end apart: 1, of which 1 were waited for; matrix products, arithmetic and copies ran while one was open for 25% of the time, Pallas kernels for 0%

profile of v15, /device:TPU:0, one launch (start us, length us, event | category | flops | bytes accessed | tf_op | source)
XLA Modules:
  0.0 80.4 jit_solution(12615880181850684624)
XLA Ops:
  0.0 0.0 copy-start
  0.0 0.8 %fusion.15 = bf16[512]{0:T(512)(128)(2,1)S(1)} fusion(s32[512]{0:T(512)} %param.10), kind=kLoop, calls=%fused_computation.27 | loop fusion | flops 4608 | bytes 3072 | tf_op jit(solution)/shard_map/convert_element_type | solution.py:52
  0.8 0.1 broadcast_in_dim.3
  1.0 1.3 %fusion.3 = bf16[512,1152]{1,0:T(8,128)(2,1)S(1)} fusion(bf16[512,1]{1,0:T(8,128)(2,1)S(1)} %broadcast_in_dim.3, bf16[512,1024]{1,0:T(8,128)(2,1)} %param.9), kind=kLoop, calls=%fused_computation.7 | loop fusion | flops 3538944 | bytes 2229248 | tf_op jit(solution)/shard_map/concatenate | solution.py:55
  2.3 0.0 copy-start.2
  2.3 0.0 copy-start.3
  2.3 1.3 %copy.29 = bf16[16,32,1152]{2,1,0:T(8,128)(2,1)} copy(bf16[16,32,1152]{2,0,1:T(8,128)(2,1)S(1)} %bitcast.22) | data formatting | bytes 2359296 | tf_op jit(solution)/shard_map/transpose | solution.py:54
  3.6 7.4 %all-to-all-start = ((bf16[16,32,1152]{2,1,0:T(8,128)(2,1)}), bf16[16,32,1152]{2,1,0:T(8,128)(2,1)S(1)}, u32[]{:S(2)}, u32[]{:S(2)}) async-start(bf16[16,32,1152]{2,1,0:T(8,128)(2,1)} %copy.29), calls=%async_computation | async-start | bytes 2359296 | tf_op jit(solution)/shard_map/all_to_all | solution.py:60
  11.0 0.0 copy-done.2
  11.1 0.0 copy-done.3
  11.1 4.0 %copy.30 = bf16[1024,1024]{0,1:T(8,128)(2,1)} copy(bf16[1024,1024]{1,0:T(8,128)(2,1)} %param.15) | data formatting | bytes 4194304 | tf_op args[6]
  15.0 4.0 %copy.31 = bf16[1024,1024]{0,1:T(8,128)(2,1)} copy(bf16[1024,1024]{1,0:T(8,128)(2,1)} %param.16) | data formatting | bytes 4194304 | tf_op args[7]
  19.0 4.8 %pad_maximum_fusion = bf16[1024,16,128]{0,2,1:T(8,128)(2,1)} fusion(bf16[1024,16,64]{0,2,1:T(8,128)(2,1)} %bitcast.21, bf16[1024,16,64]{0,2,1:T(8,128)(2,1)} %bitcast.20), kind=kLoop, calls=%fused_computation | loop fusion | flops 8388608 | bytes 8388608 | tf_op jit(solution)/shard_map/concatenate | solution.py:73
  23.8 0.0 copy-start.1
  23.8 6.5 %copy.36.weight_ref = bf16[1024,2048]{1,0:T(8,128)(2,1)} copy(bf16[1024,2048]{0,1:T(8,128)(2,1)} %bitcast.19) | data formatting | bytes 8388608 | tf_op jit(solution)/shard_map/reshape | solution.py:83
  30.3 0.0 copy-done
  30.3 0.0 copy-done.1
  30.3 0.4 fusion.4
  30.7 0.1 reshape.55
  30.8 0.7 reshape.56.query_ref
  31.5 4.6 %all-to-all-done = bf16[16,32,1152]{2,1,0:T(8,128)(2,1)S(1)} async-done(((bf16[16,32,1152]{2,1,0:T(8,128)(2,1)}), bf16[16,32,1152]{2,1,0:T(8,128)(2,1)S(1)}, u32[]{:S(2)}, u32[]{:S(2)}) %all-to-all-start) | async-done | bytes 1179680 | tf_op jit(solution)/shard_map/all_to_all | solution.py:60
  36.2 0.3 convert_reduce_fusion
  36.5 0.1 reshape.60
  36.6 0.1 slice.25
  36.7 0.4 multiply_reduce_fusion
  37.2 0.1 multiply_reduce_fusion.1
  37.3 0.8 %multiply_convert_fusion.normed_ref = bf16[128,1024]{1,0:T(8,128)(2,1)} fusion(f32[128,1024]{1,0:T(8,128)S(1)} %multiply_reduce_fusion, f32[1024]{0:T(1024)S(1)} %convert_element_type.45, f32[128]{0:T(128)S(1)} %add_rsqrt_fusion), kind=kLoop, calls=%fused_computation.18 | loop fusion | flops 393216 | bytes 791040 | tf_op jit(solution)/shard_map/convert_element_type | solution.py:72
  38.1 3.8 %shard_map.91 = bf16[16,136,128]{2,1,0:T(8,128)(2,1)} custom-call(bf16[128,1024]{1,0:T(8,128)(2,1)} %multiply_convert_fusion.normed_ref, bf16[1024,2048]{1,0:T(8,128)(2,1)} %copy.36.weight_ref, bf16[16,8,128]{2,1,0:T(8,128)(2,1)} %reshape.56.query_ref), custom_call_target="tpu_custom_call" | custom-call | tf_op jit(solution)/shard_map/pallas_call | solution.py:27
  41.9 24.2 %all_to_all.15 = bf16[16,136,128]{2,1,0:T(8,128)(2,1)S(1)} all-to-all(bf16[16,136,128]{2,1,0:T(8,128)(2,1)} %shard_map.91), channel_id=1, replica_groups=mesh['grp'=2,'blk'=16] {'blk'}, dimensions={0} | all-to-all | bytes 1114112 | tf_op jit(solution)/shard_map/all_to_all | solution.py:86
  66.1 0.1 reshape.57
  66.3 0.5 fusion.19
  66.8 0.4 fusion.1
  67.2 0.7 fusion.5
  67.9 0.1 copy.34
  68.0 0.1 reshape.62
  68.2 9.4 %all_to_all.16 = bf16[16,2,512]{2,1,0:T(2,128)(2,1)S(1)} all-to-all(bf16[16,2,512]{2,1,0:T(2,128)(2,1)S(1)} %reshape.62), channel_id=1, replica_groups=mesh['grp'=2,'blk'=16] {'blk'}, dimensions={0} | all-to-all | bytes 65536 | tf_op jit(solution)/shard_map/all_to_all | solution.py:102
  77.5 0.1 reshape.63
  77.7 0.1 reshape.59
  77.8 2.6 %fusion.6 = bf16[16,1024]{1,0:T(8,128)(2,1)} fusion(bf16[16,1024]{1,0:T(8,128)(2,1)S(1)} %reshape.59, bf16[1024,1024]{1,0:T(8,128)(2,1)} %param.17, bf16[16,1024]{1,0:T(8,128)(2,1)S(1)} %copy-done.1), kind=kOutput, calls=%fused_computation.13 | convolution fusion | flops 33603584 | bytes 2195456 | tf_op jit(solution)/shard_map/dot_general | solution.py:108
  (7 shorter events, 0.1 us)
Async XLA Ops:
  0.0 30.3 %copy-start = (bf16[1024,1024]{1,0:T(8,128)(2,1)S(1)}, bf16[1024,1024]{1,0:T(8,128)(2,1)}, u32[]{:S(2)}) copy-start(bf16[1024,1024]{1,0:T(8,128)(2,1)} %param.14) | copy-start | bytes 6291460
  2.3 8.7 %copy-start.2 = (bf16[4,1024]{1,0:T(4,128)(2,1)S(1)}, bf16[4,1024]{1,0:T(4,128)(2,1)}, u32[]{:S(2)}) copy-start(bf16[4,1024]{1,0:T(4,128)(2,1)} %param.12) | copy-start | bytes 24580
  2.3 8.7 %copy-start.3 = (bf16[1024]{0:T(1024)(128)(2,1)S(1)}, bf16[1024]{0:T(1024)(128)(2,1)}, u32[]{:S(2)}) copy-start(bf16[1024]{0:T(1024)(128)(2,1)} %param.13) | copy-start | bytes 6148
  3.6 32.5 %all-to-all-start = ((bf16[16,32,1152]{2,1,0:T(8,128)(2,1)}), bf16[16,32,1152]{2,1,0:T(8,128)(2,1)S(1)}, u32[]{:S(2)}, u32[]{:S(2)}) async-start(bf16[16,32,1152]{2,1,0:T(8,128)(2,1)} %copy.29), calls=%async_computation | async-start | bytes 2359296 | tf_op jit(solution)/shard_map/all_to_all | solution.py:60
  23.8 6.5 %copy-start.1 = (bf16[16,1024]{1,0:T(8,128)(2,1)S(1)}, bf16[16,1024]{1,0:T(8,128)(2,1)}, u32[]{:S(2)}) copy-start(bf16[16,1024]{1,0:T(8,128)(2,1)} %param.11) | copy-start | bytes 98308

commit v16 on v15

--- a/solution.py
+++ b/solution.py
@@ -9,9 +9,16 @@
 CONTRASTS = 4
 
 
-def pair_kernel(normed_ref, weight_ref, query_ref, out_ref):
-    rows = normed_ref.shape[0]
+def pair_kernel(joined_ref, gain_ref, weight_ref, query_ref, out_ref, normed_ref):
+    rows = joined_ref.shape[0]
     width = out_ref.shape[2]
+
+    @pl.when(pl.program_id(0) == 0)
+    def _():
+        joined = joined_ref[...]
+        inverse_rms = lax.rsqrt(jnp.mean(joined * joined, axis=-1, keepdims=True) + 1e-05)
+        normed_ref[...] = (joined * inverse_rms * gain_ref[...]).astype(normed_ref.dtype)
+
     pairs = jnp.dot(
         normed_ref[...], weight_ref[...], preferred_element_type=jnp.float32
     ).astype(out_ref.dtype)
@@ -20,16 +27,24 @@
         out_ref[head, rows:, :] = query_ref[head]
 
 
-def pair_payload_of(normed, weight, query_parts):
-    rows = normed.shape[0]
+def pair_payload_of(joined, gain, weight, query_parts):
+    rows, model_width = joined.shape
     heads, query_len, width = query_parts.shape
-    in_vmem = pl.BlockSpec(memory_space=pltpu.VMEM)
+    per_step = 2
     return pl.pallas_call(
         pair_kernel,
-        out_shape=jax.ShapeDtypeStruct((heads, rows + query_len, width), normed.dtype),
-        in_specs=[in_vmem, in_vmem, in_vmem],
-        out_specs=in_vmem,
-    )(normed, weight, query_parts)
+        out_shape=jax.ShapeDtypeStruct((heads, rows + query_len, width), weight.dtype),
+        grid=(heads // per_step,),
+        in_specs=[
+            pl.BlockSpec((rows, model_width), lambda j: (0, 0)),
+            pl.BlockSpec((1, model_width), lambda j: (0, 0)),
+            pl.BlockSpec((model_width, per_step * width), lambda j: (0, j)),
+            pl.BlockSpec((per_step, query_len, width), lambda j: (j, 0, 0)),
+        ],
+        out_specs=pl.BlockSpec((per_step, rows + query_len, width), lambda j: (j, 0, 0)),
+        scratch_shapes=[pltpu.VMEM((rows, model_width), weight.dtype)],
+        compiler_params=pltpu.CompilerParams(dimension_semantics=("arbitrary",)),
+    )(joined, gain, weight, query_parts)
 
 
 def local(tokens, patch_of_row, latents, contrast_gain, norm_gain, w_query, w_key, w_value, w_out):
@@ -68,8 +83,6 @@
     )
     joined = jnp.sum(arranged * contrast_gain.astype(jnp.float32)[:, None, :], axis=0)
 
-    inverse_rms = lax.rsqrt(jnp.mean(joined * joined, axis=-1, keepdims=True) + 1e-05)
-    normed = (joined * inverse_rms * norm_gain.astype(jnp.float32)).astype(jnp.bfloat16)
     pair_weight = jnp.concatenate(
         [
             w_key.reshape(model_width, head_count, head_width),
@@ -80,7 +93,12 @@
     query_parts = jnp.transpose(queries.reshape(lat_rows, head_count, head_width), (1, 0, 2))
     query_parts = query_parts.reshape(head_count, -1, 2 * head_width)
     pair_payload = jnp.tile(
-        pair_payload_of(normed, pair_weight.reshape(model_width, 2 * model_width), query_parts),
+        pair_payload_of(
+            joined,
+            norm_gain.astype(jnp.float32).reshape(1, model_width),
+            pair_weight.reshape(model_width, 2 * model_width),
+            query_parts,
+        ),
         (copies, 1, 1),
     )
     got_pairs = lax.all_to_all(pair_payload, "blk", split_axis=0, concat_axis=0, tiled=True)

time: 81 us -> 84.2 us (1.040)
  Pallas kernels: 3.75 us -> 6.92 us
    pallas_call x1, Pallas kernels: 3.75 us -> 6.92 us  [pair_payload_of(): pl.pallas_call(pair_kernel, out_shape=jax.ShapeDtypeStruct((heads, rows +...]
where the time goes in v16:
time: 84.2 us; the launch traced here: 83.4 us
  blocking collectives  33.6 us (40%)
  local copies, waits for them, and re-layouts  17.5 us (21%)
  other arithmetic  8.34 us (10%)
  starting transfers between devices  7.39 us (9%)
  Pallas kernels  6.92 us (8%)
  matrix products  5.46 us (6%)
  waiting for transfers between devices  4.04 us (5%)
    all_to_all x1, blocking collectives, local(): lax.all_to_all(pair_payload, 'blk', split_axis=0, concat_axis=0, tiled=True)  24.2 us
    all_to_all x1, blocking collectives, local(): lax.all_to_all(jnp.tile(attended_head, (copies, 1, 1)), 'blk', split_axis...  9.36 us
    unnamed x12, local copies, waits for them, and re-layouts  8.15 us
    all_to_all x1, starting transfers between devices, local(): lax.all_to_all(payload, 'blk', split_axis=0, concat_axis=0, tiled=True)  7.39 us
    pallas_call x1, Pallas kernels, pair_payload_of(): pl.pallas_call(pair_kernel, out_shape=jax.ShapeDtypeStruct((heads, rows +...  6.92 us
    reshape x1, local copies, waits for them, and re-layouts, local(): pair_weight.reshape(model_width, 2 * model_width)  6.5 us
    concatenate x1, other arithmetic, local(): jnp.concatenate([w_key.reshape(model_width, head_count, head_width), w_va...  4.8 us
    all_to_all x1, waiting for transfers between devices, local(): lax.all_to_all(payload, 'blk', split_axis=0, concat_axis=0, tiled=True)  4.04 us
  transfers between devices with their start and end apart: 1, of which 1 were waited for; matrix products, arithmetic and copies ran while one was open for 25% of the time, Pallas kernels for 0%

profile of v16, /device:TPU:0, one launch (start us, length us, event | category | flops | bytes accessed | tf_op | source)
XLA Modules:
  0.0 83.4 jit_solution(17301408189447272883)
XLA Ops:
  0.0 0.0 copy-start
  0.0 0.8 %fusion.15 = bf16[512]{0:T(512)(128)(2,1)S(1)} fusion(s32[512]{0:T(512)} %param.10), kind=kLoop, calls=%fused_computation.25 | loop fusion | flops 4608 | bytes 3072 | tf_op jit(solution)/shard_map/convert_element_type | solution.py:67
  0.8 0.1 broadcast_in_dim.3
  1.0 1.3 %fusion.3 = bf16[512,1152]{1,0:T(8,128)(2,1)S(1)} fusion(bf16[512,1]{1,0:T(8,128)(2,1)S(1)} %broadcast_in_dim.3, bf16[512,1024]{1,0:T(8,128)(2,1)} %param.9), kind=kLoop, calls=%fused_computation.7 | loop fusion | flops 3538944 | bytes 2229248 | tf_op jit(solution)/shard_map/concatenate | solution.py:70
  2.3 0.0 copy-start.2
  2.3 1.3 %copy.29 = bf16[16,32,1152]{2,1,0:T(8,128)(2,1)} copy(bf16[16,32,1152]{2,0,1:T(8,128)(2,1)S(1)} %bitcast.23) | data formatting | bytes 2359296 | tf_op jit(solution)/shard_map/transpose | solution.py:69
  3.6 7.4 %all-to-all-start = ((bf16[16,32,1152]{2,1,0:T(8,128)(2,1)}), bf16[16,32,1152]{2,1,0:T(8,128)(2,1)S(1)}, u32[]{:S(2)}, u32[]{:S(2)}) async-start(bf16[16,32,1152]{2,1,0:T(8,128)(2,1)} %copy.29), calls=%async_computation | async-start | bytes 2359296 | tf_op jit(solution)/shard_map/all_to_all | solution.py:75
  11.0 0.0 copy-done.2
  11.0 4.0 %copy.30 = bf16[1024,1024]{0,1:T(8,128)(2,1)} copy(bf16[1024,1024]{1,0:T(8,128)(2,1)} %param.15) | data formatting | bytes 4194304 | tf_op args[6]
  15.0 4.0 %copy.31 = bf16[1024,1024]{0,1:T(8,128)(2,1)} copy(bf16[1024,1024]{1,0:T(8,128)(2,1)} %param.16) | data formatting | bytes 4194304 | tf_op args[7]
  19.0 4.8 %pad_maximum_fusion = bf16[1024,16,128]{0,2,1:T(8,128)(2,1)} fusion(bf16[1024,16,64]{0,2,1:T(8,128)(2,1)} %bitcast.22, bf16[1024,16,64]{0,2,1:T(8,128)(2,1)} %bitcast.21), kind=kLoop, calls=%fused_computation | loop fusion | flops 8388608 | bytes 8388608 | tf_op jit(solution)/shard_map/concatenate | solution.py:86
  23.8 0.0 copy-start.1
  23.8 6.5 %copy.36.weight_ref = bf16[1024,2048]{1,0:T(8,128)(2,1)} copy(bf16[1024,2048]{0,1:T(8,128)(2,1)} %bitcast.20) | data formatting | bytes 8388608 | tf_op jit(solution)/shard_map/reshape | solution.py:99
  30.3 0.0 copy-done
  30.3 0.0 copy-done.1
  30.3 0.0 copy-start.3
  30.3 0.4 fusion.4
  30.7 0.1 reshape.53
  30.8 0.7 reshape.54.query_ref
  31.5 0.0 copy-done.3
  31.5 0.6 reshape.59
  32.1 4.0 %all-to-all-done = bf16[16,32,1152]{2,1,0:T(8,128)(2,1)S(1)} async-done(((bf16[16,32,1152]{2,1,0:T(8,128)(2,1)}), bf16[16,32,1152]{2,1,0:T(8,128)(2,1)S(1)}, u32[]{:S(2)}, u32[]{:S(2)}) %all-to-all-start) | async-done | bytes 1179680 | tf_op jit(solution)/shard_map/all_to_all | solution.py:75
  36.2 0.3 convert_reduce_fusion
  36.5 0.1 reshape.58
  36.6 0.1 slice.25
  36.7 1.2 %multiply_reduce_fusion.joined_ref = f32[128,1024]{1,0:T(8,128)} fusion(bf16[4,128,1024]{2,1,0:T(8,128)(2,1)S(1)} %bitcast.26, f32[4,1024]{1,0:T(4,128)S(1)} %convert_element_type.39, s32[4,128]{1,0:T(4,128)S(1)} %reshape.58), kind=kOutput, calls=%fused_computation.4 | convolution fusion | flops 135200768 | bytes 1591296 | tf_op jit(solution)/shard_map/cpk,ckd->cpd/dot_general | solution.py:81
  38.0 6.9 %shard_map.91 = bf16[16,136,128]{2,1,0:T(8,128)(2,1)} custom-call(f32[128,1024]{1,0:T(8,128)} %multiply_reduce_fusion.joined_ref, f32[1,1024]{1,0:T(1,128)} %bitcast.30, bf16[1024,2048]{1,0:T(8,128)(2,1)} %copy.36.weight_ref, bf16[16,8,128]{2,1,0:T(8,128)(2,1)} %reshape.54.query_ref), custom_call_target="tpu_custom_call" | custom-call | tf_op jit(solution)/shard_map/pallas_call | solution.py:34
  44.9 24.2 %all_to_all.15 = bf16[16,136,128]{2,1,0:T(8,128)(2,1)S(1)} all-to-all(bf16[16,136,128]{2,1,0:T(8,128)(2,1)} %shard_map.91), channel_id=1, replica_groups=mesh['grp'=2,'blk'=16] {'blk'}, dimensions={0} | all-to-all | bytes 1114112 | tf_op jit(solution)/shard_map/all_to_all | solution.py:104
  69.1 0.1 reshape.55
  69.3 0.5 fusion.19
  69.8 0.4 fusion.1
  70.2 0.7 fusion.5
  70.9 0.1 copy.34
  71.0 0.1 reshape.62
  71.2 9.4 %all_to_all.16 = bf16[16,2,512]{2,1,0:T(2,128)(2,1)S(1)} all-to-all(bf16[16,2,512]{2,1,0:T(2,128)(2,1)S(1)} %reshape.62), channel_id=1, replica_groups=mesh['grp'=2,'blk'=16] {'blk'}, dimensions={0} | all-to-all | bytes 65536 | tf_op jit(solution)/shard_map/all_to_all | solution.py:120
  80.5 0.1 reshape.63
  80.7 0.1 reshape.57
  80.8 2.6 %fusion.6 = bf16[16,1024]{1,0:T(8,128)(2,1)} fusion(bf16[16,1024]{1,0:T(8,128)(2,1)S(1)} %reshape.57, bf16[1024,1024]{1,0:T(8,128)(2,1)} %param.17, bf16[16,1024]{1,0:T(8,128)(2,1)S(1)} %copy-done.1), kind=kOutput, calls=%fused_computation.13 | convolution fusion | flops 33603584 | bytes 2195456 | tf_op jit(solution)/shard_map/dot_general | solution.py:126
  (5 shorter events, 0.1 us)
Async XLA Ops:
  0.0 30.3 %copy-start = (bf16[1024,1024]{1,0:T(8,128)(2,1)S(1)}, bf16[1024,1024]{1,0:T(8,128)(2,1)}, u32[]{:S(2)}) copy-start(bf16[1024,1024]{1,0:T(8,128)(2,1)} %param.14) | copy-start | bytes 6291460
  2.3 8.7 %copy-start.2 = (bf16[4,1024]{1,0:T(4,128)(2,1)S(1)}, bf16[4,1024]{1,0:T(4,128)(2,1)}, u32[]{:S(2)}) copy-start(bf16[4,1024]{1,0:T(4,128)(2,1)} %param.12) | copy-start | bytes 24580
  3.6 32.5 %all-to-all-start = ((bf16[16,32,1152]{2,1,0:T(8,128)(2,1)}), bf16[16,32,1152]{2,1,0:T(8,128)(2,1)S(1)}, u32[]{:S(2)}, u32[]{:S(2)}) async-start(bf16[16,32,1152]{2,1,0:T(8,128)(2,1)} %copy.29), calls=%async_computation | async-start | bytes 2359296 | tf_op jit(solution)/shard_map/all_to_all | solution.py:75
  23.8 6.5 %copy-start.1 = (bf16[16,1024]{1,0:T(8,128)(2,1)S(1)}, bf16[16,1024]{1,0:T(8,128)(2,1)}, u32[]{:S(2)}) copy-start(bf16[16,1024]{1,0:T(8,128)(2,1)} %param.11) | copy-start | bytes 98308
  30.3 1.3 %copy-start.3 = (bf16[1024]{0:T(1024)(128)(2,1)S(1)}, bf16[1024]{0:T(1024)(128)(2,1)}, u32[]{:S(2)}) copy-start(bf16[1024]{0:T(1024)(128)(2,1)} %param.13) | copy-start | bytes 6148
